TPU v7x, 32 devices: a whole 2x2x4 slice. The times are simulated.
32 devices in a mesh: grp: 2 (over y), ctx: 4 (over z), chan: 2 (over x), dec: 2 (over core).
Axes of the slice: x: 2, y: 2, z: 4, core: 2. Of those that a mesh axis runs over, the one named last changes fastest.
Arguments:
- projected: bfloat16 [3, 2048, 8192], P(None, ('grp', 'ctx', 'dec'), 'chan'), parts along dimension 1, may hold values from -6 to 6
- short_filters: float32 [3, 3, 8192], P(None, None, 'chan'), may hold values from -3 to 3
- decay_rate: float32 [16, 8192], P(None, 'chan'), may hold values from 9.765625e-05 to 0.1, as said below
- residue: float32 [16, 8192], P(None, 'chan'), may hold values from -1 to 1
- skip: float32 [8192], P('chan'), may hold values from -4 to 4
Outputs:
- mixed: bfloat16 [2048, 8192], P(('grp', 'ctx', 'dec'), 'chan'), parts along dimension 0
- final_state: float32 [32, 8192], P('grp', 'chan'), parts along dimension 0
There are 2 independent parts, one for each index of `grp`. A program takes and returns all parts, laid end to end along the dimension named above; an argument that names none is the same for every part. Nothing has to cross between parts.
Inputs may be any that keep to these rules, and one draw needn't show every extreme that they name: `decay_rate`: positive.
All inputs are finite; a program needn't handle non-finite values.
Results may differ from a plain program's by a relative error of at most 0.001.
Values may be sent and summed in bfloat16 or wider, within the bound.
No kernel may reach another device: no remote copies, remote signals or barrier semaphores. Data moves between devices by JAX's collectives and lax.ppermute only.
A program may use at most 256 MiB of HBM per device.

v0:
```python
import jax
import jax.numpy as jnp
from jax import lax
from jax.sharding import PartitionSpec as P

HIGH = lax.Precision.HIGHEST


def from_behind(value, axis, steps):
    count = lax.axis_size(axis)
    initial, last = (max(0, -steps), min(count, count - steps))
    return lax.ppermute(value, axis, [(source, source + steps) for source in range(initial, last)])


def featurize(projected, before, short_filters):
    tap_count = short_filters.shape[1]
    row_count = projected.shape[1]
    joined = jnp.concatenate([before, projected], axis=1).astype(jnp.float32)
    featured = short_filters[:, 0, None, :] * joined[:, tap_count - 1 :, :]
    for shift_by in range(1, tap_count):
        featured = (
            featured
            + short_filters[:, shift_by, None, :]
            * joined[:, tap_count - 1 - shift_by : tap_count - 1 - shift_by + row_count, :]
        )
    return featured


def chain_link(earlier, later):
    return (earlier[0] * later[0], later[0] * earlier[1] + later[1])


def local(projected, short_filters, decay_rate, residue, skip):
    tap_count = short_filters.shape[1]
    row_count = projected.shape[1]
    chan_count = projected.shape[2]
    mode_count = decay_rate.shape[0]
    edge_rows = projected[:, row_count - (tap_count - 1) :, :]
    before = from_behind(edge_rows, ("ctx", "dec"), 1)
    featured = featurize(projected, before, short_filters)
    drive_term = featured[1] * featured[2]
    block_len = 16
    block_count = row_count // block_len
    blocks = drive_term.reshape(block_count, block_len, chan_count)
    steps_done = jnp.arange(block_len + 1, dtype=jnp.float32)
    powers = jnp.exp(-decay_rate[None] * steps_done[:, None, None])
    kernel = jnp.einsum("mc,nmc->nc", residue, powers[:block_len], precision=HIGH)
    offsets = (
        jnp.arange(block_len, dtype=jnp.int32)[:, None]
        - jnp.arange(block_len, dtype=jnp.int32)[None, :]
    )
    toeplitz = jnp.where(
        (offsets >= 0)[:, :, None], kernel[jnp.maximum(offsets, 0)], jnp.float32(0.0)
    )
    within = jnp.einsum("ijc,bjc->bic", toeplitz, blocks, precision=HIGH)
    into_state = powers[:block_len][::-1]
    block_sums = jnp.einsum("jmc,bjc->bmc", into_state, blocks, precision=HIGH)
    block_decay = powers[block_len]
    decays = jnp.broadcast_to(block_decay[None], block_sums.shape)
    running = lax.associative_scan(chain_link, (decays, block_sums))[1]
    contribution = running[block_count - 1]
    starts_local = jnp.concatenate(
        [jnp.zeros((1, mode_count, chan_count), jnp.float32), running[: block_count - 1]], axis=0
    )
    rank_here = lax.axis_index(("ctx", "dec"))
    shards = lax.axis_size(("ctx", "dec"))
    device_rate = decay_rate * row_count
    received = lax.all_gather(contribution[None], ("ctx", "dec"), axis=0, tiled=True)
    rank_ids = jnp.arange(received.shape[0], dtype=jnp.int32)
    behind_by = (rank_here - 1 - rank_ids).astype(jnp.float32)
    to_here = jnp.where(
        (rank_ids < rank_here)[:, None, None],
        jnp.exp(-device_rate[None] * jnp.maximum(behind_by, 0.0)[:, None, None]),
        jnp.float32(0.0),
    )
    to_last = jnp.exp(
        -device_rate[None] * (shards - 1 - rank_ids).astype(jnp.float32)[:, None, None]
    )
    prefix = jnp.sum(to_here * received, axis=0)
    final_state = jnp.sum(to_last * received, axis=0)
    block_ids = jnp.arange(block_count, dtype=jnp.float32)
    entering = (
        starts_local
        + jnp.exp(-decay_rate[None] * block_len * block_ids[:, None, None]) * prefix[None]
    )
    out_state = residue[None] * powers[1:]
    conv_all = within + jnp.einsum("imc,bmc->bic", out_state, entering, precision=HIGH)
    conv_all = conv_all.reshape(row_count, chan_count)
    mixed = (featured[0] * (conv_all + skip[None] * drive_term)).astype(jnp.bfloat16)
    return (mixed, final_state)


def solution(mesh):
    placed = (
        P(None, ("grp", "ctx", "dec"), "chan"),
        P(None, None, "chan"),
        P(None, "chan"),
        P(None, "chan"),
        P("chan"),
    )
    return jax.shard_map(
        local,
        mesh=mesh,
        in_specs=placed,
        out_specs=(P(("grp", "ctx", "dec"), "chan"), P("grp", "chan")),
        check_vma=False,
    )
```

profile of v0, /device:TPU:0, one launch (start us, length us, event | category | flops | bytes accessed | tf_op | source)
XLA Modules:
  0.0 325.3 jit_solution(15625471550160532990)
XLA Ops:
  7.2 1.7 slice.100
  8.9 3.0 collective-permute-start
  11.9 1.8 broadcast_multiply_fusion
  13.7 0.6 multiply_exponential_fusion
  14.3 0.8 fusion.14
  15.1 0.1 fusion.17
  15.2 1.2 copy-done
  16.4 4.2 %slice_multiply_fusion.3 = (f32[16,16,4096]{2,1,0:T(8,128)}, f32[16,16,4096]{2,1,0:T(8,128)}) fusion(f32[17,16,4096]{2,1,0:T(8,128)S(1)} %multiply_exponential_fusion, f32[16,4096]{1,0:T(8,128)S(1)} %copy-done.3), kind=kLoop, calls=%fused_computation.12 | loop fusion | flops 1048576 | bytes 17039360 | tf_op jit(solution)/shard_map/mul | solution.py:86
  20.7 3.0 multiply_reduce_fusion
  23.7 0.1 reshape.70
  23.8 0.1 copy_bitcast_fusion
  23.9 0.7 copy.99
  24.6 4.6 %rev.3 = f32[16,16,4096]{2,1,0:T(8,128)} reverse(f32[16,16,4096]{2,1,0:T(8,128)} %get-tuple-element.13), dimensions={0} | reverse | bytes 8388608 | tf_op jit(solution)/shard_map/rev | solution.py:56
  29.1 18.1 %copy.78 = f32[16,16,4096]{1,0,2:T(8,128)} copy(f32[16,16,4096]{2,1,0:T(8,128)} %rev.3) | data formatting | bytes 8388608 | tf_op jit(solution)/shard_map/rev | solution.py:56
  47.3 3.8 %gather_fusion = f32[256,4096]{1,0:T(8,128)} fusion(f32[16,4096]{1,0:T(8,128)S(1)} %bitcast.42, s32[1024]{0:T(1024)S(1)} %pad_clamp_fusion), kind=kCustom, calls=%fused_computation | custom fusion | bytes 8389632 | tf_op jit(solution)/shard_map/gather | solution.py:53
  51.1 17.9 %copy.75 = f32[16,16,4096]{1,0,2:T(8,128)} copy(f32[16,16,4096]{2,1,0:T(8,128)} %bitcast.43) | data formatting | bytes 8388608 | tf_op jit(solution)/shard_map/gather | solution.py:53
  69.1 18.1 %copy.81 = f32[16,16,4096]{1,0,2:T(8,128)} copy(f32[16,16,4096]{2,1,0:T(8,128)} %get-tuple-element.12) | data formatting | bytes 8388608 | tf_op jit(solution)/shard_map/mul | solution.py:86
  87.2 1.8 maximum_convert_fusion
  89.0 1.9 fusion.4
  90.9 2.6 copy-done.1
  93.5 0.2 slice_multiply_fusion.4
  93.8 8.7 %copy.76 = f32[8,16,4096]{1,0,2:T(8,128)} copy(f32[8,16,4096]{2,1,0:T(8,128)S(1)} %bitcast.47) | data formatting | bytes 4194304 | tf_op jit(solution)/shard_map/mul | solution.py:41
  102.5 34.2 %fusion.18 = f32[4096,8,16]{2,1,0:T(8,128)} fusion(f32[8,16,4096]{1,0,2:T(8,128)} %copy.76, f32[16,16,4096]{1,0,2:T(8,128)} %copy.78), kind=kOutput, calls=%fused_computation.56 | convolution fusion | flops 100663296 | bytes 8388608 | tf_op jit(solution)/shard_map/jmc,bjc->bmc/dot_general | solution.py:57
  136.7 9.9 %copy.79 = f32[4096,8,16]{0,2,1:T(8,128)S(1)} copy(f32[4096,8,16]{2,1,0:T(8,128)} %fusion.18) | data formatting | bytes 4194304 | tf_op jit(solution)/shard_map/jmc,bjc->bmc/dot_general | solution.py:57
  146.6 0.1 slice_add_fusion.1
  146.8 0.1 slice_add_fusion.2
  146.8 1.0 fusion.16
  147.8 0.8 pad_add_fusion
  148.7 1.8 fusion.15
  150.5 0.7 slice.138
  151.2 1.1 pad.23
  152.4 1.9 pad_maximum_fusion.1
  154.2 2.7 pad.22
  156.9 2.2 fusion.9
  159.1 1.4 add.69
  160.5 0.2 pad.25
  160.7 2.8 pad.56
  163.5 1.2 pad_maximum_fusion
  164.7 2.9 pad.24
  167.6 1.7 slice.205
  169.3 3.0 slice_add_fusion
  172.3 58.7 %fusion = f32[4096,8,16]{2,1,0:T(8,128)} fusion(f32[8,16,4096]{1,0,2:T(8,128)} %copy.76, f32[16,16,4096]{1,0,2:T(8,128)} %copy.75, pred[16,16]{1,0:T(8,128)(4,1)S(1)} %subtract_compare_fusion), kind=kOutput, calls=%fused_computation.1 | convolution fusion | flops 101711872 | bytes 8388864 | tf_op jit(solution)/shard_map/ijc,bjc->bic/dot_general | solution.py:55
  231.0 3.2 multiply_reduce_fusion.1
  234.2 1.8 multiply_add_fusion
  236.0 8.7 %copy.80 = f32[8,16,4096]{1,0,2:T(8,128)} copy(f32[8,16,4096]{2,1,0:T(8,128)S(1)} %multiply_add_fusion) | data formatting | bytes 4194304 | tf_op jit(solution)/shard_map/add | solution.py:83
  244.7 59.3 %add_bitcast_fusion = f32[8,16,4096]{1,0,2:T(8,128)} fusion(f32[4096,8,16]{2,1,0:T(8,128)} %fusion, f32[8,16,4096]{1,0,2:T(8,128)} %copy.80, f32[16,16,4096]{1,0,2:T(8,128)} %copy.81), kind=kOutput, calls=%fused_computation.3 | convolution fusion | flops 101187584 | bytes 10485760 | tf_op jit(solution)/shard_map/imc,bmc->bic/dot_general | solution.py:87
  304.0 9.6 %copy.82 = f32[8,16,4096]{2,1,0:T(8,128)S(1)} copy(f32[8,16,4096]{1,0,2:T(8,128)} %add_bitcast_fusion) | data formatting | bytes 4194304 | tf_op jit(solution)/shard_map/add | solution.py:87
  313.6 4.4 %fusion.7 = bf16[128,4096]{1,0:T(8,128)(2,1)} fusion(f32[3,128,4096]{2,1,0:T(8,128)} %copy-done.1, f32[8,16,4096]{2,1,0:T(8,128)S(1)} %copy.82, f32[4096]{0:T(1024)S(1)} %copy-done.10), kind=kLoop, calls=%fused_computation.18 | loop fusion | flops 2621440 | bytes 9453568 | tf_op jit(solution)/shard_map/convert_element_type | solution.py:89
  (31 shorter events, 0.2 us)
Async XLA Ops:
  7.2 7.9 %copy-start.9 = (f32[3,3,4096]{2,1,0:T(4,128)S(1)}, f32[3,3,4096]{2,1,0:T(4,128)}, u32[]{:S(2)}) copy-start(f32[3,3,4096]{2,1,0:T(4,128)} %param.6) | copy-start | bytes 442372
  7.2 9.3 %copy-start.3 = (f32[16,4096]{1,0:T(8,128)S(1)}, f32[16,4096]{1,0:T(8,128)}, u32[]{:S(2)}) copy-start(f32[16,4096]{1,0:T(8,128)} %param.8) | copy-start | bytes 786436
  7.2 223.8 %all-gather.2.cloned.1.call-start = ((), (), s32[]{:S(2)}) async-start(), calls=%async_computation | async-start | bytes 2359296 | tf_op jit(solution)/shard_map/all_gather | solution.py:68
  8.9 78.3 %collective-permute-start = (bf16[3,2,4096]{2,1,0:T(2,128)(2,1)}, bf16[3,2,4096]{2,1,0:T(2,128)(2,1)}, u32[]{:S(2)}, u32[]{:S(2)}) collective-permute-start(bf16[3,2,4096]{2,1,0:T(2,128)(2,1)} %slice.100), channel_id=1, source_target_pairs={{0,1},{1,4},{4,5},{5,8},{8,9},{9,12},{12,13},{2,3},{3,6},{6,7},{7,... | collective-permute-start | bytes 147464 | tf_op jit(solution)/shard_map/ppermute | solution.py:12
  14.2 2.2 copy-start
  69.0 18.1 %copy-start.2 = (bf16[3,128,4096]{2,1,0:T(8,128)(2,1)S(1)}, bf16[3,128,4096]{2,1,0:T(8,128)(2,1)}, u32[]{:S(2)}) copy-start(bf16[3,128,4096]{2,1,0:T(8,128)(2,1)} %param.5) | copy-start | bytes 9437188
  87.2 1.8 copy-start.8
  90.9 2.6 copy-start.1
  136.7 10.0 %copy-start.4 = (f32[16,4096]{1,0:T(8,128)S(1)}, f32[16,4096]{1,0:T(8,128)}, u32[]{:S(2)}) copy-start(f32[16,4096]{1,0:T(8,128)} %fusion.14) | copy-start | bytes 786436
  159.1 4.4 %copy-start.7 = (f32[1,16,4096]{2,1,0:T(8,128)S(1)}, f32[1,16,4096]{2,1,0:T(8,128)}, u32[]{:S(2)}) copy-start(f32[1,16,4096]{2,1,0:T(8,128)} %slice.138) | copy-start | bytes 786436
  172.3 58.7 %copy-start.6 = (f32[16,4096]{1,0:T(8,128)S(1)}, f32[16,4096]{1,0:T(8,128)}, u32[]{:S(2)}) copy-start(f32[16,4096]{1,0:T(8,128)} %get-tuple-element.19) | copy-start | bytes 786436
  172.3 61.9 %copy-start.5 = (f32[16,4096]{1,0:T(8,128)S(1)}, f32[16,4096]{1,0:T(8,128)}, u32[]{:S(2)}) copy-start(f32[16,4096]{1,0:T(8,128)} %get-tuple-element.18) | copy-start | bytes 786436
  304.0 9.7 %copy-start.10 = (f32[4096]{0:T(1024)S(1)}, f32[4096]{0:T(1024)}, u32[]{:S(2)}) copy-start(f32[4096]{0:T(1024)} %param.9) | copy-start | bytes 49156
Sparse Core Ops, SparseCore 0:
  169.5 31.0 all-gather.1
where the time goes:
time: 331 us; the launch traced here: 325 us
  matrix products  152 us (46%)
  local copies, waits for them, and re-layouts  118 us (36%)
  other arithmetic  37.2 us (11%)
  between operations  14.7 us (4%)
    dot_general x1, matrix products, local(): jnp.einsum('imc,bmc->bic', out_state, entering, precision=HIGH)  59.3 us
    dot_general x1, matrix products, local(): within = jnp.einsum('ijc,bjc->bic', toeplitz, blocks, precision=HIGH)  58.7 us
    dot_general x1, matrix products, local(): block_sums = jnp.einsum('jmc,bjc->bmc', into_state, blocks, precision=HIGH)  34.2 us
    rev x2, local copies, waits for them, and re-layouts, local(): into_state = powers[:block_len][::-1]  22.7 us
    gather x2, local copies, waits for them, and re-layouts, local(): kernel[jnp.maximum(offsets, 0)]  21.8 us
    mul x1, local copies, waits for them, and re-layouts, local(): out_state = residue[None] * powers[1:]  18.1 us
    dot_general x1, local copies, waits for them, and re-layouts, local(): block_sums = jnp.einsum('jmc,bjc->bmc', into_state, blocks, precision=HIGH)  9.88 us
    add x1, local copies, waits for them, and re-layouts, local(): within + jnp.einsum('imc,bmc->bic', out_state, entering, precision=HIGH)  9.64 us
  transfers between devices with their start and end apart: 2, of which 0 were waited for; matrix products, arithmetic and copies ran while one was open for 42% of the time, Pallas kernels for 0%

commit v1 on v0

v1 whole, which is shorter than its diff:
```python
import functools

import jax
import jax.numpy as jnp
from jax import lax
from jax.experimental import pallas as pl
from jax.experimental.pallas import tpu as pltpu
from jax.sharding import PartitionSpec as P

CHAN_BLOCK = 512
ROW_GROUP = 8


def from_behind(value, axis, steps):
    count = lax.axis_size(axis)
    initial, last = (max(0, -steps), min(count, count - steps))
    return lax.ppermute(value, axis, [(source, source + steps) for source in range(initial, last)])


def _featurize_one(x_ref, halo_ref, filt_ref, index):
    x = x_ref[index].astype(jnp.float32)
    halo = halo_ref[index].astype(jnp.float32)
    taps = filt_ref[index]
    rows = lax.broadcasted_iota(jnp.int32, x.shape, 0)
    last = halo[halo.shape[0] - 1 : halo.shape[0]]
    second = halo[halo.shape[0] - 2 : halo.shape[0] - 1]
    back1 = jnp.where(rows == 0, last, pltpu.roll(x, 1, 0))
    back2 = jnp.where(rows == 0, second, jnp.where(rows == 1, last, pltpu.roll(x, 2, 0)))
    return taps[0:1] * x + taps[1:2] * back1 + taps[2:3] * back2


def _scan_rows(drive_ref, decay, residue, state, conv_ref):
    row_count = drive_ref.shape[0]
    modes = state.shape[0]

    def body(group, state):
        start = pl.multiple_of(group * ROW_GROUP, ROW_GROUP)
        rows = []
        block = drive_ref[pl.ds(start, ROW_GROUP), :]
        for i in range(ROW_GROUP):
            drive_row = jnp.broadcast_to(block[i : i + 1], state.shape)
            state = decay * state + drive_row
            if conv_ref is not None:
                rows.append(jnp.sum(residue * state, axis=0, keepdims=True))
        if conv_ref is not None:
            conv_ref[pl.ds(start, ROW_GROUP), :] = jnp.concatenate(rows, axis=0)
        return state

    return lax.fori_loop(0, row_count // ROW_GROUP, body, state)


def _contrib_kernel(x_ref, halo_ref, filt_ref, rate_ref, out_ref, drive_scr):
    k = _featurize_one(x_ref, halo_ref, filt_ref, 1)
    v = _featurize_one(x_ref, halo_ref, filt_ref, 2)
    drive_scr[...] = k * v
    decay = jnp.exp(-rate_ref[...])
    state = jnp.zeros(out_ref.shape, jnp.float32)
    out_ref[...] = _scan_rows(drive_scr, decay, None, state, None)


def _mix_kernel(x_ref, halo_ref, filt_ref, rate_ref, res_ref, skip_ref, init_ref, out_ref,
                drive_scr, conv_scr):
    k = _featurize_one(x_ref, halo_ref, filt_ref, 1)
    v = _featurize_one(x_ref, halo_ref, filt_ref, 2)
    drive = k * v
    drive_scr[...] = drive
    decay = jnp.exp(-rate_ref[...])
    _scan_rows(drive_scr, decay, res_ref[...], init_ref[...], conv_scr)
    q = _featurize_one(x_ref, halo_ref, filt_ref, 0)
    out_ref[...] = (q * (conv_scr[...] + skip_ref[...] * drive_scr[...])).astype(out_ref.dtype)


def _specs(row_count, modes, taps):
    x_spec = pl.BlockSpec((3, row_count, CHAN_BLOCK), lambda j: (0, 0, j))
    halo_spec = pl.BlockSpec((3, taps - 1, CHAN_BLOCK), lambda j: (0, 0, j))
    filt_spec = pl.BlockSpec((3, taps, CHAN_BLOCK), lambda j: (0, 0, j))
    mode_spec = pl.BlockSpec((modes, CHAN_BLOCK), lambda j: (0, j))
    row_spec = pl.BlockSpec((1, CHAN_BLOCK), lambda j: (0, j))
    return x_spec, halo_spec, filt_spec, mode_spec, row_spec


def contributions(projected, halo, short_filters, decay_rate):
    _, row_count, chan_count = projected.shape
    modes = decay_rate.shape[0]
    taps = short_filters.shape[1]
    x_spec, halo_spec, filt_spec, mode_spec, _ = _specs(row_count, modes, taps)
    return pl.pallas_call(
        _contrib_kernel,
        grid=(chan_count // CHAN_BLOCK,),
        in_specs=[x_spec, halo_spec, filt_spec, mode_spec],
        out_specs=mode_spec,
        out_shape=jax.ShapeDtypeStruct((modes, chan_count), jnp.float32),
        scratch_shapes=[pltpu.VMEM((row_count, CHAN_BLOCK), jnp.float32)],
    )(projected, halo, short_filters, decay_rate)


def mix(projected, halo, short_filters, decay_rate, residue, skip, prefix):
    _, row_count, chan_count = projected.shape
    modes = decay_rate.shape[0]
    taps = short_filters.shape[1]
    x_spec, halo_spec, filt_spec, mode_spec, row_spec = _specs(row_count, modes, taps)
    return pl.pallas_call(
        _mix_kernel,
        grid=(chan_count // CHAN_BLOCK,),
        in_specs=[x_spec, halo_spec, filt_spec, mode_spec, mode_spec, row_spec, mode_spec],
        out_specs=pl.BlockSpec((row_count, CHAN_BLOCK), lambda j: (0, j)),
        out_shape=jax.ShapeDtypeStruct((row_count, chan_count), jnp.bfloat16),
        scratch_shapes=[
            pltpu.VMEM((row_count, CHAN_BLOCK), jnp.float32),
            pltpu.VMEM((row_count, CHAN_BLOCK), jnp.float32),
        ],
    )(projected, halo, short_filters, decay_rate, residue, skip[None, :], prefix)


def local(projected, short_filters, decay_rate, residue, skip):
    tap_count = short_filters.shape[1]
    row_count = projected.shape[1]
    edge_rows = projected[:, row_count - (tap_count - 1) :, :]
    halo = from_behind(edge_rows, ("ctx", "dec"), 1)
    contribution = contributions(projected, halo, short_filters, decay_rate)
    received = lax.all_gather(contribution, ("ctx", "dec"), axis=0, tiled=False)
    rank_here = lax.axis_index(("ctx", "dec"))
    shard_decay = jnp.exp(-decay_rate * row_count)
    running = jnp.zeros_like(contribution)
    prefix = jnp.zeros_like(contribution)
    for shard in range(received.shape[0]):
        prefix = jnp.where(rank_here == shard, running, prefix)
        running = shard_decay * running + received[shard]
    mixed = mix(projected, halo, short_filters, decay_rate, residue, skip, prefix)
    return (mixed, running)


def solution(mesh):
    placed = (
        P(None, ("grp", "ctx", "dec"), "chan"),
        P(None, None, "chan"),
        P(None, "chan"),
        P(None, "chan"),
        P("chan"),
    )
    return jax.shard_map(
        local,
        mesh=mesh,
        in_specs=placed,
        out_specs=(P(("grp", "ctx", "dec"), "chan"), P("grp", "chan")),
        check_vma=False,
    )
```

time: 331 us -> 78.3 us (0.24); the launches traced: 325 us -> 77.9 us
  matrix products: 152 us -> 0 us
  local copies, waits for them, and re-layouts: 118 us -> 1.61 us
  waiting for transfers between devices: 0.02 us -> 35 us
  other arithmetic: 37.2 us -> 3.45 us
  Pallas kernels: 0 us -> 21.3 us
    dot_general x3 -> x0, matrix products: 152 us -> none  [the longest x1 59.3 us: local(): jnp.einsum('imc,bmc->bic', out_state, entering, precision=HIGH)]
    all_gather x1, waiting for transfers between devices: 0.01 us -> 34.1 us  [local(): received = lax.all_gather(contribution, ('ctx', 'dec'), axis=0, tiled=False)]
    mul x2 -> x0, local copies, waits for them, and re-layouts: 26.8 us -> none  [the longest x1 18.1 us: local(): out_state = residue[None] * powers[1:]]
    rev x2 -> x0, local copies, waits for them, and re-layouts: 22.7 us -> none  [local(): into_state = powers[:block_len][::-1]]
    gather x2 -> x0, local copies, waits for them, and re-layouts: 21.8 us -> none  [local(): kernel[jnp.maximum(offsets, 0)]]
    pallas_call x0 -> x2, Pallas kernels: none -> 21.3 us  [the longest x1 13.6 us: mix(): pl.pallas_call(_mix_kernel, grid=(chan_count // CHAN_BLOCK,), in_specs=[x...]
    add x2 -> x0, local copies, waits for them, and re-layouts: 18.3 us -> none  [the longest x1 9.64 us: local(): within + jnp.einsum('imc,bmc->bic', out_state, entering, precision=HIGH)]
    dot_general x1 -> x0, local copies, waits for them, and re-layouts: 9.88 us -> none  [local(): block_sums = jnp.einsum('jmc,bjc->bmc', into_state, blocks, precision=HIGH)]
  transfers between devices with their start and end apart: 2 -> 2, of which waited for: 0 -> 2; matrix products, arithmetic and copies ran while one was open for 42% -> 0% of each run, Pallas kernels for 0% -> 0%
where the time goes in v1:
time: 78.3 us; the launch traced here: 77.9 us
  waiting for transfers between devices  35 us (45%)
  Pallas kernels  21.3 us (27%)
  between operations  14.1 us (18%)
  other arithmetic  3.45 us (4%)
  starting transfers between devices  2.53 us (3%)
  local copies, waits for them, and re-layouts  1.61 us (2%)
    all_gather x1, waiting for transfers between devices, local(): received = lax.all_gather(contribution, ('ctx', 'dec'), axis=0, tiled=False)  34.1 us
    pallas_call x1, Pallas kernels, mix(): pl.pallas_call(_mix_kernel, grid=(chan_count // CHAN_BLOCK,), in_specs=[x...  13.6 us
    pallas_call x1, Pallas kernels, contributions(): pl.pallas_call(_contrib_kernel, grid=(chan_count // CHAN_BLOCK,), in_spec...  7.66 us
    add x1, other arithmetic, local(): running = shard_decay * running + received[shard]  2.53 us
    ppermute x1, starting transfers between devices, from_behind(): lax.ppermute(value, axis, [(source, source + steps) for source in range(i...  2.49 us
  transfers between devices with their start and end apart: 2, of which 2 were waited for; matrix products, arithmetic and copies ran while one was open for 0% of the time, Pallas kernels for 0%

profile of v1, /device:TPU:0, one launch (start us, length us, event | category | flops | bytes accessed | tf_op | source)
XLA Modules:
  0.0 77.9 jit_solution(10333537289879411138)
XLA Ops:
  7.2 0.0 all-gather.3.cloned.1.call-start
  7.2 1.0 %slice.27 = bf16[3,2,4096]{2,1,0:T(2,128)(2,1)S(1)} slice(bf16[3,128,4096]{2,1,0:T(8,128)(2,1)} %x_ref.3), slice={[0:3], [126:128], [0:4096]} | slice | bytes 98304 | tf_op jit(solution)/shard_map/slice | solution.py:118
  8.2 0.0 copy-start.1
  8.2 2.5 %collective-permute-start = (bf16[3,2,4096]{2,1,0:T(2,128)(2,1)S(1)}, bf16[3,2,4096]{2,1,0:T(2,128)(2,1)S(1)}, u32[]{:S(2)}, u32[]{:S(2)}) collective-permute-start(bf16[3,2,4096]{2,1,0:T(2,128)(2,1)S(1)} %slice.27), channel_id=1, source_target_pairs={{0,1},{1,4},{4,5},{5,8},{8,9},{9,12},{12,13},{2,3},{3,6},{6,7},{7,... | collective-permute-start | bytes 147464 | tf_op jit(solution)/shard_map/ppermute | solution.py:17
  10.7 0.9 %collective-permute-done.halo_ref = bf16[3,2,4096]{2,1,0:T(2,128)(2,1)S(1)} collective-permute-done((bf16[3,2,4096]{2,1,0:T(2,128)(2,1)S(1)}, bf16[3,2,4096]{2,1,0:T(2,128)(2,1)S(1)}, u32[]{:S(2)}, u32[]{:S(2)}) %collective-permute-start) | collective-permute-done | bytes 49184 | tf_op jit(solution)/shard_map/ppermute | solution.py:17
  11.6 0.0 copy-start.2
  11.6 0.6 copy-done.2
  12.2 7.7 %shard_map.68 = f32[16,4096]{1,0:T(8,128)} custom-call(bf16[3,128,4096]{2,1,0:T(8,128)(2,1)} %x_ref.3, bf16[3,2,4096]{2,1,0:T(2,128)(2,1)} %copy-done.2, f32[3,3,4096]{2,1,0:T(4,128)} %filt_ref.3, f32[16,4096]{1,0:T(8,128)} %rate_ref.3), custom_call_target="tpu_custom_call" | custom-call | tf_op jit(solution)/shard_map/pallas_call | solution.py:87
  19.8 0.0 all-gather.3.cloned.1.call-update
  19.9 34.1 %all-gather.3.cloned.1.call-done = f32[128,4096]{1,0:T(8,128)} async-done(((f32[16,4096]{1,0:T(8,128)}), f32[128,4096]{1,0:T(8,128)}) %all-gather.3.cloned.1.call-update) | async-done | bytes 2097168 | tf_op jit(solution)/shard_map/all_gather | solution.py:121
  54.0 0.0 copy-done.1
  54.0 0.0 copy-start
  54.0 2.5 %slice_add_fusion = f32[16,4096]{1,0:T(8,128)} fusion(f32[128,4096]{1,0:T(8,128)} %all-gather.3.cloned.1.call-done, f32[16,4096]{1,0:T(8,128)S(1)} %copy-done.1), kind=kLoop, calls=%fused_computation | loop fusion | flops 1179648 | bytes 2621440 | tf_op jit(solution)/shard_map/add | solution.py:128
  56.5 0.0 copy-done
  56.5 0.9 %select_select_fusion.init_ref = f32[16,4096]{1,0:T(8,128)} fusion(f32[128,4096]{1,0:T(8,128)S(1)} %copy-done, f32[16,4096]{1,0:T(8,128)S(1)} %copy-done.1, pred[]{:T(512)S(6)} %eq.28, pred[]{:T(512)S(6)} %eq.27, pred[]{:T(512)S(6)} %eq.26, pred[]{:T(512)S(6)} %eq.25, pred[]{:T(512)S(6)} %eq.24, pred[]{:T(512)S(6)} %eq.23, pred[]{:T(512)S(6)} %eq.22), kind=kLoop, calls=%fused_computation.8 | loop fusion | flops 1507328 | bytes 2359303 | tf_op jit(solution)/shard_map/jit(_where)/select_n | solution.py:127
  57.5 13.6 %shard_map.69 = bf16[128,4096]{1,0:T(8,128)(2,1)} custom-call(bf16[3,128,4096]{2,1,0:T(8,128)(2,1)} %x_ref.3, bf16[3,2,4096]{2,1,0:T(2,128)(2,1)} %copy-done.2, f32[3,3,4096]{2,1,0:T(4,128)} %filt_ref.3, f32[16,4096]{1,0:T(8,128)} %rate_ref.3, f32[16,4096]{1,0:T(8,128)} %res_ref.1, f32[1,4096]{1,0:T(1,128)} %bitcast.1, f32[16,4096]{1,0:T(8,128)} %select_select_fusion.init_ref), custom_call_target="tpu_custom_call" | custom-call | tf_op jit(solution)/shard_map/pallas_call | solution.py:102
Async XLA Ops:
  7.2 46.8 %all-gather.3.cloned.1.call-start = ((), (), s32[]{:S(2)}) async-start(), calls=%async_computation | async-start | bytes 2359296 | tf_op jit(solution)/shard_map/all_gather | solution.py:121
  8.2 45.8 %copy-start.1 = (f32[16,4096]{1,0:T(8,128)S(1)}, f32[16,4096]{1,0:T(8,128)}, u32[]{:S(2)}) copy-start(f32[16,4096]{1,0:T(8,128)} %rate_ref.3) | copy-start | bytes 786436
  8.2 3.4 %collective-permute-start = (bf16[3,2,4096]{2,1,0:T(2,128)(2,1)S(1)}, bf16[3,2,4096]{2,1,0:T(2,128)(2,1)S(1)}, u32[]{:S(2)}, u32[]{:S(2)}) collective-permute-start(bf16[3,2,4096]{2,1,0:T(2,128)(2,1)S(1)} %slice.27), channel_id=1, source_target_pairs={{0,1},{1,4},{4,5},{5,8},{8,9},{9,12},{12,13},{2,3},{3,6},{6,7},{7,... | collective-permute-start | bytes 147464 | tf_op jit(solution)/shard_map/ppermute | solution.py:17
  11.6 0.6 copy-start.2
  54.0 2.5 %copy-start = (f32[128,4096]{1,0:T(8,128)S(1)}, f32[128,4096]{1,0:T(8,128)}, u32[]{:S(2)}) copy-start(f32[128,4096]{1,0:T(8,128)} %all-gather.3.cloned.1.call-done) | copy-start | bytes 6291460
Sparse Core Ops, SparseCore 0:
  20.0 33.9 all-gather.2

commit v2 on v1

--- a/solution.py
+++ b/solution.py
@@ -112,22 +112,45 @@
     )(projected, halo, short_filters, decay_rate, residue, skip[None, :], prefix)
 
 
+def swap_cores(value):
+    return lax.ppermute(value, "dec", [(0, 1), (1, 0)])
+
+
 def local(projected, short_filters, decay_rate, residue, skip):
     tap_count = short_filters.shape[1]
     row_count = projected.shape[1]
+    chan_count = projected.shape[2]
     edge_rows = projected[:, row_count - (tap_count - 1) :, :]
     halo = from_behind(edge_rows, ("ctx", "dec"), 1)
     contribution = contributions(projected, halo, short_filters, decay_rate)
-    received = lax.all_gather(contribution, ("ctx", "dec"), axis=0, tiled=False)
-    rank_here = lax.axis_index(("ctx", "dec"))
+    core = lax.axis_index("dec")
+    other = swap_cores(contribution)
+    first_core = jnp.where(core == 0, contribution, other)
+    second_core = jnp.where(core == 0, other, contribution)
     shard_decay = jnp.exp(-decay_rate * row_count)
-    running = jnp.zeros_like(contribution)
-    prefix = jnp.zeros_like(contribution)
-    for shard in range(received.shape[0]):
-        prefix = jnp.where(rank_here == shard, running, prefix)
-        running = shard_decay * running + received[shard]
+    half = chan_count // 2
+    start = core * half
+    mine = lambda x: lax.dynamic_slice_in_dim(x, start, half, 1)
+    chip_decay = mine(shard_decay) * mine(shard_decay)
+    chip_part = mine(shard_decay) * mine(first_core) + mine(second_core)
+    received = lax.all_gather(chip_part, "ctx", axis=0, tiled=False)
+    chip_here = lax.axis_index("ctx")
+    running = jnp.zeros_like(chip_part)
+    entering = jnp.zeros_like(chip_part)
+    for chip in range(received.shape[0]):
+        entering = jnp.where(chip_here == chip, running, entering)
+        running = chip_decay * running + received[chip]
+    both = jnp.concatenate([entering, running], axis=0)
+    other_both = swap_cores(both)
+    low = jnp.where(core == 0, both, other_both)
+    high = jnp.where(core == 0, other_both, both)
+    whole = jnp.concatenate([low, high], axis=1)
+    modes = decay_rate.shape[0]
+    chip_entering = whole[:modes]
+    final_state = whole[modes:]
+    prefix = jnp.where(core == 0, chip_entering, shard_decay * chip_entering + first_core)
     mixed = mix(projected, halo, short_filters, decay_rate, residue, skip, prefix)
-    return (mixed, running)
+    return (mixed, final_state)
 
 
 def solution(mesh):

time: 78.3 us -> 52.4 us (0.67)
  waiting for transfers between devices: 35 us -> 3.69 us
  blocking collectives: 0 us -> 16.4 us
  between operations: 14.1 us -> 0.7 us
  starting transfers between devices: 2.53 us -> 5.41 us
    all_gather x1 -> x0, waiting for transfers between devices: 34.1 us -> none  [local(): received = lax.all_gather(contribution, ('ctx', 'dec'), axis=0, tiled=False)]
    all_gather x0 -> x1, blocking collectives: none -> 16.4 us  [local(): received = lax.all_gather(chip_part, 'ctx', axis=0, tiled=False)]
    ppermute x0 -> x2, starting transfers between devices: none -> 3.05 us  [swap_cores(): return lax.ppermute(value, 'dec', [(0, 1), (1, 0)])]
    ppermute x0 -> x2, waiting for transfers between devices: none -> 2.83 us  [swap_cores(): return lax.ppermute(value, 'dec', [(0, 1), (1, 0)])]
    add x1, other arithmetic: 2.53 us -> 0.94 us  [local(): chip_part = mine(shard_decay) * mine(first_core) + mine(second_core)]
    concatenate x0 -> x2, other arithmetic: none -> 0.86 us  [the longest x1 0.84 us: local(): whole = jnp.concatenate([low, high], axis=1)]
  transfers between devices with their start and end apart: 2 -> 3, of which waited for: 2 -> 3; matrix products, arithmetic and copies ran while one was open for 0% -> 0% of each run, Pallas kernels for 0% -> 0%
where the time goes in v2:
time: 52.4 us; the launch traced here: 52.1 us
  Pallas kernels  21.3 us (41%)
  blocking collectives  16.4 us (31%)
  starting transfers between devices  5.41 us (10%)
  waiting for transfers between devices  3.69 us (7%)
  other arithmetic  2.92 us (6%)
  local copies, waits for them, and re-layouts  1.65 us (3%)
  between operations  0.7 us (1%)
    all_gather x1, blocking collectives, local(): received = lax.all_gather(chip_part, 'ctx', axis=0, tiled=False)  16.4 us
    pallas_call x1, Pallas kernels, mix(): pl.pallas_call(_mix_kernel, grid=(chan_count // CHAN_BLOCK,), in_specs=[x...  13.6 us
    pallas_call x1, Pallas kernels, contributions(): pl.pallas_call(_contrib_kernel, grid=(chan_count // CHAN_BLOCK,), in_spec...  7.66 us
    ppermute x2, starting transfers between devices, swap_cores(): return lax.ppermute(value, 'dec', [(0, 1), (1, 0)])  3.05 us
    ppermute x2, waiting for transfers between devices, swap_cores(): return lax.ppermute(value, 'dec', [(0, 1), (1, 0)])  2.83 us
    ppermute x1, starting transfers between devices, from_behind(): lax.ppermute(value, axis, [(source, source + steps) for source in range(i...  2.36 us
  transfers between devices with their start and end apart: 3, of which 3 were waited for; matrix products, arithmetic and copies ran while one was open for 0% of the time, Pallas kernels for 0%

profile of v2, /device:TPU:0, one launch (start us, length us, event | category | flops | bytes accessed | tf_op | source)
XLA Modules:
  0.0 52.1 jit_solution(15061782680396472936)
XLA Ops:
  0.6 0.0 copy-start
  0.6 1.0 %slice.21 = bf16[3,2,4096]{2,1,0:T(2,128)(2,1)S(1)} slice(bf16[3,128,4096]{2,1,0:T(8,128)(2,1)} %x_ref.3), slice={[0:3], [126:128], [0:4096]} | slice | bytes 98304 | tf_op jit(solution)/shard_map/slice | solution.py:123
  1.7 2.4 %collective-permute-start = (bf16[3,2,4096]{2,1,0:T(2,128)(2,1)S(1)}, bf16[3,2,4096]{2,1,0:T(2,128)(2,1)S(1)}, u32[]{:S(2)}, u32[]{:S(2)}) collective-permute-start(bf16[3,2,4096]{2,1,0:T(2,128)(2,1)S(1)} %slice.21), channel_id=1, source_target_pairs={{0,1},{1,4},{4,5},{5,8},{8,9},{9,12},{12,13},{2,3},{3,6},{6,7},{7,... | collective-permute-start | bytes 147464 | tf_op jit(solution)/shard_map/ppermute | solution.py:17
  4.0 0.9 %collective-permute-done.halo_ref = bf16[3,2,4096]{2,1,0:T(2,128)(2,1)S(1)} collective-permute-done((bf16[3,2,4096]{2,1,0:T(2,128)(2,1)S(1)}, bf16[3,2,4096]{2,1,0:T(2,128)(2,1)S(1)}, u32[]{:S(2)}, u32[]{:S(2)}) %collective-permute-start) | collective-permute-done | bytes 49184 | tf_op jit(solution)/shard_map/ppermute | solution.py:17
  4.9 0.0 copy-start.1
  4.9 0.6 %copy-done.1 = bf16[3,2,4096]{2,1,0:T(2,128)(2,1)} copy-done((bf16[3,2,4096]{2,1,0:T(2,128)(2,1)}, bf16[3,2,4096]{2,1,0:T(2,128)(2,1)S(1)}, u32[]{:S(2)}) %copy-start.1) | copy-done | bytes 49176
  5.5 7.7 %shard_map.68 = f32[16,4096]{1,0:T(8,128)} custom-call(bf16[3,128,4096]{2,1,0:T(8,128)(2,1)} %x_ref.3, bf16[3,2,4096]{2,1,0:T(2,128)(2,1)} %copy-done.1, f32[3,3,4096]{2,1,0:T(4,128)} %filt_ref.3, f32[16,4096]{1,0:T(8,128)} %rate_ref.3), custom_call_target="tpu_custom_call" | custom-call | tf_op jit(solution)/shard_map/pallas_call | solution.py:87
  13.2 3.0 %collective-permute-start.1 = (f32[16,4096]{1,0:T(8,128)}, f32[16,4096]{1,0:T(8,128)S(1)}, u32[]{:S(2)}, u32[]{:S(2)}) collective-permute-start(f32[16,4096]{1,0:T(8,128)} %shard_map.68), channel_id=1, source_target_pairs={{0,1},{1,0},{2,3},{3,2},{4,5},{5,4},{6,7},{7,6},{8,9},{9,8},{10,11... | collective-permute-start | bytes 786440 | tf_op jit(solution)/shard_map/ppermute | solution.py:116
  16.2 0.0 copy-done
  16.2 1.3 %collective-permute-done.1 = f32[16,4096]{1,0:T(8,128)S(1)} collective-permute-done((f32[16,4096]{1,0:T(8,128)}, f32[16,4096]{1,0:T(8,128)S(1)}, u32[]{:S(2)}, u32[]{:S(2)}) %collective-permute-start.1) | collective-permute-done | bytes 262176 | tf_op jit(solution)/shard_map/ppermute | solution.py:116
  17.5 1.0 %broadcast_select_fusion.2 = f32[16,4096]{1,0:T(8,128)S(1)} fusion(f32[16,4096]{1,0:T(8,128)} %shard_map.68, f32[16,4096]{1,0:T(8,128)S(1)} %collective-permute-done.1, pred[]{:T(512)S(6)} %eq.8), kind=kLoop, calls=%fused_computation.16 | loop fusion | flops 65536 | bytes 786433 | tf_op jit(solution)/shard_map/jit(_where)/select_n | solution.py:128
  18.5 0.9 %fusion.1 = f32[16,2048]{1,0:T(8,128)S(1)} fusion(f32[16,4096]{1,0:T(8,128)} %shard_map.68, s32[]{:T(128)S(6)} %select_n.61, f32[16,4096]{1,0:T(8,128)S(1)} %collective-permute-done.1, f32[16,4096]{1,0:T(8,128)S(1)} %broadcast_select_fusion.2, f32[16,4096]{1,0:T(8,128)S(1)} %multiply_exponential_fusion, pred[]{:T(512)S(6)} %eq.8), kind=kLoop, calls=%fused_computation.12 | loop fusion | flops 98304 | bytes 655365 | tf_op jit(solution)/shard_map/add | solution.py:135
  19.5 16.4 %all-gather = f32[64,2048]{1,0:T(8,128)S(1)} all-gather(f32[16,2048]{1,0:T(8,128)S(1)} %fusion.1), channel_id=2, replica_groups=mesh['grp'=2,'ctx'=4,'chan'=2,'dec'=2] {'ctx'}, dimensions={0}, use_global_device_ids=true | all-gather | bytes 655360 | tf_op jit(solution)/shard_map/all_gather | solution.py:136
  35.9 0.1 select_select_fusion
  36.0 0.1 collective-permute-start.2
  36.0 1.5 %collective-permute-done.2 = f32[32,2048]{1,0:T(8,128)S(1)} collective-permute-done((f32[32,2048]{1,0:T(8,128)S(1)}, f32[32,2048]{1,0:T(8,128)S(1)}, u32[]{:S(2)}, u32[]{:S(2)}) %collective-permute-start.2) | collective-permute-done | bytes 262176 | tf_op jit(solution)/shard_map/ppermute | solution.py:116
  37.6 0.8 %pad_maximum_fusion = (f32[16,4096]{1,0:T(8,128)}, f32[16,4096]{1,0:T(8,128)}) fusion(f32[32,2048]{1,0:T(8,128)S(1)} %get-tuple-element.7, f32[32,2048]{1,0:T(8,128)S(1)} %get-tuple-element.6, f32[16,4096]{1,0:T(8,128)S(1)} %broadcast_select_fusion.2, f32[16,4096]{1,0:T(8,128)S(1)} %copy-done, pred[]{:T(512)S(6)} %eq.8), kind=kLoop, calls=%fused_computation.3 | loop fusion | flops 458752 | bytes 1572865 | tf_op jit(solution)/shard_map/concatenate | solution.py:147
  38.4 13.6 %shard_map.69 = bf16[128,4096]{1,0:T(8,128)(2,1)} custom-call(bf16[3,128,4096]{2,1,0:T(8,128)(2,1)} %x_ref.3, bf16[3,2,4096]{2,1,0:T(2,128)(2,1)} %copy-done.1, f32[3,3,4096]{2,1,0:T(4,128)} %filt_ref.3, f32[16,4096]{1,0:T(8,128)} %rate_ref.3, f32[16,4096]{1,0:T(8,128)} %res_ref.1, f32[1,4096]{1,0:T(1,128)} %bitcast.1, f32[16,4096]{1,0:T(8,128)} %get-tuple-element.5.init_ref), custom_call_target="tpu_custom_call" | custom-call | tf_op jit(solution)/shard_map/pallas_call | solution.py:102
  (3 shorter events, 0.1 us)
Async XLA Ops:
  0.6 15.5 %copy-start = (f32[16,4096]{1,0:T(8,128)S(1)}, f32[16,4096]{1,0:T(8,128)}, u32[]{:S(2)}) copy-start(f32[16,4096]{1,0:T(8,128)} %rate_ref.3) | copy-start | bytes 786436
  1.7 3.2 %collective-permute-start = (bf16[3,2,4096]{2,1,0:T(2,128)(2,1)S(1)}, bf16[3,2,4096]{2,1,0:T(2,128)(2,1)S(1)}, u32[]{:S(2)}, u32[]{:S(2)}) collective-permute-start(bf16[3,2,4096]{2,1,0:T(2,128)(2,1)S(1)} %slice.21), channel_id=1, source_target_pairs={{0,1},{1,4},{4,5},{5,8},{8,9},{9,12},{12,13},{2,3},{3,6},{6,7},{7,... | collective-permute-start | bytes 147464 | tf_op jit(solution)/shard_map/ppermute | solution.py:17
  4.9 0.6 %copy-start.1 = (bf16[3,2,4096]{2,1,0:T(2,128)(2,1)}, bf16[3,2,4096]{2,1,0:T(2,128)(2,1)S(1)}, u32[]{:S(2)}) copy-start(bf16[3,2,4096]{2,1,0:T(2,128)(2,1)S(1)} %collective-permute-done.halo_ref) | copy-start | bytes 147460
  13.2 4.4 %collective-permute-start.1 = (f32[16,4096]{1,0:T(8,128)}, f32[16,4096]{1,0:T(8,128)S(1)}, u32[]{:S(2)}, u32[]{:S(2)}) collective-permute-start(f32[16,4096]{1,0:T(8,128)} %shard_map.68), channel_id=1, source_target_pairs={{0,1},{1,0},{2,3},{3,2},{4,5},{5,4},{6,7},{7,6},{8,9},{9,8},{10,11... | collective-permute-start | bytes 786440 | tf_op jit(solution)/shard_map/ppermute | solution.py:116
  36.0 1.6 %collective-permute-start.2 = (f32[32,2048]{1,0:T(8,128)S(1)}, f32[32,2048]{1,0:T(8,128)S(1)}, u32[]{:S(2)}, u32[]{:S(2)}) collective-permute-start(f32[32,2048]{1,0:T(8,128)S(1)} %pad_maximum_fusion.1), channel_id=1, source_target_pairs={{0,1},{1,0},{2,3},{3,2},{4,5},{5,4},{6,7},{7,6},{8,9},{9,8},{10,11... | collective-permute-start | bytes 786440 | tf_op jit(solution)/shard_map/ppermute | solution.py:116

commit v3 on v2

--- a/solution.py
+++ b/solution.py
@@ -133,13 +133,19 @@
     mine = lambda x: lax.dynamic_slice_in_dim(x, start, half, 1)
     chip_decay = mine(shard_decay) * mine(shard_decay)
     chip_part = mine(shard_decay) * mine(first_core) + mine(second_core)
-    received = lax.all_gather(chip_part, "ctx", axis=0, tiled=False)
     chip_here = lax.axis_index("ctx")
+    chips = lax.axis_size("ctx")
+    ahead = [from_behind(chip_part, "ctx", k) for k in range(1, chips)]
+    behind = [from_behind(chip_part, "ctx", -k) for k in range(1, chips)]
     running = jnp.zeros_like(chip_part)
     entering = jnp.zeros_like(chip_part)
-    for chip in range(received.shape[0]):
+    for chip in range(chips):
+        part = chip_part
+        for k in range(1, chips):
+            part = jnp.where(chip_here - k == chip, ahead[k - 1], part)
+            part = jnp.where(chip_here + k == chip, behind[k - 1], part)
         entering = jnp.where(chip_here == chip, running, entering)
-        running = chip_decay * running + received[chip]
+        running = chip_decay * running + part
     both = jnp.concatenate([entering, running], axis=0)
     other_both = swap_cores(both)
     low = jnp.where(core == 0, both, other_both)

time: 52.4 us -> 59.4 us (1.13)
  starting transfers between devices: 5.41 us -> 25.8 us
  blocking collectives: 16.4 us -> 0 us
  waiting for transfers between devices: 3.69 us -> 6.11 us
    ppermute x1 -> x7, starting transfers between devices: 2.36 us -> 22.8 us  [from_behind(): lax.ppermute(value, axis, [(source, source + steps) for source in range(i...]
    all_gather x1 -> x0, blocking collectives: 16.4 us -> none  [local(): received = lax.all_gather(chip_part, 'ctx', axis=0, tiled=False)]
    ppermute x1 -> x7, waiting for transfers between devices: 0.86 us -> 3.27 us  [from_behind(): lax.ppermute(value, axis, [(source, source + steps) for source in range(i...]
  transfers between devices with their start and end apart: 3 -> 9, of which waited for: 3 -> 5; matrix products, arithmetic and copies ran while one was open for 0% -> 0% of each run, Pallas kernels for 0% -> 0%
where the time goes in v3:
time: 59.4 us; the launch traced here: 59 us
  starting transfers between devices  25.8 us (43%)
  Pallas kernels  21.3 us (36%)
  waiting for transfers between devices  6.11 us (10%)
  other arithmetic  3.25 us (5%)
  local copies, waits for them, and re-layouts  1.64 us (3%)
  between operations  0.84 us (1%)
    ppermute x7, starting transfers between devices, from_behind(): lax.ppermute(value, axis, [(source, source + steps) for source in range(i...  22.8 us
    pallas_call x1, Pallas kernels, mix(): pl.pallas_call(_mix_kernel, grid=(chan_count // CHAN_BLOCK,), in_specs=[x...  13.6 us
    pallas_call x1, Pallas kernels, contributions(): pl.pallas_call(_contrib_kernel, grid=(chan_count // CHAN_BLOCK,), in_spec...  7.66 us
    ppermute x7, waiting for transfers between devices, from_behind(): lax.ppermute(value, axis, [(source, source + steps) for source in range(i...  3.27 us
    ppermute x2, starting transfers between devices, swap_cores(): return lax.ppermute(value, 'dec', [(0, 1), (1, 0)])  3.05 us
    ppermute x2, waiting for transfers between devices, swap_cores(): return lax.ppermute(value, 'dec', [(0, 1), (1, 0)])  2.84 us
  transfers between devices with their start and end apart: 9, of which 5 were waited for; matrix products, arithmetic and copies ran while one was open for 0% of the time, Pallas kernels for 0%

profile of v3, /device:TPU:0, one launch (start us, length us, event | category | flops | bytes accessed | tf_op | source)
XLA Modules:
  0.0 59.0 jit_solution(4042909013077810583)
XLA Ops:
  0.6 0.0 copy-start
  0.6 1.0 %slice.9 = bf16[3,2,4096]{2,1,0:T(2,128)(2,1)S(1)} slice(bf16[3,128,4096]{2,1,0:T(8,128)(2,1)} %x_ref.3), slice={[0:3], [126:128], [0:4096]} | slice | bytes 98304 | tf_op jit(solution)/shard_map/slice | solution.py:123
  1.7 2.4 %collective-permute-start = (bf16[3,2,4096]{2,1,0:T(2,128)(2,1)S(1)}, bf16[3,2,4096]{2,1,0:T(2,128)(2,1)S(1)}, u32[]{:S(2)}, u32[]{:S(2)}) collective-permute-start(bf16[3,2,4096]{2,1,0:T(2,128)(2,1)S(1)} %slice.9), channel_id=1, source_target_pairs={{0,1},{1,4},{4,5},{5,8},{8,9},{9,12},{12,13},{2,3},{3,6},{6,7},{7,... | collective-permute-start | bytes 147464 | tf_op jit(solution)/shard_map/ppermute | solution.py:17
  4.0 0.9 %collective-permute-done.halo_ref = bf16[3,2,4096]{2,1,0:T(2,128)(2,1)S(1)} collective-permute-done((bf16[3,2,4096]{2,1,0:T(2,128)(2,1)S(1)}, bf16[3,2,4096]{2,1,0:T(2,128)(2,1)S(1)}, u32[]{:S(2)}, u32[]{:S(2)}) %collective-permute-start) | collective-permute-done | bytes 49184 | tf_op jit(solution)/shard_map/ppermute | solution.py:17
  4.9 0.0 copy-start.1
  4.9 0.6 %copy-done.1 = bf16[3,2,4096]{2,1,0:T(2,128)(2,1)} copy-done((bf16[3,2,4096]{2,1,0:T(2,128)(2,1)}, bf16[3,2,4096]{2,1,0:T(2,128)(2,1)S(1)}, u32[]{:S(2)}) %copy-start.1) | copy-done | bytes 49176
  5.5 7.7 %shard_map.68 = f32[16,4096]{1,0:T(8,128)} custom-call(bf16[3,128,4096]{2,1,0:T(8,128)(2,1)} %x_ref.3, bf16[3,2,4096]{2,1,0:T(2,128)(2,1)} %copy-done.1, f32[3,3,4096]{2,1,0:T(4,128)} %filt_ref.3, f32[16,4096]{1,0:T(8,128)} %rate_ref.3), custom_call_target="tpu_custom_call" | custom-call | tf_op jit(solution)/shard_map/pallas_call | solution.py:87
  13.2 3.0 %collective-permute-start.1 = (f32[16,4096]{1,0:T(8,128)}, f32[16,4096]{1,0:T(8,128)S(1)}, u32[]{:S(2)}, u32[]{:S(2)}) collective-permute-start(f32[16,4096]{1,0:T(8,128)} %shard_map.68), channel_id=1, source_target_pairs={{0,1},{1,0},{2,3},{3,2},{4,5},{5,4},{6,7},{7,6},{8,9},{9,8},{10,11... | collective-permute-start | bytes 786440 | tf_op jit(solution)/shard_map/ppermute | solution.py:116
  16.2 0.0 copy-done
  16.2 1.3 %collective-permute-done.1 = f32[16,4096]{1,0:T(8,128)S(1)} collective-permute-done((f32[16,4096]{1,0:T(8,128)}, f32[16,4096]{1,0:T(8,128)S(1)}, u32[]{:S(2)}, u32[]{:S(2)}) %collective-permute-start.1) | collective-permute-done | bytes 262176 | tf_op jit(solution)/shard_map/ppermute | solution.py:116
  17.5 1.0 %broadcast_select_fusion.2 = f32[16,4096]{1,0:T(8,128)S(1)} fusion(f32[16,4096]{1,0:T(8,128)} %shard_map.68, f32[16,4096]{1,0:T(8,128)S(1)} %collective-permute-done.1, pred[]{:T(512)S(6)} %eq.89), kind=kLoop, calls=%fused_computation.16 | loop fusion | flops 65536 | bytes 786433 | tf_op jit(solution)/shard_map/jit(_where)/select_n | solution.py:128
  18.5 0.9 %fusion.1 = f32[16,2048]{1,0:T(8,128)S(1)} fusion(f32[16,4096]{1,0:T(8,128)} %shard_map.68, s32[]{:T(128)S(6)} %select_n.205, f32[16,4096]{1,0:T(8,128)S(1)} %collective-permute-done.1, f32[16,4096]{1,0:T(8,128)S(1)} %broadcast_select_fusion.2, f32[16,4096]{1,0:T(8,128)S(1)} %multiply_exponential_fusion, pred[]{:T(512)S(6)} %eq.89), kind=kLoop, calls=%fused_computation.8 | loop fusion | flops 98304 | bytes 655365 | tf_op jit(solution)/shard_map/add | solution.py:135
  19.4 1.3 %collective-permute-start.2 = (f32[16,2048]{1,0:T(8,128)S(1)}, f32[16,2048]{1,0:T(8,128)S(1)}, u32[]{:S(2)}, u32[]{:S(2)}) collective-permute-start(f32[16,2048]{1,0:T(8,128)S(1)} %fusion.1), channel_id=1, source_target_pairs={{12,0},{13,1},{14,2},{15,3},{28,16},{29,17},{30,18},{31,19}} | collective-permute-start | bytes 393224 | tf_op jit(solution)/shard_map/ppermute | solution.py:17
  20.7 6.5 %collective-permute-start.3 = (f32[16,2048]{1,0:T(8,128)S(1)}, f32[16,2048]{1,0:T(8,128)S(1)}, u32[]{:S(2)}, u32[]{:S(2)}) collective-permute-start(f32[16,2048]{1,0:T(8,128)S(1)} %fusion.1), channel_id=1, source_target_pairs={{0,12},{1,13},{2,14},{3,15},{16,28},{17,29},{18,30},{19,31}} | collective-permute-start | bytes 393224 | tf_op jit(solution)/shard_map/ppermute | solution.py:17
  27.3 1.3 %collective-permute-start.4 = (f32[16,2048]{1,0:T(8,128)S(1)}, f32[16,2048]{1,0:T(8,128)S(1)}, u32[]{:S(2)}, u32[]{:S(2)}) collective-permute-start(f32[16,2048]{1,0:T(8,128)S(1)} %fusion.1), channel_id=1, source_target_pairs={{8,0},{12,4},{9,1},{13,5},{10,2},{14,6},{11,3},{15,7},{24,16},{28,... | collective-permute-start | bytes 393224 | tf_op jit(solution)/shard_map/ppermute | solution.py:17
  28.6 5.5 %collective-permute-start.5 = (f32[16,2048]{1,0:T(8,128)S(1)}, f32[16,2048]{1,0:T(8,128)S(1)}, u32[]{:S(2)}, u32[]{:S(2)}) collective-permute-start(f32[16,2048]{1,0:T(8,128)S(1)} %fusion.1), channel_id=1, source_target_pairs={{0,8},{4,12},{1,9},{5,13},{2,10},{6,14},{3,11},{7,15},{16,24},{20,... | collective-permute-start | bytes 393224 | tf_op jit(solution)/shard_map/ppermute | solution.py:17
  34.1 1.3 %collective-permute-start.6 = (f32[16,2048]{1,0:T(8,128)S(1)}, f32[16,2048]{1,0:T(8,128)S(1)}, u32[]{:S(2)}, u32[]{:S(2)}) collective-permute-start(f32[16,2048]{1,0:T(8,128)S(1)} %fusion.1), channel_id=1, source_target_pairs={{4,0},{8,4},{12,8},{5,1},{9,5},{13,9},{6,2},{10,6},{14,10},{7,3},{... | collective-permute-start | bytes 393224 | tf_op jit(solution)/shard_map/ppermute | solution.py:17
  35.4 0.0 collective-permute-done.2
  35.4 4.6 %collective-permute-start.7 = (f32[16,2048]{1,0:T(8,128)S(1)}, f32[16,2048]{1,0:T(8,128)S(1)}, u32[]{:S(2)}, u32[]{:S(2)}) collective-permute-start(f32[16,2048]{1,0:T(8,128)S(1)} %fusion.1), channel_id=1, source_target_pairs={{0,4},{4,8},{8,12},{1,5},{5,9},{9,13},{2,6},{6,10},{10,14},{3,7},{... | collective-permute-start | bytes 393224 | tf_op jit(solution)/shard_map/ppermute | solution.py:17
  40.0 0.0 collective-permute-done.3
  40.0 0.0 collective-permute-done.4
  40.0 0.0 collective-permute-done.5
  40.0 0.9 %collective-permute-done.6 = f32[16,2048]{1,0:T(8,128)S(1)} collective-permute-done((f32[16,2048]{1,0:T(8,128)S(1)}, f32[16,2048]{1,0:T(8,128)S(1)}, u32[]{:S(2)}, u32[]{:S(2)}) %collective-permute-start.6) | collective-permute-done | bytes 131104 | tf_op jit(solution)/shard_map/ppermute | solution.py:17
  40.9 1.5 %collective-permute-done.7 = f32[16,2048]{1,0:T(8,128)S(1)} collective-permute-done((f32[16,2048]{1,0:T(8,128)S(1)}, f32[16,2048]{1,0:T(8,128)S(1)}, u32[]{:S(2)}, u32[]{:S(2)}) %collective-permute-start.7) | collective-permute-done | bytes 131104 | tf_op jit(solution)/shard_map/ppermute | solution.py:17
  42.4 0.2 select_select_fusion
  42.6 0.2 select_add_fusion
  42.8 0.1 collective-permute-start.8
  42.9 1.5 %collective-permute-done.8 = f32[32,2048]{1,0:T(8,128)S(1)} collective-permute-done((f32[32,2048]{1,0:T(8,128)S(1)}, f32[32,2048]{1,0:T(8,128)S(1)}, u32[]{:S(2)}, u32[]{:S(2)}) %collective-permute-start.8) | collective-permute-done | bytes 262176 | tf_op jit(solution)/shard_map/ppermute | solution.py:116
  44.5 0.8 %pad_maximum_fusion = (f32[16,4096]{1,0:T(8,128)}, f32[16,4096]{1,0:T(8,128)}) fusion(f32[32,2048]{1,0:T(8,128)S(1)} %get-tuple-element.5, f32[32,2048]{1,0:T(8,128)S(1)} %get-tuple-element.4, f32[16,4096]{1,0:T(8,128)S(1)} %broadcast_select_fusion.2, f32[16,4096]{1,0:T(8,128)S(1)} %copy-done, pred[]{:T(512)S(6)} %eq.89), kind=kLoop, calls=%fused_computation.3 | loop fusion | flops 458752 | bytes 1572865 | tf_op jit(solution)/shard_map/concatenate | solution.py:153
  45.3 13.6 %shard_map.69 = bf16[128,4096]{1,0:T(8,128)(2,1)} custom-call(bf16[3,128,4096]{2,1,0:T(8,128)(2,1)} %x_ref.3, bf16[3,2,4096]{2,1,0:T(2,128)(2,1)} %copy-done.1, f32[3,3,4096]{2,1,0:T(4,128)} %filt_ref.3, f32[16,4096]{1,0:T(8,128)} %rate_ref.3, f32[16,4096]{1,0:T(8,128)} %res_ref.1, f32[1,4096]{1,0:T(1,128)} %bitcast.1, f32[16,4096]{1,0:T(8,128)} %get-tuple-element.3.init_ref), custom_call_target="tpu_custom_call" | custom-call | tf_op jit(solution)/shard_map/pallas_call | solution.py:102
  (3 shorter events, 0.1 us)
Async XLA Ops:
  0.6 15.5 %copy-start = (f32[16,4096]{1,0:T(8,128)S(1)}, f32[16,4096]{1,0:T(8,128)}, u32[]{:S(2)}) copy-start(f32[16,4096]{1,0:T(8,128)} %rate_ref.3) | copy-start | bytes 786436
  1.7 3.2 %collective-permute-start = (bf16[3,2,4096]{2,1,0:T(2,128)(2,1)S(1)}, bf16[3,2,4096]{2,1,0:T(2,128)(2,1)S(1)}, u32[]{:S(2)}, u32[]{:S(2)}) collective-permute-start(bf16[3,2,4096]{2,1,0:T(2,128)(2,1)S(1)} %slice.9), channel_id=1, source_target_pairs={{0,1},{1,4},{4,5},{5,8},{8,9},{9,12},{12,13},{2,3},{3,6},{6,7},{7,... | collective-permute-start | bytes 147464 | tf_op jit(solution)/shard_map/ppermute | solution.py:17
  4.9 0.6 %copy-start.1 = (bf16[3,2,4096]{2,1,0:T(2,128)(2,1)}, bf16[3,2,4096]{2,1,0:T(2,128)(2,1)S(1)}, u32[]{:S(2)}) copy-start(bf16[3,2,4096]{2,1,0:T(2,128)(2,1)S(1)} %collective-permute-done.halo_ref) | copy-start | bytes 147460
  13.2 4.4 %collective-permute-start.1 = (f32[16,4096]{1,0:T(8,128)}, f32[16,4096]{1,0:T(8,128)S(1)}, u32[]{:S(2)}, u32[]{:S(2)}) collective-permute-start(f32[16,4096]{1,0:T(8,128)} %shard_map.68), channel_id=1, source_target_pairs={{0,1},{1,0},{2,3},{3,2},{4,5},{5,4},{6,7},{7,6},{8,9},{9,8},{10,11... | collective-permute-start | bytes 786440 | tf_op jit(solution)/shard_map/ppermute | solution.py:116
  19.4 15.9 %collective-permute-start.2 = (f32[16,2048]{1,0:T(8,128)S(1)}, f32[16,2048]{1,0:T(8,128)S(1)}, u32[]{:S(2)}, u32[]{:S(2)}) collective-permute-start(f32[16,2048]{1,0:T(8,128)S(1)} %fusion.1), channel_id=1, source_target_pairs={{12,0},{13,1},{14,2},{15,3},{28,16},{29,17},{30,18},{31,19}} | collective-permute-start | bytes 393224 | tf_op jit(solution)/shard_map/ppermute | solution.py:17
  20.7 19.2 %collective-permute-start.3 = (f32[16,2048]{1,0:T(8,128)S(1)}, f32[16,2048]{1,0:T(8,128)S(1)}, u32[]{:S(2)}, u32[]{:S(2)}) collective-permute-start(f32[16,2048]{1,0:T(8,128)S(1)} %fusion.1), channel_id=1, source_target_pairs={{0,12},{1,13},{2,14},{3,15},{16,28},{17,29},{18,30},{19,31}} | collective-permute-start | bytes 393224 | tf_op jit(solution)/shard_map/ppermute | solution.py:17
  27.3 12.7 %collective-permute-start.4 = (f32[16,2048]{1,0:T(8,128)S(1)}, f32[16,2048]{1,0:T(8,128)S(1)}, u32[]{:S(2)}, u32[]{:S(2)}) collective-permute-start(f32[16,2048]{1,0:T(8,128)S(1)} %fusion.1), channel_id=1, source_target_pairs={{8,0},{12,4},{9,1},{13,5},{10,2},{14,6},{11,3},{15,7},{24,16},{28,... | collective-permute-start | bytes 393224 | tf_op jit(solution)/shard_map/ppermute | solution.py:17
  28.6 11.4 %collective-permute-start.5 = (f32[16,2048]{1,0:T(8,128)S(1)}, f32[16,2048]{1,0:T(8,128)S(1)}, u32[]{:S(2)}, u32[]{:S(2)}) collective-permute-start(f32[16,2048]{1,0:T(8,128)S(1)} %fusion.1), channel_id=1, source_target_pairs={{0,8},{4,12},{1,9},{5,13},{2,10},{6,14},{3,11},{7,15},{16,24},{20,... | collective-permute-start | bytes 393224 | tf_op jit(solution)/shard_map/ppermute | solution.py:17
  34.1 6.9 %collective-permute-start.6 = (f32[16,2048]{1,0:T(8,128)S(1)}, f32[16,2048]{1,0:T(8,128)S(1)}, u32[]{:S(2)}, u32[]{:S(2)}) collective-permute-start(f32[16,2048]{1,0:T(8,128)S(1)} %fusion.1), channel_id=1, source_target_pairs={{4,0},{8,4},{12,8},{5,1},{9,5},{13,9},{6,2},{10,6},{14,10},{7,3},{... | collective-permute-start | bytes 393224 | tf_op jit(solution)/shard_map/ppermute | solution.py:17
  35.4 7.1 %collective-permute-start.7 = (f32[16,2048]{1,0:T(8,128)S(1)}, f32[16,2048]{1,0:T(8,128)S(1)}, u32[]{:S(2)}, u32[]{:S(2)}) collective-permute-start(f32[16,2048]{1,0:T(8,128)S(1)} %fusion.1), channel_id=1, source_target_pairs={{0,4},{4,8},{8,12},{1,5},{5,9},{9,13},{2,6},{6,10},{10,14},{3,7},{... | collective-permute-start | bytes 393224 | tf_op jit(solution)/shard_map/ppermute | solution.py:17
  42.8 1.6 %collective-permute-start.8 = (f32[32,2048]{1,0:T(8,128)S(1)}, f32[32,2048]{1,0:T(8,128)S(1)}, u32[]{:S(2)}, u32[]{:S(2)}) collective-permute-start(f32[32,2048]{1,0:T(8,128)S(1)} %pad_maximum_fusion.1), channel_id=1, source_target_pairs={{0,1},{1,0},{2,3},{3,2},{4,5},{5,4},{6,7},{7,6},{8,9},{9,8},{10,11... | collective-permute-start | bytes 786440 | tf_op jit(solution)/shard_map/ppermute | solution.py:116

commit v4 on v2

--- a/solution.py
+++ b/solution.py
@@ -58,16 +58,44 @@
     out_ref[...] = _scan_rows(drive_scr, decay, None, state, None)
 
 
-def _mix_kernel(x_ref, halo_ref, filt_ref, rate_ref, res_ref, skip_ref, init_ref, out_ref,
-                drive_scr, conv_scr):
+def _local_kernel(x_ref, halo_ref, filt_ref, rate_ref, res_ref, skip_ref, out_ref, drive_scr):
     k = _featurize_one(x_ref, halo_ref, filt_ref, 1)
     v = _featurize_one(x_ref, halo_ref, filt_ref, 2)
-    drive = k * v
-    drive_scr[...] = drive
+    drive_scr[...] = k * v
     decay = jnp.exp(-rate_ref[...])
-    _scan_rows(drive_scr, decay, res_ref[...], init_ref[...], conv_scr)
+    state = jnp.zeros(rate_ref.shape, jnp.float32)
+    _scan_rows(drive_scr, decay, res_ref[...], state, out_ref)
+    out_ref[...] = out_ref[...] + skip_ref[...] * drive_scr[...]
+
+
+def _finish_kernel(x_ref, halo_ref, filt_ref, rate_ref, res_ref, init_ref, local_ref, out_ref,
+                   corr_scr):
+    modes, chan_block = rate_ref.shape
+    row_count = local_ref.shape[0]
+    lanes = 128
+    steps = lax.broadcasted_iota(jnp.int32, (ROW_GROUP, lanes), 0).astype(jnp.float32) + 1.0
+    for group in range(chan_block // lanes):
+        cols = slice(group * lanes, (group + 1) * lanes)
+        rate = rate_ref[:, cols]
+        weight = res_ref[:, cols] * init_ref[:, cols]
+        terms = []
+        jumps = []
+        for m in range(modes):
+            rate_m = jnp.broadcast_to(rate[m : m + 1], (ROW_GROUP, lanes))
+            terms.append(jnp.broadcast_to(weight[m : m + 1], (ROW_GROUP, lanes)) * jnp.exp(-rate_m * steps))
+            jumps.append(jnp.exp(-rate_m * float(ROW_GROUP)))
+
+        def body(block, terms):
+            start = pl.multiple_of(block * ROW_GROUP, ROW_GROUP)
+            total = terms[0]
+            for m in range(1, modes):
+                total = total + terms[m]
+            corr_scr[pl.ds(start, ROW_GROUP), cols] = total
+            return tuple(terms[m] * jumps[m] for m in range(modes))
+
+        lax.fori_loop(0, row_count // ROW_GROUP, body, tuple(terms))
     q = _featurize_one(x_ref, halo_ref, filt_ref, 0)
-    out_ref[...] = (q * (conv_scr[...] + skip_ref[...] * drive_scr[...])).astype(out_ref.dtype)
+    out_ref[...] = (q * (local_ref[...] + corr_scr[...])).astype(out_ref.dtype)
 
 
 def _specs(row_count, modes, taps):
@@ -94,22 +122,35 @@
     )(projected, halo, short_filters, decay_rate)
 
 
-def mix(projected, halo, short_filters, decay_rate, residue, skip, prefix):
+def local_scan(projected, halo, short_filters, decay_rate, residue, skip):
     _, row_count, chan_count = projected.shape
     modes = decay_rate.shape[0]
     taps = short_filters.shape[1]
     x_spec, halo_spec, filt_spec, mode_spec, row_spec = _specs(row_count, modes, taps)
     return pl.pallas_call(
-        _mix_kernel,
+        _local_kernel,
         grid=(chan_count // CHAN_BLOCK,),
-        in_specs=[x_spec, halo_spec, filt_spec, mode_spec, mode_spec, row_spec, mode_spec],
+        in_specs=[x_spec, halo_spec, filt_spec, mode_spec, mode_spec, row_spec],
         out_specs=pl.BlockSpec((row_count, CHAN_BLOCK), lambda j: (0, j)),
+        out_shape=jax.ShapeDtypeStruct((row_count, chan_count), jnp.float32),
+        scratch_shapes=[pltpu.VMEM((row_count, CHAN_BLOCK), jnp.float32)],
+    )(projected, halo, short_filters, decay_rate, residue, skip[None, :])
+
+
+def finish(projected, halo, short_filters, decay_rate, residue, prefix, local_part):
+    _, row_count, chan_count = projected.shape
+    modes = decay_rate.shape[0]
+    taps = short_filters.shape[1]
+    x_spec, halo_spec, filt_spec, mode_spec, _ = _specs(row_count, modes, taps)
+    tile_spec = pl.BlockSpec((row_count, CHAN_BLOCK), lambda j: (0, j))
+    return pl.pallas_call(
+        _finish_kernel,
+        grid=(chan_count // CHAN_BLOCK,),
+        in_specs=[x_spec, halo_spec, filt_spec, mode_spec, mode_spec, mode_spec, tile_spec],
+        out_specs=tile_spec,
         out_shape=jax.ShapeDtypeStruct((row_count, chan_count), jnp.bfloat16),
-        scratch_shapes=[
-            pltpu.VMEM((row_count, CHAN_BLOCK), jnp.float32),
-            pltpu.VMEM((row_count, CHAN_BLOCK), jnp.float32),
-        ],
-    )(projected, halo, short_filters, decay_rate, residue, skip[None, :], prefix)
+        scratch_shapes=[pltpu.VMEM((row_count, CHAN_BLOCK), jnp.float32)],
+    )(projected, halo, short_filters, decay_rate, residue, prefix, local_part)
 
 
 def swap_cores(value):
@@ -131,26 +172,20 @@
     half = chan_count // 2
     start = core * half
     mine = lambda x: lax.dynamic_slice_in_dim(x, start, half, 1)
-    chip_decay = mine(shard_decay) * mine(shard_decay)
     chip_part = mine(shard_decay) * mine(first_core) + mine(second_core)
-    received = lax.all_gather(chip_part, "ctx", axis=0, tiled=False)
+    received = lax.all_gather(chip_part, ("ctx", "dec"), axis=0, tiled=False)
+    local_part = local_scan(projected, halo, short_filters, decay_rate, residue, skip)
     chip_here = lax.axis_index("ctx")
-    running = jnp.zeros_like(chip_part)
-    entering = jnp.zeros_like(chip_part)
-    for chip in range(received.shape[0]):
+    chip_decay = shard_decay * shard_decay
+    running = jnp.zeros_like(contribution)
+    entering = jnp.zeros_like(contribution)
+    for chip in range(received.shape[0] // 2):
+        part = jnp.concatenate([received[2 * chip], received[2 * chip + 1]], axis=1)
         entering = jnp.where(chip_here == chip, running, entering)
-        running = chip_decay * running + received[chip]
-    both = jnp.concatenate([entering, running], axis=0)
-    other_both = swap_cores(both)
-    low = jnp.where(core == 0, both, other_both)
-    high = jnp.where(core == 0, other_both, both)
-    whole = jnp.concatenate([low, high], axis=1)
-    modes = decay_rate.shape[0]
-    chip_entering = whole[:modes]
-    final_state = whole[modes:]
-    prefix = jnp.where(core == 0, chip_entering, shard_decay * chip_entering + first_core)
-    mixed = mix(projected, halo, short_filters, decay_rate, residue, skip, prefix)
-    return (mixed, final_state)
+        running = chip_decay * running + part
+    prefix = jnp.where(core == 0, entering, shard_decay * entering + first_core)
+    mixed = finish(projected, halo, short_filters, decay_rate, residue, prefix, local_part)
+    return (mixed, running)
 
 
 def solution(mesh):

time: 52.4 us -> 74 us (1.41)
  blocking collectives: 16.4 us -> 0 us
  between operations: 0.7 us -> 14.1 us
  Pallas kernels: 21.3 us -> 33 us
  waiting for transfers between devices: 3.69 us -> 13.8 us
  local copies, waits for them, and re-layouts: 1.65 us -> 3.02 us
  other arithmetic: 2.92 us -> 4.28 us
    all_gather x1 -> x0, blocking collectives: 16.4 us -> none  [local(): received = lax.all_gather(chip_part, 'ctx', axis=0, tiled=False)]
    pallas_call x1 -> x2, Pallas kernels: 13.6 us -> 25.3 us  [the longest x1 13 us: local_scan(): pl.pallas_call(_local_kernel, grid=(chan_count // CHAN_BLOCK,), in_specs=...]
    all_gather x0 -> x1, waiting for transfers between devices: none -> 11.6 us  [local(): received = lax.all_gather(chip_part, ('ctx', 'dec'), axis=0, tiled=False)]
    ppermute x2 -> x1, waiting for transfers between devices: 2.83 us -> 1.32 us  [swap_cores(): return lax.ppermute(value, 'dec', [(0, 1), (1, 0)])]
    slice x0 -> x1, local copies, waits for them, and re-layouts: none -> 1.37 us  [local(): part = jnp.concatenate([received[2 * chip], received[2 * chip + 1]], axis=1)]
    concatenate x2 -> x0, other arithmetic: 0.86 us -> none  [the longest x1 0.84 us: local(): whole = jnp.concatenate([low, high], axis=1)]
    add x0 -> x1, other arithmetic: none -> 0.82 us  [local(): running = chip_decay * running + part]
    select_n x2 -> x1, other arithmetic: 0.1 us -> 0.85 us  [local(): prefix = jnp.where(core == 0, entering, shard_decay * entering + first_core)]
  transfers between devices with their start and end apart: 3 -> 3, of which waited for: 3 -> 3; matrix products, arithmetic and copies ran while one was open for 0% -> 0% of each run, Pallas kernels for 0% -> 18%
where the time goes in v4:
time: 74 us; the launch traced here: 73.6 us
  Pallas kernels  33 us (45%)
  between operations  14.1 us (19%)
  waiting for transfers between devices  13.8 us (19%)
  starting transfers between devices  5.38 us (7%)
  other arithmetic  4.28 us (6%)
  local copies, waits for them, and re-layouts  3.02 us (4%)
    pallas_call x1, Pallas kernels, local_scan(): pl.pallas_call(_local_kernel, grid=(chan_count // CHAN_BLOCK,), in_specs=...  13 us
    pallas_call x1, Pallas kernels, finish(): pl.pallas_call(_finish_kernel, grid=(chan_count // CHAN_BLOCK,), in_specs...  12.4 us
    all_gather x1, waiting for transfers between devices, local(): received = lax.all_gather(chip_part, ('ctx', 'dec'), axis=0, tiled=False)  11.6 us
    pallas_call x1, Pallas kernels, contributions(): pl.pallas_call(_contrib_kernel, grid=(chan_count // CHAN_BLOCK,), in_spec...  7.66 us
    ppermute x1, starting transfers between devices, swap_cores(): return lax.ppermute(value, 'dec', [(0, 1), (1, 0)])  2.98 us
    ppermute x1, starting transfers between devices, from_behind(): lax.ppermute(value, axis, [(source, source + steps) for source in range(i...  2.36 us
    add x1, other arithmetic, local(): chip_part = mine(shard_decay) * mine(first_core) + mine(second_core)  1.59 us
  transfers between devices with their start and end apart: 3, of which 3 were waited for; matrix products, arithmetic and copies ran while one was open for 0% of the time, Pallas kernels for 18%

profile of v4, /device:TPU:0, one launch (start us, length us, event | category | flops | bytes accessed | tf_op | source)
XLA Modules:
  0.0 73.6 jit_solution(13633169067028745417)
XLA Ops:
  7.2 0.0 copy-start
  7.2 0.0 all-gather.3.cloned.1.call-start
  7.2 1.0 %slice.27 = bf16[3,2,4096]{2,1,0:T(2,128)(2,1)S(1)} slice(bf16[3,128,4096]{2,1,0:T(8,128)(2,1)} %x_ref.5), slice={[0:3], [126:128], [0:4096]} | slice | bytes 98304 | tf_op jit(solution)/shard_map/slice | solution.py:164
  8.2 2.4 %collective-permute-start = (bf16[3,2,4096]{2,1,0:T(2,128)(2,1)S(1)}, bf16[3,2,4096]{2,1,0:T(2,128)(2,1)S(1)}, u32[]{:S(2)}, u32[]{:S(2)}) collective-permute-start(bf16[3,2,4096]{2,1,0:T(2,128)(2,1)S(1)} %slice.27), channel_id=1, source_target_pairs={{0,1},{1,4},{4,5},{5,8},{8,9},{9,12},{12,13},{2,3},{3,6},{6,7},{7,... | collective-permute-start | bytes 147464 | tf_op jit(solution)/shard_map/ppermute | solution.py:17
  10.6 0.9 %collective-permute-done.halo_ref = bf16[3,2,4096]{2,1,0:T(2,128)(2,1)S(1)} collective-permute-done((bf16[3,2,4096]{2,1,0:T(2,128)(2,1)S(1)}, bf16[3,2,4096]{2,1,0:T(2,128)(2,1)S(1)}, u32[]{:S(2)}, u32[]{:S(2)}) %collective-permute-start) | collective-permute-done | bytes 49184 | tf_op jit(solution)/shard_map/ppermute | solution.py:17
  11.5 0.0 copy-start.2
  11.5 0.6 copy-done.2
  12.1 7.7 %shard_map.68 = f32[16,4096]{1,0:T(8,128)} custom-call(bf16[3,128,4096]{2,1,0:T(8,128)(2,1)} %x_ref.5, bf16[3,2,4096]{2,1,0:T(2,128)(2,1)} %copy-done.2, f32[3,3,4096]{2,1,0:T(4,128)} %filt_ref.5, f32[16,4096]{1,0:T(8,128)} %rate_ref.5), custom_call_target="tpu_custom_call" | custom-call | tf_op jit(solution)/shard_map/pallas_call | solution.py:115
  19.7 3.0 %collective-permute-start.1 = (f32[16,4096]{1,0:T(8,128)}, f32[16,4096]{1,0:T(8,128)S(1)}, u32[]{:S(2)}, u32[]{:S(2)}) collective-permute-start(f32[16,4096]{1,0:T(8,128)} %shard_map.68), channel_id=1, source_target_pairs={{0,1},{1,0},{2,3},{3,2},{4,5},{5,4},{6,7},{7,6},{8,9},{9,8},{10,11... | collective-permute-start | bytes 786440 | tf_op jit(solution)/shard_map/ppermute | solution.py:157
  22.7 0.0 copy-done
  22.8 1.3 %collective-permute-done.1 = f32[16,4096]{1,0:T(8,128)S(1)} collective-permute-done((f32[16,4096]{1,0:T(8,128)}, f32[16,4096]{1,0:T(8,128)S(1)}, u32[]{:S(2)}, u32[]{:S(2)}) %collective-permute-start.1) | collective-permute-done | bytes 262176 | tf_op jit(solution)/shard_map/ppermute | solution.py:157
  24.1 1.0 %broadcast_select_fusion = f32[16,4096]{1,0:T(8,128)S(1)} fusion(f32[16,4096]{1,0:T(8,128)} %shard_map.68, f32[16,4096]{1,0:T(8,128)S(1)} %collective-permute-done.1, pred[]{:T(512)S(6)} %eq.15), kind=kLoop, calls=%fused_computation.8 | loop fusion | flops 65536 | bytes 786433 | tf_op jit(solution)/shard_map/jit(_where)/select_n | solution.py:169
  25.1 1.6 %fusion = f32[16,2048]{1,0:T(8,128)} fusion(f32[16,4096]{1,0:T(8,128)} %shard_map.68, s32[]{:T(128)S(6)} %select_n.44, f32[16,4096]{1,0:T(8,128)S(1)} %collective-permute-done.1, f32[16,4096]{1,0:T(8,128)S(1)} %broadcast_select_fusion, f32[16,4096]{1,0:T(8,128)S(1)} %multiply_exponential_fusion, pred[]{:T(512)S(6)} %eq.15), kind=kLoop, calls=%fused_computation.7 | loop fusion | flops 98304 | bytes 655365 | tf_op jit(solution)/shard_map/add | solution.py:175
  26.7 0.0 all-gather.3.cloned.1.call-update
  26.7 0.0 copy-start.1
  26.7 13.0 %shard_map.69.local_ref = f32[128,4096]{1,0:T(8,128)} custom-call(bf16[3,128,4096]{2,1,0:T(8,128)(2,1)} %x_ref.5, bf16[3,2,4096]{2,1,0:T(2,128)(2,1)} %copy-done.2, f32[3,3,4096]{2,1,0:T(4,128)} %filt_ref.5, f32[16,4096]{1,0:T(8,128)} %rate_ref.5, f32[16,4096]{1,0:T(8,128)} %res_ref.3, f32[1,4096]{1,0:T(1,128)} %bitcast.1), custom_call_target="tpu_custom_call" | custom-call | tf_op jit(solution)/shard_map/pallas_call | solution.py:130
  39.7 11.6 %all-gather.3.cloned.1.call-done = f32[128,2048]{1,0:T(8,128)} async-done(((f32[16,2048]{1,0:T(8,128)}), f32[128,2048]{1,0:T(8,128)}) %all-gather.3.cloned.1.call-update) | async-done | bytes 1048592 | tf_op jit(solution)/shard_map/all_gather | solution.py:176
  51.3 1.4 %fusion.1 = (f32[16,2048]{1,0:T(8,128)S(1)}, f32[16,2048]{1,0:T(8,128)S(1)}, f32[16,2048]{1,0:T(8,128)S(1)}, f32[16,2048]{1,0:T(8,128)S(1)}, f32[16,2048]{1,0:T(...) fusion(f32[128,2048]{1,0:T(8,128)} %all-gather.3.cloned.1.call-done), kind=kLoop, calls=%fused_computation.9 | loop fusion | bytes 2097152 | tf_op jit(solution)/shard_map/slice | solution.py:183
  52.7 0.0 copy-done.1
  52.7 0.8 %maximum_add_fusion.3 = f32[16,4096]{1,0:T(8,128)} fusion(f32[16,2048]{1,0:T(8,128)S(1)} %get-tuple-element.9, f32[16,2048]{1,0:T(8,128)S(1)} %get-tuple-element.2, f32[16,2048]{1,0:T(8,128)S(1)} %get-tuple-element.3, f32[16,2048]{1,0:T(8,128)S(1)} %get-tuple-element.4, f32[16,2048]{1,0:T(8,128)S(1)} %get-tuple-element.5, ...), kind=kLoop, calls=%fused_computation.3 | loop fusion | flops 983040 | bytes 1572864 | tf_op jit(solution)/shard_map/add | solution.py:185
  53.5 0.8 %add_select_fusion.init_ref = f32[16,4096]{1,0:T(8,128)} fusion(f32[16,4096]{1,0:T(8,128)S(1)} %broadcast_select_fusion, f32[16,2048]{1,0:T(8,128)S(1)} %get-tuple-element.3, f32[16,2048]{1,0:T(8,128)S(1)} %get-tuple-element.4, f32[16,2048]{1,0:T(8,128)S(1)} %get-tuple-element.5, f32[16,2048]{1,0:T(8,128)S(1)} %get-tuple-element.6, ...), kind=kLoop, calls=%fused_computation.4 | loop fusion | flops 1179648 | bytes 1572868 | tf_op jit(solution)/shard_map/jit(_where)/select_n | solution.py:186
  54.4 12.4 %shard_map.70 = bf16[128,4096]{1,0:T(8,128)(2,1)} custom-call(bf16[3,128,4096]{2,1,0:T(8,128)(2,1)} %x_ref.5, bf16[3,2,4096]{2,1,0:T(2,128)(2,1)} %copy-done.2, f32[3,3,4096]{2,1,0:T(4,128)} %filt_ref.5, f32[16,4096]{1,0:T(8,128)} %rate_ref.5, f32[16,4096]{1,0:T(8,128)} %res_ref.3, f32[16,4096]{1,0:T(8,128)} %add_select_fusion.init_ref, ...), custom_call_target="tpu_custom_call" | custom-call | tf_op jit(solution)/shard_map/pallas_call | solution.py:146
  (1 shorter events, 0.0 us)
Async XLA Ops:
  7.2 15.6 %copy-start = (f32[16,4096]{1,0:T(8,128)S(1)}, f32[16,4096]{1,0:T(8,128)}, u32[]{:S(2)}) copy-start(f32[16,4096]{1,0:T(8,128)} %rate_ref.5) | copy-start | bytes 786436
  7.2 44.1 %all-gather.3.cloned.1.call-start = ((), (), s32[]{:S(2)}) async-start(), calls=%async_computation | async-start | bytes 1179648 | tf_op jit(solution)/shard_map/all_gather | solution.py:176
  8.2 3.2 %collective-permute-start = (bf16[3,2,4096]{2,1,0:T(2,128)(2,1)S(1)}, bf16[3,2,4096]{2,1,0:T(2,128)(2,1)S(1)}, u32[]{:S(2)}, u32[]{:S(2)}) collective-permute-start(bf16[3,2,4096]{2,1,0:T(2,128)(2,1)S(1)} %slice.27), channel_id=1, source_target_pairs={{0,1},{1,4},{4,5},{5,8},{8,9},{9,12},{12,13},{2,3},{3,6},{6,7},{7,... | collective-permute-start | bytes 147464 | tf_op jit(solution)/shard_map/ppermute | solution.py:17
  11.5 0.6 copy-start.2
  19.7 4.4 %collective-permute-start.1 = (f32[16,4096]{1,0:T(8,128)}, f32[16,4096]{1,0:T(8,128)S(1)}, u32[]{:S(2)}, u32[]{:S(2)}) collective-permute-start(f32[16,4096]{1,0:T(8,128)} %shard_map.68), channel_id=1, source_target_pairs={{0,1},{1,0},{2,3},{3,2},{4,5},{5,4},{6,7},{7,6},{8,9},{9,8},{10,11... | collective-permute-start | bytes 786440 | tf_op jit(solution)/shard_map/ppermute | solution.py:157
  26.7 26.0 %copy-start.1 = (f32[16,4096]{1,0:T(8,128)S(1)}, f32[16,4096]{1,0:T(8,128)}, u32[]{:S(2)}) copy-start(f32[16,4096]{1,0:T(8,128)} %rate_ref.5) | copy-start | bytes 786436
Sparse Core Ops, SparseCore 0:
  26.8 24.4 all-gather.2

commit v5 on v1

--- a/solution.py
+++ b/solution.py
@@ -112,22 +112,36 @@
     )(projected, halo, short_filters, decay_rate, residue, skip[None, :], prefix)
 
 
+def swap_cores(value):
+    return lax.ppermute(value, "dec", [(0, 1), (1, 0)])
+
+
 def local(projected, short_filters, decay_rate, residue, skip):
     tap_count = short_filters.shape[1]
     row_count = projected.shape[1]
+    modes = decay_rate.shape[0]
     edge_rows = projected[:, row_count - (tap_count - 1) :, :]
     halo = from_behind(edge_rows, ("ctx", "dec"), 1)
     contribution = contributions(projected, halo, short_filters, decay_rate)
-    received = lax.all_gather(contribution, ("ctx", "dec"), axis=0, tiled=False)
-    rank_here = lax.axis_index(("ctx", "dec"))
+    received = lax.all_gather(contribution, "ctx", axis=0, tiled=False)
     shard_decay = jnp.exp(-decay_rate * row_count)
+    chip_decay = shard_decay * shard_decay
+    chip_here = lax.axis_index("ctx")
     running = jnp.zeros_like(contribution)
-    prefix = jnp.zeros_like(contribution)
-    for shard in range(received.shape[0]):
-        prefix = jnp.where(rank_here == shard, running, prefix)
-        running = shard_decay * running + received[shard]
+    entering = jnp.zeros_like(contribution)
+    for chip in range(received.shape[0]):
+        entering = jnp.where(chip_here == chip, running, entering)
+        running = chip_decay * running + received[chip]
+    core = lax.axis_index("dec")
+    mine = jnp.concatenate([entering, running, contribution], axis=0)
+    theirs = swap_cores(mine)
+    first = jnp.where(core == 0, mine, theirs)
+    second = jnp.where(core == 0, theirs, mine)
+    chip_entering = shard_decay * first[:modes] + second[:modes]
+    final_state = shard_decay * first[modes : 2 * modes] + second[modes : 2 * modes]
+    prefix = jnp.where(core == 0, chip_entering, shard_decay * chip_entering + first[2 * modes :])
     mixed = mix(projected, halo, short_filters, decay_rate, residue, skip, prefix)
-    return (mixed, running)
+    return (mixed, final_state)
 
 
 def solution(mesh):

time: 78.3 us -> 79.3 us (1.013)
  waiting for transfers between devices: 35 us -> 36.1 us
    ppermute x0 -> x1, waiting for transfers between devices: none -> 2.27 us  [swap_cores(): return lax.ppermute(value, 'dec', [(0, 1), (1, 0)])]
    add x1, other arithmetic: 2.53 us -> 0.91 us  [local(): final_state = shard_decay * first[modes:2 * modes] + second[modes:2 * modes]]
    all_gather x1, waiting for transfers between devices: 34.1 us -> 33 us  [local(): received = lax.all_gather(contribution, 'ctx', axis=0, tiled=False)]
    concatenate x0 -> x1, other arithmetic: none -> 1 us  [local(): mine = jnp.concatenate([entering, running, contribution], axis=0)]
  transfers between devices with their start and end apart: 2 -> 3, of which waited for: 2 -> 3; matrix products, arithmetic and copies ran while one was open for 0% -> 0% of each run, Pallas kernels for 0% -> 0%
where the time goes in v5:
time: 79.3 us; the launch traced here: 79 us
  waiting for transfers between devices  36.1 us (46%)
  Pallas kernels  21.3 us (27%)
  between operations  14.1 us (18%)
  other arithmetic  3.39 us (4%)
  starting transfers between devices  2.47 us (3%)
  local copies, waits for them, and re-layouts  1.64 us (2%)
    all_gather x1, waiting for transfers between devices, local(): received = lax.all_gather(contribution, 'ctx', axis=0, tiled=False)  33 us
    pallas_call x1, Pallas kernels, mix(): pl.pallas_call(_mix_kernel, grid=(chan_count // CHAN_BLOCK,), in_specs=[x...  13.6 us
    pallas_call x1, Pallas kernels, contributions(): pl.pallas_call(_contrib_kernel, grid=(chan_count // CHAN_BLOCK,), in_spec...  7.66 us
    ppermute x1, starting transfers between devices, from_behind(): lax.ppermute(value, axis, [(source, source + steps) for source in range(i...  2.36 us
    ppermute x1, waiting for transfers between devices, swap_cores(): return lax.ppermute(value, 'dec', [(0, 1), (1, 0)])  2.27 us
  transfers between devices with their start and end apart: 3, of which 3 were waited for; matrix products, arithmetic and copies ran while one was open for 0% of the time, Pallas kernels for 0%

profile of v5, /device:TPU:0, one launch (start us, length us, event | category | flops | bytes accessed | tf_op | source)
XLA Modules:
  0.0 79.0 jit_solution(16202245634551407269)
XLA Ops:
  7.2 0.0 copy-start
  7.2 0.0 all-gather.3.cloned.1.call-start
  7.2 1.0 %slice.30 = bf16[3,2,4096]{2,1,0:T(2,128)(2,1)S(1)} slice(bf16[3,128,4096]{2,1,0:T(8,128)(2,1)} %x_ref.3), slice={[0:3], [126:128], [0:4096]} | slice | bytes 98304 | tf_op jit(solution)/shard_map/slice | solution.py:123
  8.2 2.4 %collective-permute-start = (bf16[3,2,4096]{2,1,0:T(2,128)(2,1)S(1)}, bf16[3,2,4096]{2,1,0:T(2,128)(2,1)S(1)}, u32[]{:S(2)}, u32[]{:S(2)}) collective-permute-start(bf16[3,2,4096]{2,1,0:T(2,128)(2,1)S(1)} %slice.30), channel_id=1, source_target_pairs={{0,1},{1,4},{4,5},{5,8},{8,9},{9,12},{12,13},{2,3},{3,6},{6,7},{7,... | collective-permute-start | bytes 147464 | tf_op jit(solution)/shard_map/ppermute | solution.py:17
  10.6 0.9 %collective-permute-done.halo_ref = bf16[3,2,4096]{2,1,0:T(2,128)(2,1)S(1)} collective-permute-done((bf16[3,2,4096]{2,1,0:T(2,128)(2,1)S(1)}, bf16[3,2,4096]{2,1,0:T(2,128)(2,1)S(1)}, u32[]{:S(2)}, u32[]{:S(2)}) %collective-permute-start) | collective-permute-done | bytes 49184 | tf_op jit(solution)/shard_map/ppermute | solution.py:17
  11.5 0.0 copy-start.2
  11.5 0.6 copy-done.2
  12.1 7.7 %shard_map.68 = f32[16,4096]{1,0:T(8,128)} custom-call(bf16[3,128,4096]{2,1,0:T(8,128)(2,1)} %x_ref.3, bf16[3,2,4096]{2,1,0:T(2,128)(2,1)} %copy-done.2, f32[3,3,4096]{2,1,0:T(4,128)} %filt_ref.3, f32[16,4096]{1,0:T(8,128)} %rate_ref.3), custom_call_target="tpu_custom_call" | custom-call | tf_op jit(solution)/shard_map/pallas_call | solution.py:87
  19.7 0.0 copy-start.1
  19.7 0.0 all-gather.3.cloned.1.call-update
  19.8 33.0 %all-gather.3.cloned.1.call-done = f32[64,4096]{1,0:T(8,128)} async-done(((f32[16,4096]{1,0:T(8,128)}), f32[64,4096]{1,0:T(8,128)}) %all-gather.3.cloned.1.call-update) | async-done | bytes 1048592 | tf_op jit(solution)/shard_map/all_gather | solution.py:126
  52.7 0.0 copy-done
  52.7 1.3 %select_select_fusion = (f32[16,4096]{1,0:T(8,128)S(1)}, f32[16,4096]{1,0:T(8,128)S(1)}) fusion(f32[64,4096]{1,0:T(8,128)} %all-gather.3.cloned.1.call-done, pred[]{:T(512)S(6)} %eq.18, pred[]{:T(512)S(6)} %eq.17, pred[]{:T(512)S(6)} %eq.16, f32[16,4096]{1,0:T(8,128)S(1)} %copy-done), kind=kLoop, calls=%fused_computation.13 | loop fusion | flops 917504 | bytes 1835011 | tf_op jit(solution)/shard_map/jit(_where)/select_n | solution.py:133
  54.1 1.0 %pad_maximum_fusion = f32[48,4096]{1,0:T(8,128)S(1)} fusion(f32[16,4096]{1,0:T(8,128)} %shard_map.68, f32[16,4096]{1,0:T(8,128)S(1)} %get-tuple-element.7, f32[16,4096]{1,0:T(8,128)S(1)} %get-tuple-element.6), kind=kLoop, calls=%fused_computation | loop fusion | flops 393216 | bytes 1572864 | tf_op jit(solution)/shard_map/concatenate | solution.py:136
  55.1 0.1 collective-permute-start.1
  55.2 2.3 %collective-permute-done.1 = f32[48,4096]{1,0:T(8,128)S(1)} collective-permute-done((f32[48,4096]{1,0:T(8,128)S(1)}, f32[48,4096]{1,0:T(8,128)S(1)}, u32[]{:S(2)}, u32[]{:S(2)}) %collective-permute-start.1) | collective-permute-done | bytes 786464 | tf_op jit(solution)/shard_map/ppermute | solution.py:116
  57.4 0.0 copy-done.1
  57.4 0.2 broadcast_select_fusion
  57.6 0.9 %slice_add_fusion = (f32[16,4096]{1,0:T(8,128)}, f32[16,4096]{1,0:T(8,128)}) fusion(f32[48,4096]{1,0:T(8,128)S(1)} %get-tuple-element.4, f32[48,4096]{1,0:T(8,128)S(1)} %get-tuple-element.5, f32[16,4096]{1,0:T(8,128)S(1)} %copy-done, pred[]{:T(512)S(6)} %eq.15), kind=kLoop, calls=%fused_computation.3 | loop fusion | flops 589824 | bytes 2097153 | tf_op jit(solution)/shard_map/add | solution.py:141
  58.5 13.6 %shard_map.69 = bf16[128,4096]{1,0:T(8,128)(2,1)} custom-call(bf16[3,128,4096]{2,1,0:T(8,128)(2,1)} %x_ref.3, bf16[3,2,4096]{2,1,0:T(2,128)(2,1)} %copy-done.2, f32[3,3,4096]{2,1,0:T(4,128)} %filt_ref.3, f32[16,4096]{1,0:T(8,128)} %rate_ref.3, f32[16,4096]{1,0:T(8,128)} %res_ref.1, f32[1,4096]{1,0:T(1,128)} %bitcast.1, f32[16,4096]{1,0:T(8,128)} %get-tuple-element.3.init_ref), custom_call_target="tpu_custom_call" | custom-call | tf_op jit(solution)/shard_map/pallas_call | solution.py:102
Async XLA Ops:
  7.2 45.6 %copy-start = (f32[16,4096]{1,0:T(8,128)S(1)}, f32[16,4096]{1,0:T(8,128)}, u32[]{:S(2)}) copy-start(f32[16,4096]{1,0:T(8,128)} %rate_ref.3) | copy-start | bytes 786436
  7.2 45.6 %all-gather.3.cloned.1.call-start = ((), (), s32[]{:S(2)}) async-start(), calls=%async_computation | async-start | bytes 1310720 | tf_op jit(solution)/shard_map/all_gather | solution.py:126
  8.2 3.2 %collective-permute-start = (bf16[3,2,4096]{2,1,0:T(2,128)(2,1)S(1)}, bf16[3,2,4096]{2,1,0:T(2,128)(2,1)S(1)}, u32[]{:S(2)}, u32[]{:S(2)}) collective-permute-start(bf16[3,2,4096]{2,1,0:T(2,128)(2,1)S(1)} %slice.30), channel_id=1, source_target_pairs={{0,1},{1,4},{4,5},{5,8},{8,9},{9,12},{12,13},{2,3},{3,6},{6,7},{7,... | collective-permute-start | bytes 147464 | tf_op jit(solution)/shard_map/ppermute | solution.py:17
  11.5 0.6 copy-start.2
  19.7 37.7 %copy-start.1 = (f32[16,4096]{1,0:T(8,128)S(1)}, f32[16,4096]{1,0:T(8,128)}, u32[]{:S(2)}) copy-start(f32[16,4096]{1,0:T(8,128)} %shard_map.68) | copy-start | bytes 786436
  55.1 2.4 %collective-permute-start.1 = (f32[48,4096]{1,0:T(8,128)S(1)}, f32[48,4096]{1,0:T(8,128)S(1)}, u32[]{:S(2)}, u32[]{:S(2)}) collective-permute-start(f32[48,4096]{1,0:T(8,128)S(1)} %pad_maximum_fusion), channel_id=1, source_target_pairs={{0,1},{1,0},{2,3},{3,2},{4,5},{5,4},{6,7},{7,6},{8,9},{9,8},{10,11... | collective-permute-start | bytes 2359304 | tf_op jit(solution)/shard_map/ppermute | solution.py:116
Sparse Core Ops, SparseCore 0:
  19.9 32.8 all-gather.2

commit v6 on v2

v6 whole, which is shorter than its diff:
```python
import functools

import jax
import jax.numpy as jnp
from jax import lax
from jax.experimental import pallas as pl
from jax.experimental.pallas import tpu as pltpu
from jax.sharding import PartitionSpec as P

CHAN_BLOCK = 512
ROW_GROUP = 8


def from_behind(value, axis, steps):
    count = lax.axis_size(axis)
    initial, last = (max(0, -steps), min(count, count - steps))
    return lax.ppermute(value, axis, [(source, source + steps) for source in range(initial, last)])


def _featurize_one(x_ref, halo_ref, filt_ref, index):
    x = x_ref[index].astype(jnp.float32)
    halo = halo_ref[index].astype(jnp.float32)
    taps = filt_ref[index]
    last = halo[halo.shape[0] - 1 : halo.shape[0]]
    second = halo[halo.shape[0] - 2 : halo.shape[0] - 1]
    body = taps[0:1] * x + taps[1:2] * pltpu.roll(x, 1, 0) + taps[2:3] * pltpu.roll(x, 2, 0)
    head_x = x[:ROW_GROUP]
    rows = lax.broadcasted_iota(jnp.int32, head_x.shape, 0)
    back1 = jnp.where(rows == 0, last, pltpu.roll(head_x, 1, 0))
    back2 = jnp.where(rows == 0, second, jnp.where(rows == 1, last, pltpu.roll(head_x, 2, 0)))
    head = taps[0:1] * head_x + taps[1:2] * back1 + taps[2:3] * back2
    return jnp.concatenate([head, body[ROW_GROUP:]], axis=0)


def _reduce_rows(ys):
    sub = lax.broadcasted_iota(jnp.int32, ys[0].shape, 0)
    low4 = sub < 4
    a = [jnp.where(low4, ys[i], ys[i + 4]) + pltpu.roll(jnp.where(low4, ys[i + 4], ys[i]), 4, 0) for i in range(4)]
    m2 = jnp.bitwise_and(sub, 3) < 2
    b = [jnp.where(m2, a[i] + pltpu.roll(a[i], 6, 0), a[i + 2] + pltpu.roll(a[i + 2], 2, 0)) for i in range(2)]
    m1 = jnp.bitwise_and(sub, 1) == 0
    return jnp.where(m1, b[0] + pltpu.roll(b[0], 7, 0), b[1] + pltpu.roll(b[1], 1, 0))


def _scan_rows(drive_ref, decay, residue, state, conv_ref):
    row_count = drive_ref.shape[0]
    low = slice(0, ROW_GROUP)
    high = slice(ROW_GROUP, 2 * ROW_GROUP)

    def body(group, state):
        start = pl.multiple_of(group * ROW_GROUP, ROW_GROUP)
        ys = []
        block = drive_ref[pl.ds(start, ROW_GROUP), :]
        for i in range(ROW_GROUP):
            drive_row = jnp.broadcast_to(block[i : i + 1], state.shape)
            state = decay * state + drive_row
            if conv_ref is not None:
                ys.append(residue[low] * state[low] + residue[high] * state[high])
        if conv_ref is not None:
            conv_ref[pl.ds(start, ROW_GROUP), :] = _reduce_rows(ys)
        return state

    return lax.fori_loop(0, row_count // ROW_GROUP, body, state)


def _contrib_kernel(x_ref, halo_ref, filt_ref, rate_ref, out_ref, drive_ref):
    k = _featurize_one(x_ref, halo_ref, filt_ref, 1)
    v = _featurize_one(x_ref, halo_ref, filt_ref, 2)
    drive_ref[...] = k * v
    decay = jnp.exp(-rate_ref[...])
    state = jnp.zeros(out_ref.shape, jnp.float32)
    out_ref[...] = _scan_rows(drive_ref, decay, None, state, None)


def _mix_kernel(x_ref, halo_ref, filt_ref, rate_ref, res_ref, skip_ref, init_ref, drive_ref, out_ref,
                conv_scr):
    decay = jnp.exp(-rate_ref[...])
    _scan_rows(drive_ref, decay, res_ref[...], init_ref[...], conv_scr)
    q = _featurize_one(x_ref, halo_ref, filt_ref, 0)
    out_ref[...] = (q * (conv_scr[...] + skip_ref[...] * drive_ref[...])).astype(out_ref.dtype)


def _specs(row_count, modes, taps, features=3):
    x_spec = pl.BlockSpec((features, row_count, CHAN_BLOCK), lambda j: (0, 0, j))
    halo_spec = pl.BlockSpec((features, taps - 1, CHAN_BLOCK), lambda j: (0, 0, j))
    filt_spec = pl.BlockSpec((features, taps, CHAN_BLOCK), lambda j: (0, 0, j))
    mode_spec = pl.BlockSpec((modes, CHAN_BLOCK), lambda j: (0, j))
    row_spec = pl.BlockSpec((1, CHAN_BLOCK), lambda j: (0, j))
    return x_spec, halo_spec, filt_spec, mode_spec, row_spec


def contributions(projected, halo, short_filters, decay_rate):
    _, row_count, chan_count = projected.shape
    modes = decay_rate.shape[0]
    taps = short_filters.shape[1]
    x_spec, halo_spec, filt_spec, mode_spec, _ = _specs(row_count, modes, taps)
    return pl.pallas_call(
        _contrib_kernel,
        grid=(chan_count // CHAN_BLOCK,),
        in_specs=[x_spec, halo_spec, filt_spec, mode_spec],
        out_specs=[mode_spec, pl.BlockSpec((row_count, CHAN_BLOCK), lambda j: (0, j))],
        out_shape=[
            jax.ShapeDtypeStruct((modes, chan_count), jnp.float32),
            jax.ShapeDtypeStruct((row_count, chan_count), jnp.float32),
        ],
    )(projected, halo, short_filters, decay_rate)


def mix(projected, halo, short_filters, decay_rate, residue, skip, prefix, drive):
    _, row_count, chan_count = projected.shape
    modes = decay_rate.shape[0]
    taps = short_filters.shape[1]
    x_spec, halo_spec, filt_spec, mode_spec, row_spec = _specs(row_count, modes, taps, 1)
    tile_spec = pl.BlockSpec((row_count, CHAN_BLOCK), lambda j: (0, j))
    return pl.pallas_call(
        _mix_kernel,
        grid=(chan_count // CHAN_BLOCK,),
        in_specs=[x_spec, halo_spec, filt_spec, mode_spec, mode_spec, row_spec, mode_spec, tile_spec],
        out_specs=tile_spec,
        out_shape=jax.ShapeDtypeStruct((row_count, chan_count), jnp.bfloat16),
        scratch_shapes=[pltpu.VMEM((row_count, CHAN_BLOCK), jnp.float32)],
    )(projected, halo, short_filters, decay_rate, residue, skip[None, :], prefix, drive)


def swap_cores(value):
    return lax.ppermute(value, "dec", [(0, 1), (1, 0)])


def local(projected, short_filters, decay_rate, residue, skip):
    tap_count = short_filters.shape[1]
    row_count = projected.shape[1]
    chan_count = projected.shape[2]
    edge_rows = projected[:, row_count - (tap_count - 1) :, :]
    halo = from_behind(edge_rows, ("ctx", "dec"), 1)
    contribution, drive = contributions(projected, halo, short_filters, decay_rate)
    core = lax.axis_index("dec")
    other = swap_cores(contribution)
    first_core = jnp.where(core == 0, contribution, other)
    second_core = jnp.where(core == 0, other, contribution)
    shard_decay = jnp.exp(-decay_rate * row_count)
    half = chan_count // 2
    start = core * half
    mine = lambda x: lax.dynamic_slice_in_dim(x, start, half, 1)
    chip_decay = mine(shard_decay) * mine(shard_decay)
    chip_part = mine(shard_decay) * mine(first_core) + mine(second_core)
    received = lax.all_gather(chip_part, "ctx", axis=0, tiled=False)
    chip_here = lax.axis_index("ctx")
    running = jnp.zeros_like(chip_part)
    entering = jnp.zeros_like(chip_part)
    for chip in range(received.shape[0]):
        entering = jnp.where(chip_here == chip, running, entering)
        running = chip_decay * running + received[chip]
    both = jnp.concatenate([entering, running], axis=0)
    other_both = swap_cores(both)
    low = jnp.where(core == 0, both, other_both)
    high = jnp.where(core == 0, other_both, both)
    whole = jnp.concatenate([low, high], axis=1)
    modes = decay_rate.shape[0]
    chip_entering = whole[:modes]
    final_state = whole[modes:]
    prefix = jnp.where(core == 0, chip_entering, shard_decay * chip_entering + first_core)
    mixed = mix(projected, halo, short_filters, decay_rate, residue, skip, prefix, drive)
    return (mixed, final_state)


def solution(mesh):
    placed = (
        P(None, ("grp", "ctx", "dec"), "chan"),
        P(None, None, "chan"),
        P(None, "chan"),
        P(None, "chan"),
        P("chan"),
    )
    return jax.shard_map(
        local,
        mesh=mesh,
        in_specs=placed,
        out_specs=(P(("grp", "ctx", "dec"), "chan"), P("grp", "chan")),
        check_vma=False,
    )
```

time: 52.4 us -> 49.9 us (0.952)
  Pallas kernels: 21.3 us -> 18.6 us
    pallas_call x1, Pallas kernels: 13.6 us -> 10.5 us  [mix(): pl.pallas_call(_mix_kernel, grid=(chan_count // CHAN_BLOCK,), in_specs=[x...]
where the time goes in v6:
time: 49.9 us; the launch traced here: 49.4 us
  Pallas kernels  18.6 us (37%)
  blocking collectives  16.4 us (33%)
  starting transfers between devices  5.41 us (11%)
  waiting for transfers between devices  3.69 us (7%)
  other arithmetic  2.93 us (6%)
  local copies, waits for them, and re-layouts  1.64 us (3%)
  between operations  0.7 us (1%)
    all_gather x1, blocking collectives, local(): received = lax.all_gather(chip_part, 'ctx', axis=0, tiled=False)  16.4 us
    pallas_call x1, Pallas kernels, mix(): pl.pallas_call(_mix_kernel, grid=(chan_count // CHAN_BLOCK,), in_specs=[x...  10.5 us
    pallas_call x1, Pallas kernels, contributions(): pl.pallas_call(_contrib_kernel, grid=(chan_count // CHAN_BLOCK,), in_spec...  8.08 us
    ppermute x2, starting transfers between devices, swap_cores(): return lax.ppermute(value, 'dec', [(0, 1), (1, 0)])  3.05 us
    ppermute x2, waiting for transfers between devices, swap_cores(): return lax.ppermute(value, 'dec', [(0, 1), (1, 0)])  2.83 us
    ppermute x1, starting transfers between devices, from_behind(): lax.ppermute(value, axis, [(source, source + steps) for source in range(i...  2.36 us
    slice x1, local copies, waits for them, and re-layouts, local(): edge_rows = projected[:, row_count - (tap_count - 1):, :]  1.02 us
  transfers between devices with their start and end apart: 3, of which 3 were waited for; matrix products, arithmetic and copies ran while one was open for 0% of the time, Pallas kernels for 0%

profile of v6, /device:TPU:0, one launch (start us, length us, event | category | flops | bytes accessed | tf_op | source)
XLA Modules:
  0.0 49.4 jit_solution(4218865060390955189)
XLA Ops:
  0.6 0.0 copy-start
  0.6 1.0 %slice.21 = bf16[3,2,4096]{2,1,0:T(2,128)(2,1)S(1)} slice(bf16[3,128,4096]{2,1,0:T(8,128)(2,1)} %x_ref.3), slice={[0:3], [126:128], [0:4096]} | slice | bytes 98304 | tf_op jit(solution)/shard_map/slice | solution.py:133
  1.7 2.4 %collective-permute-start = (bf16[3,2,4096]{2,1,0:T(2,128)(2,1)S(1)}, bf16[3,2,4096]{2,1,0:T(2,128)(2,1)S(1)}, u32[]{:S(2)}, u32[]{:S(2)}) collective-permute-start(bf16[3,2,4096]{2,1,0:T(2,128)(2,1)S(1)} %slice.21), channel_id=1, source_target_pairs={{0,1},{1,4},{4,5},{5,8},{8,9},{9,12},{12,13},{2,3},{3,6},{6,7},{7,... | collective-permute-start | bytes 147464 | tf_op jit(solution)/shard_map/ppermute | solution.py:17
  4.0 0.9 %collective-permute-done.halo_ref = bf16[3,2,4096]{2,1,0:T(2,128)(2,1)S(1)} collective-permute-done((bf16[3,2,4096]{2,1,0:T(2,128)(2,1)S(1)}, bf16[3,2,4096]{2,1,0:T(2,128)(2,1)S(1)}, u32[]{:S(2)}, u32[]{:S(2)}) %collective-permute-start) | collective-permute-done | bytes 49184 | tf_op jit(solution)/shard_map/ppermute | solution.py:17
  4.9 0.0 copy-start.1
  4.9 0.6 %copy-done.1 = bf16[3,2,4096]{2,1,0:T(2,128)(2,1)} copy-done((bf16[3,2,4096]{2,1,0:T(2,128)(2,1)}, bf16[3,2,4096]{2,1,0:T(2,128)(2,1)S(1)}, u32[]{:S(2)}) %copy-start.1) | copy-done | bytes 49176
  5.5 8.1 %shard_map.68 = (f32[16,4096]{1,0:T(8,128)}, f32[128,4096]{1,0:T(8,128)}) custom-call(bf16[3,128,4096]{2,1,0:T(8,128)(2,1)} %x_ref.3, bf16[3,2,4096]{2,1,0:T(2,128)(2,1)} %copy-done.1, f32[3,3,4096]{2,1,0:T(4,128)} %filt_ref.3, f32[16,4096]{1,0:T(8,128)} %rate_ref.3), custom_call_target="tpu_custom_call" | custom-call | tf_op jit(solution)/shard_map/pallas_call | solution.py:97
  13.6 3.0 %collective-permute-start.1 = (f32[16,4096]{1,0:T(8,128)}, f32[16,4096]{1,0:T(8,128)S(1)}, u32[]{:S(2)}, u32[]{:S(2)}) collective-permute-start(f32[16,4096]{1,0:T(8,128)} %get-tuple-element.4), channel_id=1, source_target_pairs={{0,1},{1,0},{2,3},{3,2},{4,5},{5,4},{6,7},{7,6},{8,9},{9,8},{10,11... | collective-permute-start | bytes 786440 | tf_op jit(solution)/shard_map/ppermute | solution.py:126
  16.6 0.0 copy-done
  16.6 1.3 %collective-permute-done.1 = f32[16,4096]{1,0:T(8,128)S(1)} collective-permute-done((f32[16,4096]{1,0:T(8,128)}, f32[16,4096]{1,0:T(8,128)S(1)}, u32[]{:S(2)}, u32[]{:S(2)}) %collective-permute-start.1) | collective-permute-done | bytes 262176 | tf_op jit(solution)/shard_map/ppermute | solution.py:126
  17.9 1.0 %broadcast_select_fusion.2 = f32[16,4096]{1,0:T(8,128)S(1)} fusion(f32[16,4096]{1,0:T(8,128)} %get-tuple-element.4, f32[16,4096]{1,0:T(8,128)S(1)} %collective-permute-done.1, pred[]{:T(512)S(6)} %eq.8), kind=kLoop, calls=%fused_computation.16 | loop fusion | flops 65536 | bytes 786433 | tf_op jit(solution)/shard_map/jit(_where)/select_n | solution.py:138
  18.9 0.9 %fusion.1 = f32[16,2048]{1,0:T(8,128)S(1)} fusion(f32[16,4096]{1,0:T(8,128)} %get-tuple-element.4, s32[]{:T(128)S(6)} %select_n.61, f32[16,4096]{1,0:T(8,128)S(1)} %collective-permute-done.1, f32[16,4096]{1,0:T(8,128)S(1)} %broadcast_select_fusion.2, f32[16,4096]{1,0:T(8,128)S(1)} %multiply_exponential_fusion, pred[]{:T(512)S(6)} %eq.8), kind=kLoop, calls=%fused_computation.12 | loop fusion | flops 98304 | bytes 655365 | tf_op jit(solution)/shard_map/add | solution.py:145
  19.9 16.4 %all-gather = f32[64,2048]{1,0:T(8,128)S(1)} all-gather(f32[16,2048]{1,0:T(8,128)S(1)} %fusion.1), channel_id=2, replica_groups=mesh['grp'=2,'ctx'=4,'chan'=2,'dec'=2] {'ctx'}, dimensions={0}, use_global_device_ids=true | all-gather | bytes 655360 | tf_op jit(solution)/shard_map/all_gather | solution.py:146
  36.3 0.1 select_select_fusion
  36.4 0.1 collective-permute-start.2
  36.4 1.5 %collective-permute-done.2 = f32[32,2048]{1,0:T(8,128)S(1)} collective-permute-done((f32[32,2048]{1,0:T(8,128)S(1)}, f32[32,2048]{1,0:T(8,128)S(1)}, u32[]{:S(2)}, u32[]{:S(2)}) %collective-permute-start.2) | collective-permute-done | bytes 262176 | tf_op jit(solution)/shard_map/ppermute | solution.py:126
  38.0 0.8 %pad_maximum_fusion = (f32[16,4096]{1,0:T(8,128)}, f32[16,4096]{1,0:T(8,128)}) fusion(f32[32,2048]{1,0:T(8,128)S(1)} %get-tuple-element.11, f32[32,2048]{1,0:T(8,128)S(1)} %get-tuple-element.10, f32[16,4096]{1,0:T(8,128)S(1)} %broadcast_select_fusion.2, f32[16,4096]{1,0:T(8,128)S(1)} %copy-done, pred[]{:T(512)S(6)} %eq.8), kind=kLoop, calls=%fused_computation.3 | loop fusion | flops 458752 | bytes 1572865 | tf_op jit(solution)/shard_map/concatenate | solution.py:157
  38.9 10.5 %shard_map.69 = bf16[128,4096]{1,0:T(8,128)(2,1)} custom-call(bf16[3,128,4096]{2,1,0:T(8,128)(2,1)} %x_ref.3, bf16[3,2,4096]{2,1,0:T(2,128)(2,1)} %copy-done.1, f32[3,3,4096]{2,1,0:T(4,128)} %filt_ref.3, f32[16,4096]{1,0:T(8,128)} %rate_ref.3, f32[16,4096]{1,0:T(8,128)} %res_ref.1, f32[1,4096]{1,0:T(1,128)} %bitcast.1, ...), custom_call_target="tpu_custom_call" | custom-call | tf_op jit(solution)/shard_map/pallas_call | solution.py:115
  (3 shorter events, 0.1 us)
Async XLA Ops:
  0.6 15.9 %copy-start = (f32[16,4096]{1,0:T(8,128)S(1)}, f32[16,4096]{1,0:T(8,128)}, u32[]{:S(2)}) copy-start(f32[16,4096]{1,0:T(8,128)} %rate_ref.3) | copy-start | bytes 786436
  1.7 3.2 %collective-permute-start = (bf16[3,2,4096]{2,1,0:T(2,128)(2,1)S(1)}, bf16[3,2,4096]{2,1,0:T(2,128)(2,1)S(1)}, u32[]{:S(2)}, u32[]{:S(2)}) collective-permute-start(bf16[3,2,4096]{2,1,0:T(2,128)(2,1)S(1)} %slice.21), channel_id=1, source_target_pairs={{0,1},{1,4},{4,5},{5,8},{8,9},{9,12},{12,13},{2,3},{3,6},{6,7},{7,... | collective-permute-start | bytes 147464 | tf_op jit(solution)/shard_map/ppermute | solution.py:17
  4.9 0.6 %copy-start.1 = (bf16[3,2,4096]{2,1,0:T(2,128)(2,1)}, bf16[3,2,4096]{2,1,0:T(2,128)(2,1)S(1)}, u32[]{:S(2)}) copy-start(bf16[3,2,4096]{2,1,0:T(2,128)(2,1)S(1)} %collective-permute-done.halo_ref) | copy-start | bytes 147460
  13.6 4.4 %collective-permute-start.1 = (f32[16,4096]{1,0:T(8,128)}, f32[16,4096]{1,0:T(8,128)S(1)}, u32[]{:S(2)}, u32[]{:S(2)}) collective-permute-start(f32[16,4096]{1,0:T(8,128)} %get-tuple-element.4), channel_id=1, source_target_pairs={{0,1},{1,0},{2,3},{3,2},{4,5},{5,4},{6,7},{7,6},{8,9},{9,8},{10,11... | collective-permute-start | bytes 786440 | tf_op jit(solution)/shard_map/ppermute | solution.py:126
  36.4 1.6 %collective-permute-start.2 = (f32[32,2048]{1,0:T(8,128)S(1)}, f32[32,2048]{1,0:T(8,128)S(1)}, u32[]{:S(2)}, u32[]{:S(2)}) collective-permute-start(f32[32,2048]{1,0:T(8,128)S(1)} %pad_maximum_fusion.1), channel_id=1, source_target_pairs={{0,1},{1,0},{2,3},{3,2},{4,5},{5,4},{6,7},{7,6},{8,9},{9,8},{10,11... | collective-permute-start | bytes 786440 | tf_op jit(solution)/shard_map/ppermute | solution.py:126

commit v7 on v6

--- a/solution.py
+++ b/solution.py
@@ -72,10 +72,13 @@
     out_ref[...] = _scan_rows(drive_ref, decay, None, state, None)
 
 
-def _mix_kernel(x_ref, halo_ref, filt_ref, rate_ref, res_ref, skip_ref, init_ref, drive_ref, out_ref,
-                conv_scr):
+def _mix_kernel(x_ref, halo_ref, filt_ref, rate_ref, res_ref, skip_ref, init_lo_ref, init_hi_ref,
+                fin_lo_ref, fin_hi_ref, drive_ref, out_ref, fin_ref, conv_scr):
+    in_low = pl.program_id(0) < pl.num_programs(0) // 2
+    init = jnp.where(in_low, init_lo_ref[...], init_hi_ref[...])
+    fin_ref[...] = jnp.where(in_low, fin_lo_ref[...], fin_hi_ref[...])
     decay = jnp.exp(-rate_ref[...])
-    _scan_rows(drive_ref, decay, res_ref[...], init_ref[...], conv_scr)
+    _scan_rows(drive_ref, decay, res_ref[...], init, conv_scr)
     q = _featurize_one(x_ref, halo_ref, filt_ref, 0)
     out_ref[...] = (q * (conv_scr[...] + skip_ref[...] * drive_ref[...])).astype(out_ref.dtype)
 
@@ -106,20 +109,28 @@
     )(projected, halo, short_filters, decay_rate)
 
 
-def mix(projected, halo, short_filters, decay_rate, residue, skip, prefix, drive):
+def mix(projected, halo, short_filters, decay_rate, residue, skip, prefix_halves, final_halves, drive):
     _, row_count, chan_count = projected.shape
     modes = decay_rate.shape[0]
     taps = short_filters.shape[1]
     x_spec, halo_spec, filt_spec, mode_spec, row_spec = _specs(row_count, modes, taps, 1)
     tile_spec = pl.BlockSpec((row_count, CHAN_BLOCK), lambda j: (0, j))
+    per_half = chan_count // 2 // CHAN_BLOCK
+    low_spec = pl.BlockSpec((modes, CHAN_BLOCK), lambda j: (0, jnp.minimum(j, per_half - 1)))
+    high_spec = pl.BlockSpec((modes, CHAN_BLOCK), lambda j: (0, jnp.maximum(j - per_half, 0)))
     return pl.pallas_call(
         _mix_kernel,
         grid=(chan_count // CHAN_BLOCK,),
-        in_specs=[x_spec, halo_spec, filt_spec, mode_spec, mode_spec, row_spec, mode_spec, tile_spec],
-        out_specs=tile_spec,
-        out_shape=jax.ShapeDtypeStruct((row_count, chan_count), jnp.bfloat16),
+        in_specs=[x_spec, halo_spec, filt_spec, mode_spec, mode_spec, row_spec,
+                  low_spec, high_spec, low_spec, high_spec, tile_spec],
+        out_specs=[tile_spec, mode_spec],
+        out_shape=[
+            jax.ShapeDtypeStruct((row_count, chan_count), jnp.bfloat16),
+            jax.ShapeDtypeStruct((modes, chan_count), jnp.float32),
+        ],
         scratch_shapes=[pltpu.VMEM((row_count, CHAN_BLOCK), jnp.float32)],
-    )(projected, halo, short_filters, decay_rate, residue, skip[None, :], prefix, drive)
+    )(projected, halo, short_filters, decay_rate, residue, skip[None, :], *prefix_halves,
+      *final_halves, drive)
 
 
 def swap_cores(value):
@@ -130,36 +141,41 @@
     tap_count = short_filters.shape[1]
     row_count = projected.shape[1]
     chan_count = projected.shape[2]
+    modes = decay_rate.shape[0]
     edge_rows = projected[:, row_count - (tap_count - 1) :, :]
     halo = from_behind(edge_rows, ("ctx", "dec"), 1)
     contribution, drive = contributions(projected, halo, short_filters, decay_rate)
     core = lax.axis_index("dec")
-    other = swap_cores(contribution)
-    first_core = jnp.where(core == 0, contribution, other)
-    second_core = jnp.where(core == 0, other, contribution)
-    shard_decay = jnp.exp(-decay_rate * row_count)
+    first = core == 0
     half = chan_count // 2
-    start = core * half
-    mine = lambda x: lax.dynamic_slice_in_dim(x, start, half, 1)
-    chip_decay = mine(shard_decay) * mine(shard_decay)
-    chip_part = mine(shard_decay) * mine(first_core) + mine(second_core)
+    pick = lambda x: jnp.where(first, x[:, :half], x[:, half:])
+    other_half = lambda x: jnp.where(first, x[:, half:], x[:, :half])
+    kept = pick(contribution)
+    partner = swap_cores(other_half(contribution))
+    shard_decay = pick(jnp.exp(-decay_rate * row_count))
+    first_core = jnp.where(first, kept, partner)
+    second_core = jnp.where(first, partner, kept)
+    chip_part = shard_decay * first_core + second_core
     received = lax.all_gather(chip_part, "ctx", axis=0, tiled=False)
     chip_here = lax.axis_index("ctx")
+    chip_decay = shard_decay * shard_decay
     running = jnp.zeros_like(chip_part)
     entering = jnp.zeros_like(chip_part)
     for chip in range(received.shape[0]):
         entering = jnp.where(chip_here == chip, running, entering)
         running = chip_decay * running + received[chip]
-    both = jnp.concatenate([entering, running], axis=0)
+    second_entering = shard_decay * entering + first_core
+    both = jnp.concatenate([entering, running, second_entering], axis=0)
     other_both = swap_cores(both)
-    low = jnp.where(core == 0, both, other_both)
-    high = jnp.where(core == 0, other_both, both)
-    whole = jnp.concatenate([low, high], axis=1)
-    modes = decay_rate.shape[0]
-    chip_entering = whole[:modes]
-    final_state = whole[modes:]
-    prefix = jnp.where(core == 0, chip_entering, shard_decay * chip_entering + first_core)
-    mixed = mix(projected, halo, short_filters, decay_rate, residue, skip, prefix, drive)
+    low = jnp.where(first, both, other_both)
+    high = jnp.where(first, other_both, both)
+    prefix_halves = (
+        jnp.where(first, low[:modes], low[2 * modes :]),
+        jnp.where(first, high[:modes], high[2 * modes :]),
+    )
+    final_halves = (low[modes : 2 * modes], high[modes : 2 * modes])
+    mixed, final_state = mix(projected, halo, short_filters, decay_rate, residue, skip,
+                             prefix_halves, final_halves, drive)
     return (mixed, final_state)
 
 

time: 49.9 us -> 51.8 us (1.038)
  other arithmetic: 2.93 us -> 4.01 us
  blocking collectives: 16.4 us -> 17.2 us
    add x1 -> x2, other arithmetic: 0.94 us -> 2.07 us  [the longest x1 1.06 us: local(): second_entering = shard_decay * entering + first_core]
    concatenate x2 -> x1, other arithmetic: 0.86 us -> 0.03 us  [local(): both = jnp.concatenate([entering, running, second_entering], axis=0)]
    slice x0 -> x1, other arithmetic: none -> 0.83 us  [local(): final_halves = (low[modes:2 * modes], high[modes:2 * modes])]
    all_gather x1, blocking collectives: 16.4 us -> 17.2 us  [local(): received = lax.all_gather(chip_part, 'ctx', axis=0, tiled=False)]
    select_n x3 -> x2, other arithmetic: 1.08 us -> 1.05 us  [the longest x1 0.98 us: local(): other_half = lambda x: jnp.where(first, x[:, half:], x[:, :half])]
where the time goes in v7:
time: 51.8 us; the launch traced here: 51.2 us
  Pallas kernels  18.7 us (36%)
  blocking collectives  17.2 us (33%)
  starting transfers between devices  5.48 us (11%)
  other arithmetic  4.01 us (8%)
  waiting for transfers between devices  3.49 us (7%)
  local copies, waits for them, and re-layouts  1.65 us (3%)
  between operations  0.71 us (1%)
    all_gather x1, blocking collectives, local(): received = lax.all_gather(chip_part, 'ctx', axis=0, tiled=False)  17.2 us
    pallas_call x1, Pallas kernels, mix(): pl.pallas_call(_mix_kernel, grid=(chan_count // CHAN_BLOCK,), in_specs=[x...  10.6 us
    pallas_call x1, Pallas kernels, contributions(): pl.pallas_call(_contrib_kernel, grid=(chan_count // CHAN_BLOCK,), in_spec...  8.06 us
    ppermute x2, starting transfers between devices, swap_cores(): return lax.ppermute(value, 'dec', [(0, 1), (1, 0)])  3.12 us
    ppermute x2, waiting for transfers between devices, swap_cores(): return lax.ppermute(value, 'dec', [(0, 1), (1, 0)])  2.64 us
    ppermute x1, starting transfers between devices, from_behind(): lax.ppermute(value, axis, [(source, source + steps) for source in range(i...  2.36 us
    add x1, other arithmetic, local(): second_entering = shard_decay * entering + first_core  1.06 us
  transfers between devices with their start and end apart: 3, of which 3 were waited for; matrix products, arithmetic and copies ran while one was open for 0% of the time, Pallas kernels for 0%

profile of v7, /device:TPU:0, one launch (start us, length us, event | category | flops | bytes accessed | tf_op | source)
XLA Modules:
  0.0 51.2 jit_solution(14753999151763806167)
XLA Ops:
  0.6 0.0 copy-start
  0.6 1.0 %slice.47 = bf16[3,2,4096]{2,1,0:T(2,128)(2,1)S(1)} slice(bf16[3,128,4096]{2,1,0:T(8,128)(2,1)} %x_ref.3), slice={[0:3], [126:128], [0:4096]} | slice | bytes 98304 | tf_op jit(solution)/shard_map/slice | solution.py:145
  1.7 2.4 %collective-permute-start = (bf16[3,2,4096]{2,1,0:T(2,128)(2,1)S(1)}, bf16[3,2,4096]{2,1,0:T(2,128)(2,1)S(1)}, u32[]{:S(2)}, u32[]{:S(2)}) collective-permute-start(bf16[3,2,4096]{2,1,0:T(2,128)(2,1)S(1)} %slice.47), channel_id=1, source_target_pairs={{0,1},{1,4},{4,5},{5,8},{8,9},{9,12},{12,13},{2,3},{3,6},{6,7},{7,... | collective-permute-start | bytes 147464 | tf_op jit(solution)/shard_map/ppermute | solution.py:17
  4.0 0.9 %collective-permute-done.halo_ref = bf16[3,2,4096]{2,1,0:T(2,128)(2,1)S(1)} collective-permute-done((bf16[3,2,4096]{2,1,0:T(2,128)(2,1)S(1)}, bf16[3,2,4096]{2,1,0:T(2,128)(2,1)S(1)}, u32[]{:S(2)}, u32[]{:S(2)}) %collective-permute-start) | collective-permute-done | bytes 49184 | tf_op jit(solution)/shard_map/ppermute | solution.py:17
  4.9 0.0 copy-start.1
  4.9 0.6 %copy-done.1 = bf16[3,2,4096]{2,1,0:T(2,128)(2,1)} copy-done((bf16[3,2,4096]{2,1,0:T(2,128)(2,1)}, bf16[3,2,4096]{2,1,0:T(2,128)(2,1)S(1)}, u32[]{:S(2)}) %copy-start.1) | copy-done | bytes 49176
  5.5 8.1 %shard_map.68 = (f32[16,4096]{1,0:T(8,128)}, f32[128,4096]{1,0:T(8,128)}) custom-call(bf16[3,128,4096]{2,1,0:T(8,128)(2,1)} %x_ref.3, bf16[3,2,4096]{2,1,0:T(2,128)(2,1)} %copy-done.1, f32[3,3,4096]{2,1,0:T(4,128)} %filt_ref.3, f32[16,4096]{1,0:T(8,128)} %rate_ref.3), custom_call_target="tpu_custom_call" | custom-call | tf_op jit(solution)/shard_map/pallas_call | solution.py:100
  13.6 1.0 %slice_select_fusion.3 = f32[16,2048]{1,0:T(8,128)S(1)} fusion(f32[16,4096]{1,0:T(8,128)} %get-tuple-element.4, pred[]{:T(512)S(6)} %eq.13), kind=kLoop, calls=%fused_computation.14 | loop fusion | flops 32768 | bytes 393217 | tf_op jit(solution)/shard_map/jit(_where)/select_n | solution.py:152
  14.6 3.0 %collective-permute-start.1 = (f32[16,2048]{1,0:T(8,128)S(1)}, f32[16,2048]{1,0:T(8,128)S(1)}, u32[]{:S(2)}, u32[]{:S(2)}) collective-permute-start(f32[16,2048]{1,0:T(8,128)S(1)} %slice_select_fusion.3), channel_id=1, source_target_pairs={{0,1},{1,0},{2,3},{3,2},{4,5},{5,4},{6,7},{7,6},{8,9},{9,8},{10,11... | collective-permute-start | bytes 393224 | tf_op jit(solution)/shard_map/ppermute | solution.py:137
  17.6 0.0 copy-done
  17.7 0.9 %collective-permute-done.1 = f32[16,2048]{1,0:T(8,128)S(1)} collective-permute-done((f32[16,2048]{1,0:T(8,128)S(1)}, f32[16,2048]{1,0:T(8,128)S(1)}, u32[]{:S(2)}, u32[]{:S(2)}) %collective-permute-start.1) | collective-permute-done | bytes 131104 | tf_op jit(solution)/shard_map/ppermute | solution.py:137
  18.6 1.0 %select_add_fusion = (f32[16,2048]{1,0:T(8,128)S(1)}, f32[16,2048]{1,0:T(8,128)S(1)}) fusion(f32[16,2048]{1,0:T(8,128)S(1)} %collective-permute-done.1, pred[]{:T(512)S(6)} %eq.13, f32[16,4096]{1,0:T(8,128)} %get-tuple-element.4, f32[16,4096]{1,0:T(8,128)S(1)} %multiply_exponential_fusion), kind=kLoop, calls=%fused_computation.13 | loop fusion | flops 196608 | bytes 917505 | tf_op jit(solution)/shard_map/add | solution.py:158
  19.6 17.2 %all-gather = f32[64,2048]{1,0:T(8,128)S(1)} all-gather(f32[16,2048]{1,0:T(8,128)S(1)} %get-tuple-element.8), channel_id=2, replica_groups=mesh['grp'=2,'ctx'=4,'chan'=2,'dec'=2] {'ctx'}, dimensions={0}, use_global_device_ids=true | all-gather | bytes 655360 | tf_op jit(solution)/shard_map/all_gather | solution.py:159
  36.8 1.1 %multiply_add_fusion = (f32[16,2048]{1,0:T(8,128)S(1)}, f32[16,2048]{1,0:T(8,128)S(1)}, f32[16,2048]{1,0:T(8,128)S(1)}) fusion(f32[16,2048]{1,0:T(8,128)S(1)} %get-tuple-element.9, f32[16,2048]{1,0:T(8,128)S(1)} %collective-permute-done.1, pred[]{:T(512)S(6)} %eq.13, f32[16,4096]{1,0:T(8,128)} %get-tuple-element.4, pred[]{:T(512)S(6)} %eq.16, pred[]{:T(512)S(6)} %eq.15, ...), kind=kLoop, calls=%fused_computation.11 | loop fusion | flops 524288 | bytes 1441796 | tf_op jit(solution)/shard_map/add | solution.py:167
  37.9 0.1 collective-permute-start.2
  38.0 1.7 %collective-permute-done.2 = f32[48,2048]{1,0:T(8,128)S(1)} collective-permute-done((f32[48,2048]{1,0:T(8,128)S(1)}, f32[48,2048]{1,0:T(8,128)S(1)}, u32[]{:S(2)}, u32[]{:S(2)}) %collective-permute-start.2) | collective-permute-done | bytes 393248 | tf_op jit(solution)/shard_map/ppermute | solution.py:137
  39.7 0.1 broadcast_select_fusion
  39.7 0.8 %fusion = (f32[16,2048]{1,0:T(8,128)}, f32[16,2048]{1,0:T(8,128)}, f32[16,2048]{1,0:T(8,128)}, f32[16,2048]{1,0:T(8,128)}) fusion(f32[48,2048]{1,0:T(8,128)S(1)} %get-tuple-element.10, pred[]{:T(512)S(6)} %eq.13, f32[48,2048]{1,0:T(8,128)S(1)} %get-tuple-element.11), kind=kLoop, calls=%fused_computation.17 | loop fusion | flops 65536 | bytes 1310721 | tf_op jit(solution)/shard_map/slice | solution.py:176
  40.6 10.6 %shard_map.69 = (bf16[128,4096]{1,0:T(8,128)(2,1)}, f32[16,4096]{1,0:T(8,128)}) custom-call(bf16[3,128,4096]{2,1,0:T(8,128)(2,1)} %x_ref.3, bf16[3,2,4096]{2,1,0:T(2,128)(2,1)} %copy-done.1, f32[3,3,4096]{2,1,0:T(4,128)} %filt_ref.3, f32[16,4096]{1,0:T(8,128)} %rate_ref.3, f32[16,4096]{1,0:T(8,128)} %res_ref.1, f32[1,4096]{1,0:T(1,128)} %bitcast.1, ...), custom_call_target="tpu_custom_call" | custom-call | tf_op jit(solution)/shard_map/pallas_call | solution.py:121
  (2 shorter events, 0.1 us)
Async XLA Ops:
  0.6 17.0 %copy-start = (f32[16,4096]{1,0:T(8,128)S(1)}, f32[16,4096]{1,0:T(8,128)}, u32[]{:S(2)}) copy-start(f32[16,4096]{1,0:T(8,128)} %rate_ref.3) | copy-start | bytes 786436
  1.7 3.2 %collective-permute-start = (bf16[3,2,4096]{2,1,0:T(2,128)(2,1)S(1)}, bf16[3,2,4096]{2,1,0:T(2,128)(2,1)S(1)}, u32[]{:S(2)}, u32[]{:S(2)}) collective-permute-start(bf16[3,2,4096]{2,1,0:T(2,128)(2,1)S(1)} %slice.47), channel_id=1, source_target_pairs={{0,1},{1,4},{4,5},{5,8},{8,9},{9,12},{12,13},{2,3},{3,6},{6,7},{7,... | collective-permute-start | bytes 147464 | tf_op jit(solution)/shard_map/ppermute | solution.py:17
  4.9 0.6 %copy-start.1 = (bf16[3,2,4096]{2,1,0:T(2,128)(2,1)}, bf16[3,2,4096]{2,1,0:T(2,128)(2,1)S(1)}, u32[]{:S(2)}) copy-start(bf16[3,2,4096]{2,1,0:T(2,128)(2,1)S(1)} %collective-permute-done.halo_ref) | copy-start | bytes 147460
  14.6 4.0 %collective-permute-start.1 = (f32[16,2048]{1,0:T(8,128)S(1)}, f32[16,2048]{1,0:T(8,128)S(1)}, u32[]{:S(2)}, u32[]{:S(2)}) collective-permute-start(f32[16,2048]{1,0:T(8,128)S(1)} %slice_select_fusion.3), channel_id=1, source_target_pairs={{0,1},{1,0},{2,3},{3,2},{4,5},{5,4},{6,7},{7,6},{8,9},{9,8},{10,11... | collective-permute-start | bytes 393224 | tf_op jit(solution)/shard_map/ppermute | solution.py:137
  37.9 1.8 %collective-permute-start.2 = (f32[48,2048]{1,0:T(8,128)S(1)}, f32[48,2048]{1,0:T(8,128)S(1)}, u32[]{:S(2)}, u32[]{:S(2)}) collective-permute-start(f32[48,2048]{1,0:T(8,128)S(1)} %pad_maximum_fusion), channel_id=1, source_target_pairs={{0,1},{1,0},{2,3},{3,2},{4,5},{5,4},{6,7},{7,6},{8,9},{9,8},{10,11... | collective-permute-start | bytes 1179656 | tf_op jit(solution)/shard_map/ppermute | solution.py:137

commit v8 on v6

--- a/solution.py
+++ b/solution.py
@@ -7,7 +7,8 @@
 from jax.experimental.pallas import tpu as pltpu
 from jax.sharding import PartitionSpec as P
 
-CHAN_BLOCK = 512
+CHAN_BLOCK = 1024
+LANE_BLOCK = 512
 ROW_GROUP = 8
 
 
@@ -46,21 +47,27 @@
     row_count = drive_ref.shape[0]
     low = slice(0, ROW_GROUP)
     high = slice(ROW_GROUP, 2 * ROW_GROUP)
+    finals = []
+    for lane_start in range(0, drive_ref.shape[1], LANE_BLOCK):
+        lanes = slice(lane_start, lane_start + LANE_BLOCK)
+        decay_part = decay[:, lanes]
+        residue_part = None if residue is None else residue[:, lanes]
 
-    def body(group, state):
-        start = pl.multiple_of(group * ROW_GROUP, ROW_GROUP)
-        ys = []
-        block = drive_ref[pl.ds(start, ROW_GROUP), :]
-        for i in range(ROW_GROUP):
-            drive_row = jnp.broadcast_to(block[i : i + 1], state.shape)
-            state = decay * state + drive_row
+        def body(group, state):
+            start = pl.multiple_of(group * ROW_GROUP, ROW_GROUP)
+            ys = []
+            block = drive_ref[pl.ds(start, ROW_GROUP), lanes]
+            for i in range(ROW_GROUP):
+                drive_row = jnp.broadcast_to(block[i : i + 1], state.shape)
+                state = decay_part * state + drive_row
+                if conv_ref is not None:
+                    ys.append(residue_part[low] * state[low] + residue_part[high] * state[high])
             if conv_ref is not None:
-                ys.append(residue[low] * state[low] + residue[high] * state[high])
-        if conv_ref is not None:
-            conv_ref[pl.ds(start, ROW_GROUP), :] = _reduce_rows(ys)
-        return state
+                conv_ref[pl.ds(start, ROW_GROUP), lanes] = _reduce_rows(ys)
+            return state
 
-    return lax.fori_loop(0, row_count // ROW_GROUP, body, state)
+        finals.append(lax.fori_loop(0, row_count // ROW_GROUP, body, state[:, lanes]))
+    return jnp.concatenate(finals, axis=1)
 
 
 def _contrib_kernel(x_ref, halo_ref, filt_ref, rate_ref, out_ref, drive_ref):

time: 49.9 us -> 48.4 us (0.970)
  Pallas kernels: 18.6 us -> 17.3 us
    pallas_call x1, Pallas kernels: 8.08 us -> 6.81 us  [contributions(): pl.pallas_call(_contrib_kernel, grid=(chan_count // CHAN_BLOCK,), in_spec...]
where the time goes in v8:
time: 48.4 us; the launch traced here: 48.1 us
  Pallas kernels  17.3 us (36%)
  blocking collectives  16.4 us (34%)
  starting transfers between devices  5.41 us (11%)
  waiting for transfers between devices  3.69 us (8%)
  other arithmetic  2.93 us (6%)
  local copies, waits for them, and re-layouts  1.64 us (3%)
  between operations  0.7 us (1%)
    all_gather x1, blocking collectives, local(): received = lax.all_gather(chip_part, 'ctx', axis=0, tiled=False)  16.4 us
    pallas_call x1, Pallas kernels, mix(): pl.pallas_call(_mix_kernel, grid=(chan_count // CHAN_BLOCK,), in_specs=[x...  10.5 us
    pallas_call x1, Pallas kernels, contributions(): pl.pallas_call(_contrib_kernel, grid=(chan_count // CHAN_BLOCK,), in_spec...  6.81 us
    ppermute x2, starting transfers between devices, swap_cores(): return lax.ppermute(value, 'dec', [(0, 1), (1, 0)])  3.05 us
    ppermute x2, waiting for transfers between devices, swap_cores(): return lax.ppermute(value, 'dec', [(0, 1), (1, 0)])  2.83 us
    ppermute x1, starting transfers between devices, from_behind(): lax.ppermute(value, axis, [(source, source + steps) for source in range(i...  2.36 us
    slice x1, local copies, waits for them, and re-layouts, local(): edge_rows = projected[:, row_count - (tap_count - 1):, :]  1.02 us
    select_n x1, other arithmetic, local(): first_core = jnp.where(core == 0, contribution, other)  0.98 us
  transfers between devices with their start and end apart: 3, of which 3 were waited for; matrix products, arithmetic and copies ran while one was open for 0% of the time, Pallas kernels for 0%

profile of v8, /device:TPU:0, one launch (start us, length us, event | category | flops | bytes accessed | tf_op | source)
XLA Modules:
  0.0 48.1 jit_solution(5089565628880802917)
XLA Ops:
  0.6 0.0 copy-start
  0.6 1.0 %slice.21 = bf16[3,2,4096]{2,1,0:T(2,128)(2,1)S(1)} slice(bf16[3,128,4096]{2,1,0:T(8,128)(2,1)} %x_ref.3), slice={[0:3], [126:128], [0:4096]} | slice | bytes 98304 | tf_op jit(solution)/shard_map/slice | solution.py:140
  1.7 2.4 %collective-permute-start = (bf16[3,2,4096]{2,1,0:T(2,128)(2,1)S(1)}, bf16[3,2,4096]{2,1,0:T(2,128)(2,1)S(1)}, u32[]{:S(2)}, u32[]{:S(2)}) collective-permute-start(bf16[3,2,4096]{2,1,0:T(2,128)(2,1)S(1)} %slice.21), channel_id=1, source_target_pairs={{0,1},{1,4},{4,5},{5,8},{8,9},{9,12},{12,13},{2,3},{3,6},{6,7},{7,... | collective-permute-start | bytes 147464 | tf_op jit(solution)/shard_map/ppermute | solution.py:18
  4.0 0.9 %collective-permute-done.halo_ref = bf16[3,2,4096]{2,1,0:T(2,128)(2,1)S(1)} collective-permute-done((bf16[3,2,4096]{2,1,0:T(2,128)(2,1)S(1)}, bf16[3,2,4096]{2,1,0:T(2,128)(2,1)S(1)}, u32[]{:S(2)}, u32[]{:S(2)}) %collective-permute-start) | collective-permute-done | bytes 49184 | tf_op jit(solution)/shard_map/ppermute | solution.py:18
  4.9 0.0 copy-start.1
  4.9 0.6 %copy-done.1 = bf16[3,2,4096]{2,1,0:T(2,128)(2,1)} copy-done((bf16[3,2,4096]{2,1,0:T(2,128)(2,1)}, bf16[3,2,4096]{2,1,0:T(2,128)(2,1)S(1)}, u32[]{:S(2)}) %copy-start.1) | copy-done | bytes 49176
  5.5 6.8 %shard_map.68 = (f32[16,4096]{1,0:T(8,128)}, f32[128,4096]{1,0:T(8,128)}) custom-call(bf16[3,128,4096]{2,1,0:T(8,128)(2,1)} %x_ref.3, bf16[3,2,4096]{2,1,0:T(2,128)(2,1)} %copy-done.1, f32[3,3,4096]{2,1,0:T(4,128)} %filt_ref.3, f32[16,4096]{1,0:T(8,128)} %rate_ref.3), custom_call_target="tpu_custom_call" | custom-call | tf_op jit(solution)/shard_map/pallas_call | solution.py:104
  12.3 3.0 %collective-permute-start.1 = (f32[16,4096]{1,0:T(8,128)}, f32[16,4096]{1,0:T(8,128)S(1)}, u32[]{:S(2)}, u32[]{:S(2)}) collective-permute-start(f32[16,4096]{1,0:T(8,128)} %get-tuple-element.4), channel_id=1, source_target_pairs={{0,1},{1,0},{2,3},{3,2},{4,5},{5,4},{6,7},{7,6},{8,9},{9,8},{10,11... | collective-permute-start | bytes 786440 | tf_op jit(solution)/shard_map/ppermute | solution.py:133
  15.3 0.0 copy-done
  15.4 1.3 %collective-permute-done.1 = f32[16,4096]{1,0:T(8,128)S(1)} collective-permute-done((f32[16,4096]{1,0:T(8,128)}, f32[16,4096]{1,0:T(8,128)S(1)}, u32[]{:S(2)}, u32[]{:S(2)}) %collective-permute-start.1) | collective-permute-done | bytes 262176 | tf_op jit(solution)/shard_map/ppermute | solution.py:133
  16.7 1.0 %broadcast_select_fusion.2 = f32[16,4096]{1,0:T(8,128)S(1)} fusion(f32[16,4096]{1,0:T(8,128)} %get-tuple-element.4, f32[16,4096]{1,0:T(8,128)S(1)} %collective-permute-done.1, pred[]{:T(512)S(6)} %eq.8), kind=kLoop, calls=%fused_computation.16 | loop fusion | flops 65536 | bytes 786433 | tf_op jit(solution)/shard_map/jit(_where)/select_n | solution.py:145
  17.7 0.9 %fusion.1 = f32[16,2048]{1,0:T(8,128)S(1)} fusion(f32[16,4096]{1,0:T(8,128)} %get-tuple-element.4, s32[]{:T(128)S(6)} %select_n.61, f32[16,4096]{1,0:T(8,128)S(1)} %collective-permute-done.1, f32[16,4096]{1,0:T(8,128)S(1)} %broadcast_select_fusion.2, f32[16,4096]{1,0:T(8,128)S(1)} %multiply_exponential_fusion, pred[]{:T(512)S(6)} %eq.8), kind=kLoop, calls=%fused_computation.12 | loop fusion | flops 98304 | bytes 655365 | tf_op jit(solution)/shard_map/add | solution.py:152
  18.6 16.4 %all-gather = f32[64,2048]{1,0:T(8,128)S(1)} all-gather(f32[16,2048]{1,0:T(8,128)S(1)} %fusion.1), channel_id=2, replica_groups=mesh['grp'=2,'ctx'=4,'chan'=2,'dec'=2] {'ctx'}, dimensions={0}, use_global_device_ids=true | all-gather | bytes 655360 | tf_op jit(solution)/shard_map/all_gather | solution.py:153
  35.0 0.1 select_select_fusion
  35.1 0.1 collective-permute-start.2
  35.2 1.5 %collective-permute-done.2 = f32[32,2048]{1,0:T(8,128)S(1)} collective-permute-done((f32[32,2048]{1,0:T(8,128)S(1)}, f32[32,2048]{1,0:T(8,128)S(1)}, u32[]{:S(2)}, u32[]{:S(2)}) %collective-permute-start.2) | collective-permute-done | bytes 262176 | tf_op jit(solution)/shard_map/ppermute | solution.py:133
  36.7 0.8 %pad_maximum_fusion = (f32[16,4096]{1,0:T(8,128)}, f32[16,4096]{1,0:T(8,128)}) fusion(f32[32,2048]{1,0:T(8,128)S(1)} %get-tuple-element.11, f32[32,2048]{1,0:T(8,128)S(1)} %get-tuple-element.10, f32[16,4096]{1,0:T(8,128)S(1)} %broadcast_select_fusion.2, f32[16,4096]{1,0:T(8,128)S(1)} %copy-done, pred[]{:T(512)S(6)} %eq.8), kind=kLoop, calls=%fused_computation.3 | loop fusion | flops 458752 | bytes 1572865 | tf_op jit(solution)/shard_map/concatenate | solution.py:164
  37.6 10.5 %shard_map.69 = bf16[128,4096]{1,0:T(8,128)(2,1)} custom-call(bf16[3,128,4096]{2,1,0:T(8,128)(2,1)} %x_ref.3, bf16[3,2,4096]{2,1,0:T(2,128)(2,1)} %copy-done.1, f32[3,3,4096]{2,1,0:T(4,128)} %filt_ref.3, f32[16,4096]{1,0:T(8,128)} %rate_ref.3, f32[16,4096]{1,0:T(8,128)} %res_ref.1, f32[1,4096]{1,0:T(1,128)} %bitcast.1, ...), custom_call_target="tpu_custom_call" | custom-call | tf_op jit(solution)/shard_map/pallas_call | solution.py:122
  (3 shorter events, 0.1 us)
Async XLA Ops:
  0.6 14.7 %copy-start = (f32[16,4096]{1,0:T(8,128)S(1)}, f32[16,4096]{1,0:T(8,128)}, u32[]{:S(2)}) copy-start(f32[16,4096]{1,0:T(8,128)} %rate_ref.3) | copy-start | bytes 786436
  1.7 3.2 %collective-permute-start = (bf16[3,2,4096]{2,1,0:T(2,128)(2,1)S(1)}, bf16[3,2,4096]{2,1,0:T(2,128)(2,1)S(1)}, u32[]{:S(2)}, u32[]{:S(2)}) collective-permute-start(bf16[3,2,4096]{2,1,0:T(2,128)(2,1)S(1)} %slice.21), channel_id=1, source_target_pairs={{0,1},{1,4},{4,5},{5,8},{8,9},{9,12},{12,13},{2,3},{3,6},{6,7},{7,... | collective-permute-start | bytes 147464 | tf_op jit(solution)/shard_map/ppermute | solution.py:18
  4.9 0.6 %copy-start.1 = (bf16[3,2,4096]{2,1,0:T(2,128)(2,1)}, bf16[3,2,4096]{2,1,0:T(2,128)(2,1)S(1)}, u32[]{:S(2)}) copy-start(bf16[3,2,4096]{2,1,0:T(2,128)(2,1)S(1)} %collective-permute-done.halo_ref) | copy-start | bytes 147460
  12.3 4.4 %collective-permute-start.1 = (f32[16,4096]{1,0:T(8,128)}, f32[16,4096]{1,0:T(8,128)S(1)}, u32[]{:S(2)}, u32[]{:S(2)}) collective-permute-start(f32[16,4096]{1,0:T(8,128)} %get-tuple-element.4), channel_id=1, source_target_pairs={{0,1},{1,0},{2,3},{3,2},{4,5},{5,4},{6,7},{7,6},{8,9},{9,8},{10,11... | collective-permute-start | bytes 786440 | tf_op jit(solution)/shard_map/ppermute | solution.py:133
  35.1 1.6 %collective-permute-start.2 = (f32[32,2048]{1,0:T(8,128)S(1)}, f32[32,2048]{1,0:T(8,128)S(1)}, u32[]{:S(2)}, u32[]{:S(2)}) collective-permute-start(f32[32,2048]{1,0:T(8,128)S(1)} %pad_maximum_fusion.1), channel_id=1, source_target_pairs={{0,1},{1,0},{2,3},{3,2},{4,5},{5,4},{6,7},{7,6},{8,9},{9,8},{10,11... | collective-permute-start | bytes 786440 | tf_op jit(solution)/shard_map/ppermute | solution.py:133

commit v9 on v8

--- a/solution.py
+++ b/solution.py
@@ -8,6 +8,7 @@
 from jax.sharding import PartitionSpec as P
 
 CHAN_BLOCK = 1024
+CONTRIB_BLOCK = 2048
 LANE_BLOCK = 512
 ROW_GROUP = 8
 
@@ -87,12 +88,12 @@
     out_ref[...] = (q * (conv_scr[...] + skip_ref[...] * drive_ref[...])).astype(out_ref.dtype)
 
 
-def _specs(row_count, modes, taps, features=3):
-    x_spec = pl.BlockSpec((features, row_count, CHAN_BLOCK), lambda j: (0, 0, j))
-    halo_spec = pl.BlockSpec((features, taps - 1, CHAN_BLOCK), lambda j: (0, 0, j))
-    filt_spec = pl.BlockSpec((features, taps, CHAN_BLOCK), lambda j: (0, 0, j))
-    mode_spec = pl.BlockSpec((modes, CHAN_BLOCK), lambda j: (0, j))
-    row_spec = pl.BlockSpec((1, CHAN_BLOCK), lambda j: (0, j))
+def _specs(row_count, modes, taps, features=3, block=CHAN_BLOCK):
+    x_spec = pl.BlockSpec((features, row_count, block), lambda j: (0, 0, j))
+    halo_spec = pl.BlockSpec((features, taps - 1, block), lambda j: (0, 0, j))
+    filt_spec = pl.BlockSpec((features, taps, block), lambda j: (0, 0, j))
+    mode_spec = pl.BlockSpec((modes, block), lambda j: (0, j))
+    row_spec = pl.BlockSpec((1, block), lambda j: (0, j))
     return x_spec, halo_spec, filt_spec, mode_spec, row_spec
 
 
@@ -100,12 +101,13 @@
     _, row_count, chan_count = projected.shape
     modes = decay_rate.shape[0]
     taps = short_filters.shape[1]
-    x_spec, halo_spec, filt_spec, mode_spec, _ = _specs(row_count, modes, taps)
+    block = min(CONTRIB_BLOCK, chan_count)
+    x_spec, halo_spec, filt_spec, mode_spec, _ = _specs(row_count, modes, taps, 3, block)
     return pl.pallas_call(
         _contrib_kernel,
-        grid=(chan_count // CHAN_BLOCK,),
+        grid=(chan_count // block,),
         in_specs=[x_spec, halo_spec, filt_spec, mode_spec],
-        out_specs=[mode_spec, pl.BlockSpec((row_count, CHAN_BLOCK), lambda j: (0, j))],
+        out_specs=[mode_spec, pl.BlockSpec((row_count, block), lambda j: (0, j))],
         out_shape=[
             jax.ShapeDtypeStruct((modes, chan_count), jnp.float32),
             jax.ShapeDtypeStruct((row_count, chan_count), jnp.float32),
@@ -117,15 +119,16 @@
     _, row_count, chan_count = projected.shape
     modes = decay_rate.shape[0]
     taps = short_filters.shape[1]
-    x_spec, halo_spec, filt_spec, mode_spec, row_spec = _specs(row_count, modes, taps, 1)
-    tile_spec = pl.BlockSpec((row_count, CHAN_BLOCK), lambda j: (0, j))
+    block = min(CHAN_BLOCK, chan_count)
+    x_spec, halo_spec, filt_spec, mode_spec, row_spec = _specs(row_count, modes, taps, 1, block)
+    tile_spec = pl.BlockSpec((row_count, block), lambda j: (0, j))
     return pl.pallas_call(
         _mix_kernel,
-        grid=(chan_count // CHAN_BLOCK,),
+        grid=(chan_count // block,),
         in_specs=[x_spec, halo_spec, filt_spec, mode_spec, mode_spec, row_spec, mode_spec, tile_spec],
         out_specs=tile_spec,
         out_shape=jax.ShapeDtypeStruct((row_count, chan_count), jnp.bfloat16),
-        scratch_shapes=[pltpu.VMEM((row_count, CHAN_BLOCK), jnp.float32)],
+        scratch_shapes=[pltpu.VMEM((row_count, block), jnp.float32)],
     )(projected, halo, short_filters, decay_rate, residue, skip[None, :], prefix, drive)
 
 

time: 48.4 us -> 48.6 us (level)
  no operation moved by 1% of the time
where the time goes in v9:
time: 48.6 us; the launch traced here: 48.4 us
  Pallas kernels  17.6 us (36%)
  blocking collectives  16.4 us (34%)
  starting transfers between devices  5.41 us (11%)
  waiting for transfers between devices  3.69 us (8%)
  other arithmetic  2.93 us (6%)
  local copies, waits for them, and re-layouts  1.64 us (3%)
  between operations  0.7 us (1%)
    all_gather x1, blocking collectives, local(): received = lax.all_gather(chip_part, 'ctx', axis=0, tiled=False)  16.4 us
    pallas_call x1, Pallas kernels, mix(): pl.pallas_call(_mix_kernel, grid=(chan_count // block,), in_specs=[x_spec...  10.5 us
    pallas_call x1, Pallas kernels, contributions(): pl.pallas_call(_contrib_kernel, grid=(chan_count // block,), in_specs=[x_...  7.05 us
    ppermute x2, starting transfers between devices, swap_cores(): return lax.ppermute(value, 'dec', [(0, 1), (1, 0)])  3.05 us
    ppermute x2, waiting for transfers between devices, swap_cores(): return lax.ppermute(value, 'dec', [(0, 1), (1, 0)])  2.83 us
    ppermute x1, starting transfers between devices, from_behind(): lax.ppermute(value, axis, [(source, source + steps) for source in range(i...  2.36 us
    slice x1, local copies, waits for them, and re-layouts, local(): edge_rows = projected[:, row_count - (tap_count - 1):, :]  1.02 us
    select_n x1, other arithmetic, local(): first_core = jnp.where(core == 0, contribution, other)  0.98 us
  transfers between devices with their start and end apart: 3, of which 3 were waited for; matrix products, arithmetic and copies ran while one was open for 0% of the time, Pallas kernels for 0%

profile of v9, /device:TPU:0, one launch (start us, length us, event | category | flops | bytes accessed | tf_op | source)
XLA Modules:
  0.0 48.4 jit_solution(14337663139551130002)
XLA Ops:
  0.6 0.0 copy-start
  0.6 1.0 %slice.21 = bf16[3,2,4096]{2,1,0:T(2,128)(2,1)S(1)} slice(bf16[3,128,4096]{2,1,0:T(8,128)(2,1)} %x_ref.3), slice={[0:3], [126:128], [0:4096]} | slice | bytes 98304 | tf_op jit(solution)/shard_map/slice | solution.py:143
  1.7 2.4 %collective-permute-start = (bf16[3,2,4096]{2,1,0:T(2,128)(2,1)S(1)}, bf16[3,2,4096]{2,1,0:T(2,128)(2,1)S(1)}, u32[]{:S(2)}, u32[]{:S(2)}) collective-permute-start(bf16[3,2,4096]{2,1,0:T(2,128)(2,1)S(1)} %slice.21), channel_id=1, source_target_pairs={{0,1},{1,4},{4,5},{5,8},{8,9},{9,12},{12,13},{2,3},{3,6},{6,7},{7,... | collective-permute-start | bytes 147464 | tf_op jit(solution)/shard_map/ppermute | solution.py:19
  4.0 0.9 %collective-permute-done.halo_ref = bf16[3,2,4096]{2,1,0:T(2,128)(2,1)S(1)} collective-permute-done((bf16[3,2,4096]{2,1,0:T(2,128)(2,1)S(1)}, bf16[3,2,4096]{2,1,0:T(2,128)(2,1)S(1)}, u32[]{:S(2)}, u32[]{:S(2)}) %collective-permute-start) | collective-permute-done | bytes 49184 | tf_op jit(solution)/shard_map/ppermute | solution.py:19
  4.9 0.0 copy-start.1
  4.9 0.6 %copy-done.1 = bf16[3,2,4096]{2,1,0:T(2,128)(2,1)} copy-done((bf16[3,2,4096]{2,1,0:T(2,128)(2,1)}, bf16[3,2,4096]{2,1,0:T(2,128)(2,1)S(1)}, u32[]{:S(2)}) %copy-start.1) | copy-done | bytes 49176
  5.5 7.0 %shard_map.68 = (f32[16,4096]{1,0:T(8,128)}, f32[128,4096]{1,0:T(8,128)}) custom-call(bf16[3,128,4096]{2,1,0:T(8,128)(2,1)} %x_ref.3, bf16[3,2,4096]{2,1,0:T(2,128)(2,1)} %copy-done.1, f32[3,3,4096]{2,1,0:T(4,128)} %filt_ref.3, f32[16,4096]{1,0:T(8,128)} %rate_ref.3), custom_call_target="tpu_custom_call" | custom-call | tf_op jit(solution)/shard_map/pallas_call | solution.py:106
  12.6 3.0 %collective-permute-start.1 = (f32[16,4096]{1,0:T(8,128)}, f32[16,4096]{1,0:T(8,128)S(1)}, u32[]{:S(2)}, u32[]{:S(2)}) collective-permute-start(f32[16,4096]{1,0:T(8,128)} %get-tuple-element.4), channel_id=1, source_target_pairs={{0,1},{1,0},{2,3},{3,2},{4,5},{5,4},{6,7},{7,6},{8,9},{9,8},{10,11... | collective-permute-start | bytes 786440 | tf_op jit(solution)/shard_map/ppermute | solution.py:136
  15.5 0.0 copy-done
  15.6 1.3 %collective-permute-done.1 = f32[16,4096]{1,0:T(8,128)S(1)} collective-permute-done((f32[16,4096]{1,0:T(8,128)}, f32[16,4096]{1,0:T(8,128)S(1)}, u32[]{:S(2)}, u32[]{:S(2)}) %collective-permute-start.1) | collective-permute-done | bytes 262176 | tf_op jit(solution)/shard_map/ppermute | solution.py:136
  16.9 1.0 %broadcast_select_fusion.2 = f32[16,4096]{1,0:T(8,128)S(1)} fusion(f32[16,4096]{1,0:T(8,128)} %get-tuple-element.4, f32[16,4096]{1,0:T(8,128)S(1)} %collective-permute-done.1, pred[]{:T(512)S(6)} %eq.8), kind=kLoop, calls=%fused_computation.16 | loop fusion | flops 65536 | bytes 786433 | tf_op jit(solution)/shard_map/jit(_where)/select_n | solution.py:148
  17.9 0.9 %fusion.1 = f32[16,2048]{1,0:T(8,128)S(1)} fusion(f32[16,4096]{1,0:T(8,128)} %get-tuple-element.4, s32[]{:T(128)S(6)} %select_n.61, f32[16,4096]{1,0:T(8,128)S(1)} %collective-permute-done.1, f32[16,4096]{1,0:T(8,128)S(1)} %broadcast_select_fusion.2, f32[16,4096]{1,0:T(8,128)S(1)} %multiply_exponential_fusion, pred[]{:T(512)S(6)} %eq.8), kind=kLoop, calls=%fused_computation.12 | loop fusion | flops 98304 | bytes 655365 | tf_op jit(solution)/shard_map/add | solution.py:155
  18.8 16.4 %all-gather = f32[64,2048]{1,0:T(8,128)S(1)} all-gather(f32[16,2048]{1,0:T(8,128)S(1)} %fusion.1), channel_id=2, replica_groups=mesh['grp'=2,'ctx'=4,'chan'=2,'dec'=2] {'ctx'}, dimensions={0}, use_global_device_ids=true | all-gather | bytes 655360 | tf_op jit(solution)/shard_map/all_gather | solution.py:156
  35.2 0.1 select_select_fusion
  35.3 0.1 collective-permute-start.2
  35.4 1.5 %collective-permute-done.2 = f32[32,2048]{1,0:T(8,128)S(1)} collective-permute-done((f32[32,2048]{1,0:T(8,128)S(1)}, f32[32,2048]{1,0:T(8,128)S(1)}, u32[]{:S(2)}, u32[]{:S(2)}) %collective-permute-start.2) | collective-permute-done | bytes 262176 | tf_op jit(solution)/shard_map/ppermute | solution.py:136
  37.0 0.8 %pad_maximum_fusion = (f32[16,4096]{1,0:T(8,128)}, f32[16,4096]{1,0:T(8,128)}) fusion(f32[32,2048]{1,0:T(8,128)S(1)} %get-tuple-element.11, f32[32,2048]{1,0:T(8,128)S(1)} %get-tuple-element.10, f32[16,4096]{1,0:T(8,128)S(1)} %broadcast_select_fusion.2, f32[16,4096]{1,0:T(8,128)S(1)} %copy-done, pred[]{:T(512)S(6)} %eq.8), kind=kLoop, calls=%fused_computation.3 | loop fusion | flops 458752 | bytes 1572865 | tf_op jit(solution)/shard_map/concatenate | solution.py:167
  37.8 10.5 %shard_map.69 = bf16[128,4096]{1,0:T(8,128)(2,1)} custom-call(bf16[3,128,4096]{2,1,0:T(8,128)(2,1)} %x_ref.3, bf16[3,2,4096]{2,1,0:T(2,128)(2,1)} %copy-done.1, f32[3,3,4096]{2,1,0:T(4,128)} %filt_ref.3, f32[16,4096]{1,0:T(8,128)} %rate_ref.3, f32[16,4096]{1,0:T(8,128)} %res_ref.1, f32[1,4096]{1,0:T(1,128)} %bitcast.1, ...), custom_call_target="tpu_custom_call" | custom-call | tf_op jit(solution)/shard_map/pallas_call | solution.py:125
  (3 shorter events, 0.1 us)
Async XLA Ops:
  0.6 14.9 %copy-start = (f32[16,4096]{1,0:T(8,128)S(1)}, f32[16,4096]{1,0:T(8,128)}, u32[]{:S(2)}) copy-start(f32[16,4096]{1,0:T(8,128)} %rate_ref.3) | copy-start | bytes 786436
  1.7 3.2 %collective-permute-start = (bf16[3,2,4096]{2,1,0:T(2,128)(2,1)S(1)}, bf16[3,2,4096]{2,1,0:T(2,128)(2,1)S(1)}, u32[]{:S(2)}, u32[]{:S(2)}) collective-permute-start(bf16[3,2,4096]{2,1,0:T(2,128)(2,1)S(1)} %slice.21), channel_id=1, source_target_pairs={{0,1},{1,4},{4,5},{5,8},{8,9},{9,12},{12,13},{2,3},{3,6},{6,7},{7,... | collective-permute-start | bytes 147464 | tf_op jit(solution)/shard_map/ppermute | solution.py:19
  4.9 0.6 %copy-start.1 = (bf16[3,2,4096]{2,1,0:T(2,128)(2,1)}, bf16[3,2,4096]{2,1,0:T(2,128)(2,1)S(1)}, u32[]{:S(2)}) copy-start(bf16[3,2,4096]{2,1,0:T(2,128)(2,1)S(1)} %collective-permute-done.halo_ref) | copy-start | bytes 147460
  12.6 4.4 %collective-permute-start.1 = (f32[16,4096]{1,0:T(8,128)}, f32[16,4096]{1,0:T(8,128)S(1)}, u32[]{:S(2)}, u32[]{:S(2)}) collective-permute-start(f32[16,4096]{1,0:T(8,128)} %get-tuple-element.4), channel_id=1, source_target_pairs={{0,1},{1,0},{2,3},{3,2},{4,5},{5,4},{6,7},{7,6},{8,9},{9,8},{10,11... | collective-permute-start | bytes 786440 | tf_op jit(solution)/shard_map/ppermute | solution.py:136
  35.3 1.6 %collective-permute-start.2 = (f32[32,2048]{1,0:T(8,128)S(1)}, f32[32,2048]{1,0:T(8,128)S(1)}, u32[]{:S(2)}, u32[]{:S(2)}) collective-permute-start(f32[32,2048]{1,0:T(8,128)S(1)} %pad_maximum_fusion.1), channel_id=1, source_target_pairs={{0,1},{1,0},{2,3},{3,2},{4,5},{5,4},{6,7},{7,6},{8,9},{9,8},{10,11... | collective-permute-start | bytes 786440 | tf_op jit(solution)/shard_map/ppermute | solution.py:136

commit v10 on v8

--- a/solution.py
+++ b/solution.py
@@ -75,14 +75,19 @@
     v = _featurize_one(x_ref, halo_ref, filt_ref, 2)
     drive_ref[...] = k * v
     decay = jnp.exp(-rate_ref[...])
-    state = jnp.zeros(out_ref.shape, jnp.float32)
-    out_ref[...] = _scan_rows(drive_ref, decay, None, state, None)
-
-
-def _mix_kernel(x_ref, halo_ref, filt_ref, rate_ref, res_ref, skip_ref, init_ref, drive_ref, out_ref,
-                conv_scr):
+    block = rate_ref.shape[1]
+    start = pl.multiple_of(pl.program_id(0) * block, block)
+    state = jnp.zeros(rate_ref.shape, jnp.float32)
+    out_ref[:, pl.ds(start, block)] = _scan_rows(drive_ref, decay, None, state, None)
+
+
+def _mix_kernel(x_ref, halo_ref, filt_ref, rate_ref, res_ref, skip_ref, init_ref, fin_in_ref, drive_ref,
+                out_ref, fin_ref, conv_scr):
+    block = rate_ref.shape[1]
+    start = pl.multiple_of(pl.program_id(0) * block, block)
+    fin_ref[...] = fin_in_ref[:, pl.ds(start, block)]
     decay = jnp.exp(-rate_ref[...])
-    _scan_rows(drive_ref, decay, res_ref[...], init_ref[...], conv_scr)
+    _scan_rows(drive_ref, decay, res_ref[...], init_ref[:, pl.ds(start, block)], conv_scr)
     q = _featurize_one(x_ref, halo_ref, filt_ref, 0)
     out_ref[...] = (q * (conv_scr[...] + skip_ref[...] * drive_ref[...])).astype(out_ref.dtype)
 
@@ -105,7 +110,7 @@
         _contrib_kernel,
         grid=(chan_count // CHAN_BLOCK,),
         in_specs=[x_spec, halo_spec, filt_spec, mode_spec],
-        out_specs=[mode_spec, pl.BlockSpec((row_count, CHAN_BLOCK), lambda j: (0, j))],
+        out_specs=[pl.BlockSpec(memory_space=pltpu.VMEM), pl.BlockSpec((row_count, CHAN_BLOCK), lambda j: (0, j))],
         out_shape=[
             jax.ShapeDtypeStruct((modes, chan_count), jnp.float32),
             jax.ShapeDtypeStruct((row_count, chan_count), jnp.float32),
@@ -113,20 +118,24 @@
     )(projected, halo, short_filters, decay_rate)
 
 
-def mix(projected, halo, short_filters, decay_rate, residue, skip, prefix, drive):
+def mix(projected, halo, short_filters, decay_rate, residue, skip, prefix, final_state, drive):
     _, row_count, chan_count = projected.shape
     modes = decay_rate.shape[0]
     taps = short_filters.shape[1]
     x_spec, halo_spec, filt_spec, mode_spec, row_spec = _specs(row_count, modes, taps, 1)
     tile_spec = pl.BlockSpec((row_count, CHAN_BLOCK), lambda j: (0, j))
+    whole = pl.BlockSpec(memory_space=pltpu.VMEM)
     return pl.pallas_call(
         _mix_kernel,
         grid=(chan_count // CHAN_BLOCK,),
-        in_specs=[x_spec, halo_spec, filt_spec, mode_spec, mode_spec, row_spec, mode_spec, tile_spec],
-        out_specs=tile_spec,
-        out_shape=jax.ShapeDtypeStruct((row_count, chan_count), jnp.bfloat16),
+        in_specs=[x_spec, halo_spec, filt_spec, mode_spec, mode_spec, row_spec, whole, whole, tile_spec],
+        out_specs=[tile_spec, mode_spec],
+        out_shape=[
+            jax.ShapeDtypeStruct((row_count, chan_count), jnp.bfloat16),
+            jax.ShapeDtypeStruct((modes, chan_count), jnp.float32),
+        ],
         scratch_shapes=[pltpu.VMEM((row_count, CHAN_BLOCK), jnp.float32)],
-    )(projected, halo, short_filters, decay_rate, residue, skip[None, :], prefix, drive)
+    )(projected, halo, short_filters, decay_rate, residue, skip[None, :], prefix, final_state, drive)
 
 
 def swap_cores(value):
@@ -137,21 +146,26 @@
     tap_count = short_filters.shape[1]
     row_count = projected.shape[1]
     chan_count = projected.shape[2]
+    modes = decay_rate.shape[0]
     edge_rows = projected[:, row_count - (tap_count - 1) :, :]
     halo = from_behind(edge_rows, ("ctx", "dec"), 1)
     contribution, drive = contributions(projected, halo, short_filters, decay_rate)
     core = lax.axis_index("dec")
+    first = core == 0
     other = swap_cores(contribution)
-    first_core = jnp.where(core == 0, contribution, other)
-    second_core = jnp.where(core == 0, other, contribution)
     shard_decay = jnp.exp(-decay_rate * row_count)
     half = chan_count // 2
-    start = core * half
-    mine = lambda x: lax.dynamic_slice_in_dim(x, start, half, 1)
-    chip_decay = mine(shard_decay) * mine(shard_decay)
-    chip_part = mine(shard_decay) * mine(first_core) + mine(second_core)
+    lo = lambda x: x[:, :half]
+    hi = lambda x: x[:, half:]
+    chip_part = jnp.where(
+        first,
+        lo(shard_decay) * lo(contribution) + lo(other),
+        hi(shard_decay) * hi(other) + hi(contribution),
+    )
+    half_decay = jnp.where(first, lo(shard_decay), hi(shard_decay))
     received = lax.all_gather(chip_part, "ctx", axis=0, tiled=False)
     chip_here = lax.axis_index("ctx")
+    chip_decay = half_decay * half_decay
     running = jnp.zeros_like(chip_part)
     entering = jnp.zeros_like(chip_part)
     for chip in range(received.shape[0]):
@@ -159,14 +173,14 @@
         running = chip_decay * running + received[chip]
     both = jnp.concatenate([entering, running], axis=0)
     other_both = swap_cores(both)
-    low = jnp.where(core == 0, both, other_both)
-    high = jnp.where(core == 0, other_both, both)
+    low = jnp.where(first, both, other_both)
+    high = jnp.where(first, other_both, both)
     whole = jnp.concatenate([low, high], axis=1)
-    modes = decay_rate.shape[0]
     chip_entering = whole[:modes]
     final_state = whole[modes:]
-    prefix = jnp.where(core == 0, chip_entering, shard_decay * chip_entering + first_core)
-    mixed = mix(projected, halo, short_filters, decay_rate, residue, skip, prefix, drive)
+    prefix = jnp.where(first, chip_entering, shard_decay * chip_entering + other)
+    mixed, final_state = mix(projected, halo, short_filters, decay_rate, residue, skip, prefix,
+                             final_state, drive)
     return (mixed, final_state)
 
 

time: 48.4 us -> 48.5 us (level)
  other arithmetic: 2.93 us -> 2.05 us
  blocking collectives: 16.4 us -> 17.2 us
    add x1 -> x0, other arithmetic: 0.94 us -> none  [local(): chip_part = mine(shard_decay) * mine(first_core) + mine(second_core)]
    all_gather x1, blocking collectives: 16.4 us -> 17.2 us  [local(): received = lax.all_gather(chip_part, 'ctx', axis=0, tiled=False)]
where the time goes in v10:
time: 48.5 us; the launch traced here: 48.2 us
  Pallas kernels  17.5 us (36%)
  blocking collectives  17.2 us (35%)
  starting transfers between devices  5.41 us (11%)
  waiting for transfers between devices  3.69 us (8%)
  other arithmetic  2.05 us (4%)
  local copies, waits for them, and re-layouts  1.64 us (3%)
  between operations  0.69 us (1%)
    all_gather x1, blocking collectives, local(): received = lax.all_gather(chip_part, 'ctx', axis=0, tiled=False)  17.2 us
    pallas_call x1, Pallas kernels, mix(): pl.pallas_call(_mix_kernel, grid=(chan_count // CHAN_BLOCK,), in_specs=[x...  10.7 us
    pallas_call x1, Pallas kernels, contributions(): pl.pallas_call(_contrib_kernel, grid=(chan_count // CHAN_BLOCK,), in_spec...  6.85 us
    ppermute x2, starting transfers between devices, swap_cores(): return lax.ppermute(value, 'dec', [(0, 1), (1, 0)])  3.05 us
    ppermute x2, waiting for transfers between devices, swap_cores(): return lax.ppermute(value, 'dec', [(0, 1), (1, 0)])  2.83 us
    ppermute x1, starting transfers between devices, from_behind(): lax.ppermute(value, axis, [(source, source + steps) for source in range(i...  2.36 us
    slice x1, local copies, waits for them, and re-layouts, local(): edge_rows = projected[:, row_count - (tap_count - 1):, :]  1.02 us
    select_n x1, other arithmetic, local(): jnp.where(first, lo(shard_decay) * lo(contribution) + lo(other), hi(shard...  1.01 us
  transfers between devices with their start and end apart: 3, of which 3 were waited for; matrix products, arithmetic and copies ran while one was open for 0% of the time, Pallas kernels for 0%

profile of v10, /device:TPU:0, one launch (start us, length us, event | category | flops | bytes accessed | tf_op | source)
XLA Modules:
  0.0 48.2 jit_solution(17619802086154781655)
XLA Ops:
  0.6 0.0 copy-start
  0.6 1.0 %slice.41 = bf16[3,2,4096]{2,1,0:T(2,128)(2,1)S(1)} slice(bf16[3,128,4096]{2,1,0:T(8,128)(2,1)} %x_ref.3), slice={[0:3], [126:128], [0:4096]} | slice | bytes 98304 | tf_op jit(solution)/shard_map/slice | solution.py:150
  1.7 2.4 %collective-permute-start = (bf16[3,2,4096]{2,1,0:T(2,128)(2,1)S(1)}, bf16[3,2,4096]{2,1,0:T(2,128)(2,1)S(1)}, u32[]{:S(2)}, u32[]{:S(2)}) collective-permute-start(bf16[3,2,4096]{2,1,0:T(2,128)(2,1)S(1)} %slice.41), channel_id=1, source_target_pairs={{0,1},{1,4},{4,5},{5,8},{8,9},{9,12},{12,13},{2,3},{3,6},{6,7},{7,... | collective-permute-start | bytes 147464 | tf_op jit(solution)/shard_map/ppermute | solution.py:18
  4.0 0.9 %collective-permute-done.halo_ref = bf16[3,2,4096]{2,1,0:T(2,128)(2,1)S(1)} collective-permute-done((bf16[3,2,4096]{2,1,0:T(2,128)(2,1)S(1)}, bf16[3,2,4096]{2,1,0:T(2,128)(2,1)S(1)}, u32[]{:S(2)}, u32[]{:S(2)}) %collective-permute-start) | collective-permute-done | bytes 49184 | tf_op jit(solution)/shard_map/ppermute | solution.py:18
  4.9 0.0 copy-start.1
  4.9 0.6 %copy-done.1 = bf16[3,2,4096]{2,1,0:T(2,128)(2,1)} copy-done((bf16[3,2,4096]{2,1,0:T(2,128)(2,1)}, bf16[3,2,4096]{2,1,0:T(2,128)(2,1)S(1)}, u32[]{:S(2)}) %copy-start.1) | copy-done | bytes 49176
  5.5 6.8 %shard_map.68 = (f32[16,4096]{1,0:T(8,128)}, f32[128,4096]{1,0:T(8,128)}) custom-call(bf16[3,128,4096]{2,1,0:T(8,128)(2,1)} %x_ref.3, bf16[3,2,4096]{2,1,0:T(2,128)(2,1)} %copy-done.1, f32[3,3,4096]{2,1,0:T(4,128)} %filt_ref.3, f32[16,4096]{1,0:T(8,128)} %rate_ref.3), custom_call_target="tpu_custom_call" | custom-call | tf_op jit(solution)/shard_map/pallas_call | solution.py:109
  12.4 3.0 %collective-permute-start.1 = (f32[16,4096]{1,0:T(8,128)}, f32[16,4096]{1,0:T(8,128)S(1)}, u32[]{:S(2)}, u32[]{:S(2)}) collective-permute-start(f32[16,4096]{1,0:T(8,128)} %get-tuple-element.4), channel_id=1, source_target_pairs={{0,1},{1,0},{2,3},{3,2},{4,5},{5,4},{6,7},{7,6},{8,9},{9,8},{10,11... | collective-permute-start | bytes 786440 | tf_op jit(solution)/shard_map/ppermute | solution.py:142
  15.3 0.0 copy-done
  15.4 1.3 %collective-permute-done.1 = f32[16,4096]{1,0:T(8,128)S(1)} collective-permute-done((f32[16,4096]{1,0:T(8,128)}, f32[16,4096]{1,0:T(8,128)S(1)}, u32[]{:S(2)}, u32[]{:S(2)}) %collective-permute-start.1) | collective-permute-done | bytes 262176 | tf_op jit(solution)/shard_map/ppermute | solution.py:142
  16.7 1.0 %fusion.2 = f32[16,2048]{1,0:T(8,128)S(1)} fusion(f32[16,4096]{1,0:T(8,128)S(1)} %collective-permute-done.1, f32[16,4096]{1,0:T(8,128)} %get-tuple-element.4, f32[16,4096]{1,0:T(8,128)S(1)} %multiply_exponential_fusion, pred[]{:T(512)S(6)} %eq.13), kind=kLoop, calls=%fused_computation.13 | loop fusion | flops 163840 | bytes 917505 | tf_op jit(solution)/shard_map/jit(_where)/select_n | solution.py:160
  17.7 17.2 %all-gather = f32[64,2048]{1,0:T(8,128)S(1)} all-gather(f32[16,2048]{1,0:T(8,128)S(1)} %fusion.2), channel_id=2, replica_groups=mesh['grp'=2,'ctx'=4,'chan'=2,'dec'=2] {'ctx'}, dimensions={0}, use_global_device_ids=true | all-gather | bytes 655360 | tf_op jit(solution)/shard_map/all_gather | solution.py:166
  34.9 0.1 select_select_fusion
  35.0 0.1 collective-permute-start.2
  35.1 1.5 %collective-permute-done.2 = f32[32,2048]{1,0:T(8,128)S(1)} collective-permute-done((f32[32,2048]{1,0:T(8,128)S(1)}, f32[32,2048]{1,0:T(8,128)S(1)}, u32[]{:S(2)}, u32[]{:S(2)}) %collective-permute-start.2) | collective-permute-done | bytes 262176 | tf_op jit(solution)/shard_map/ppermute | solution.py:142
  36.6 0.9 %pad_maximum_fusion = (f32[16,4096]{1,0:T(8,128)}, f32[16,4096]{1,0:T(8,128)}) fusion(f32[32,2048]{1,0:T(8,128)S(1)} %get-tuple-element.11, f32[32,2048]{1,0:T(8,128)S(1)} %get-tuple-element.10, f32[16,4096]{1,0:T(8,128)S(1)} %collective-permute-done.1, f32[16,4096]{1,0:T(8,128)S(1)} %copy-done, pred[]{:T(512)S(6)} %eq.13), kind=kLoop, calls=%fused_computation.3 | loop fusion | flops 458752 | bytes 1572865 | tf_op jit(solution)/shard_map/concatenate | solution.py:178
  37.5 10.7 %shard_map.69 = (bf16[128,4096]{1,0:T(8,128)(2,1)}, f32[16,4096]{1,0:T(8,128)}) custom-call(bf16[3,128,4096]{2,1,0:T(8,128)(2,1)} %x_ref.3, bf16[3,2,4096]{2,1,0:T(2,128)(2,1)} %copy-done.1, f32[3,3,4096]{2,1,0:T(4,128)} %filt_ref.3, f32[16,4096]{1,0:T(8,128)} %rate_ref.3, f32[16,4096]{1,0:T(8,128)} %res_ref.1, f32[1,4096]{1,0:T(1,128)} %bitcast.1, ...), custom_call_target="tpu_custom_call" | custom-call | tf_op jit(solution)/shard_map/pallas_call | solution.py:128
  (3 shorter events, 0.1 us)
Async XLA Ops:
  0.6 14.7 %copy-start = (f32[16,4096]{1,0:T(8,128)S(1)}, f32[16,4096]{1,0:T(8,128)}, u32[]{:S(2)}) copy-start(f32[16,4096]{1,0:T(8,128)} %rate_ref.3) | copy-start | bytes 786436
  1.7 3.2 %collective-permute-start = (bf16[3,2,4096]{2,1,0:T(2,128)(2,1)S(1)}, bf16[3,2,4096]{2,1,0:T(2,128)(2,1)S(1)}, u32[]{:S(2)}, u32[]{:S(2)}) collective-permute-start(bf16[3,2,4096]{2,1,0:T(2,128)(2,1)S(1)} %slice.41), channel_id=1, source_target_pairs={{0,1},{1,4},{4,5},{5,8},{8,9},{9,12},{12,13},{2,3},{3,6},{6,7},{7,... | collective-permute-start | bytes 147464 | tf_op jit(solution)/shard_map/ppermute | solution.py:18
  4.9 0.6 %copy-start.1 = (bf16[3,2,4096]{2,1,0:T(2,128)(2,1)}, bf16[3,2,4096]{2,1,0:T(2,128)(2,1)S(1)}, u32[]{:S(2)}) copy-start(bf16[3,2,4096]{2,1,0:T(2,128)(2,1)S(1)} %collective-permute-done.halo_ref) | copy-start | bytes 147460
  12.4 4.4 %collective-permute-start.1 = (f32[16,4096]{1,0:T(8,128)}, f32[16,4096]{1,0:T(8,128)S(1)}, u32[]{:S(2)}, u32[]{:S(2)}) collective-permute-start(f32[16,4096]{1,0:T(8,128)} %get-tuple-element.4), channel_id=1, source_target_pairs={{0,1},{1,0},{2,3},{3,2},{4,5},{5,4},{6,7},{7,6},{8,9},{9,8},{10,11... | collective-permute-start | bytes 786440 | tf_op jit(solution)/shard_map/ppermute | solution.py:142
  35.0 1.6 %collective-permute-start.2 = (f32[32,2048]{1,0:T(8,128)S(1)}, f32[32,2048]{1,0:T(8,128)S(1)}, u32[]{:S(2)}, u32[]{:S(2)}) collective-permute-start(f32[32,2048]{1,0:T(8,128)S(1)} %pad_maximum_fusion.1), channel_id=1, source_target_pairs={{0,1},{1,0},{2,3},{3,2},{4,5},{5,4},{6,7},{7,6},{8,9},{9,8},{10,11... | collective-permute-start | bytes 786440 | tf_op jit(solution)/shard_map/ppermute | solution.py:142

commit v11 on v10

--- a/solution.py
+++ b/solution.py
@@ -81,23 +81,28 @@
     out_ref[:, pl.ds(start, block)] = _scan_rows(drive_ref, decay, None, state, None)
 
 
-def _mix_kernel(x_ref, halo_ref, filt_ref, rate_ref, res_ref, skip_ref, init_ref, fin_in_ref, drive_ref,
-                out_ref, fin_ref, conv_scr):
-    block = rate_ref.shape[1]
-    start = pl.multiple_of(pl.program_id(0) * block, block)
-    fin_ref[...] = fin_in_ref[:, pl.ds(start, block)]
+def _mix_kernel(x_ref, halo_ref, filt_ref, rate_ref, res_ref, skip_ref, own_ref, partner_ref, other_ref,
+                decay_ref, flag_ref, drive_ref, out_ref, fin_ref, conv_scr):
+    modes = rate_ref.shape[0]
+    first = flag_ref[0:1, 0:1] > 0.5
+    in_low = pl.program_id(0) < pl.num_programs(0) // 2
+    from_own = jnp.logical_not(jnp.logical_xor(first, in_low))
+    halves = jnp.where(from_own, own_ref[...], partner_ref[...])
+    entering = halves[:modes]
+    fin_ref[...] = halves[modes:]
+    init = jnp.where(first, entering, decay_ref[...] * entering + other_ref[...])
     decay = jnp.exp(-rate_ref[...])
-    _scan_rows(drive_ref, decay, res_ref[...], init_ref[:, pl.ds(start, block)], conv_scr)
+    _scan_rows(drive_ref, decay, res_ref[...], init, conv_scr)
     q = _featurize_one(x_ref, halo_ref, filt_ref, 0)
     out_ref[...] = (q * (conv_scr[...] + skip_ref[...] * drive_ref[...])).astype(out_ref.dtype)
 
 
-def _specs(row_count, modes, taps, features=3):
-    x_spec = pl.BlockSpec((features, row_count, CHAN_BLOCK), lambda j: (0, 0, j))
-    halo_spec = pl.BlockSpec((features, taps - 1, CHAN_BLOCK), lambda j: (0, 0, j))
-    filt_spec = pl.BlockSpec((features, taps, CHAN_BLOCK), lambda j: (0, 0, j))
-    mode_spec = pl.BlockSpec((modes, CHAN_BLOCK), lambda j: (0, j))
-    row_spec = pl.BlockSpec((1, CHAN_BLOCK), lambda j: (0, j))
+def _specs(row_count, modes, taps, features=3, block=CHAN_BLOCK):
+    x_spec = pl.BlockSpec((features, row_count, block), lambda j: (0, 0, j))
+    halo_spec = pl.BlockSpec((features, taps - 1, block), lambda j: (0, 0, j))
+    filt_spec = pl.BlockSpec((features, taps, block), lambda j: (0, 0, j))
+    mode_spec = pl.BlockSpec((modes, block), lambda j: (0, j))
+    row_spec = pl.BlockSpec((1, block), lambda j: (0, j))
     return x_spec, halo_spec, filt_spec, mode_spec, row_spec
 
 
@@ -118,24 +123,30 @@
     )(projected, halo, short_filters, decay_rate)
 
 
-def mix(projected, halo, short_filters, decay_rate, residue, skip, prefix, final_state, drive):
+def mix(projected, halo, short_filters, decay_rate, residue, skip, own, partner, other, shard_decay,
+        flag, drive):
     _, row_count, chan_count = projected.shape
     modes = decay_rate.shape[0]
     taps = short_filters.shape[1]
-    x_spec, halo_spec, filt_spec, mode_spec, row_spec = _specs(row_count, modes, taps, 1)
-    tile_spec = pl.BlockSpec((row_count, CHAN_BLOCK), lambda j: (0, j))
-    whole = pl.BlockSpec(memory_space=pltpu.VMEM)
+    block = min(CHAN_BLOCK, chan_count // 2)
+    x_spec, halo_spec, filt_spec, mode_spec, row_spec = _specs(row_count, modes, taps, 1, block)
+    tile_spec = pl.BlockSpec((row_count, block), lambda j: (0, j))
+    per_half = chan_count // 2 // block
+    half_spec = pl.BlockSpec((2 * modes, block), lambda j: (0, j % per_half))
+    flag_spec = pl.BlockSpec(flag.shape, lambda j: (0, 0))
     return pl.pallas_call(
         _mix_kernel,
-        grid=(chan_count // CHAN_BLOCK,),
-        in_specs=[x_spec, halo_spec, filt_spec, mode_spec, mode_spec, row_spec, whole, whole, tile_spec],
+        grid=(chan_count // block,),
+        in_specs=[x_spec, halo_spec, filt_spec, mode_spec, mode_spec, row_spec, half_spec, half_spec,
+                  mode_spec, mode_spec, flag_spec, tile_spec],
         out_specs=[tile_spec, mode_spec],
         out_shape=[
             jax.ShapeDtypeStruct((row_count, chan_count), jnp.bfloat16),
             jax.ShapeDtypeStruct((modes, chan_count), jnp.float32),
         ],
-        scratch_shapes=[pltpu.VMEM((row_count, CHAN_BLOCK), jnp.float32)],
-    )(projected, halo, short_filters, decay_rate, residue, skip[None, :], prefix, final_state, drive)
+        scratch_shapes=[pltpu.VMEM((row_count, block), jnp.float32)],
+    )(projected, halo, short_filters, decay_rate, residue, skip[None, :], own, partner, other,
+      shard_decay, flag, drive)
 
 
 def swap_cores(value):
@@ -173,14 +184,9 @@
         running = chip_decay * running + received[chip]
     both = jnp.concatenate([entering, running], axis=0)
     other_both = swap_cores(both)
-    low = jnp.where(first, both, other_both)
-    high = jnp.where(first, other_both, both)
-    whole = jnp.concatenate([low, high], axis=1)
-    chip_entering = whole[:modes]
-    final_state = whole[modes:]
-    prefix = jnp.where(first, chip_entering, shard_decay * chip_entering + other)
-    mixed, final_state = mix(projected, halo, short_filters, decay_rate, residue, skip, prefix,
-                             final_state, drive)
+    flag = jnp.where(first, jnp.ones((8, 128), jnp.float32), jnp.zeros((8, 128), jnp.float32))
+    mixed, final_state = mix(projected, halo, short_filters, decay_rate, residue, skip, both,
+                             other_both, other, shard_decay, flag, drive)
     return (mixed, final_state)
 
 

time: 48.5 us -> 48.8 us (level)
  other arithmetic: 2.05 us -> 1.24 us
  local copies, waits for them, and re-layouts: 1.64 us -> 2.35 us
    concatenate x1 -> x0, other arithmetic: 0.87 us -> none  [local(): whole = jnp.concatenate([low, high], axis=1)]
    select_n x0 -> x1, local copies, waits for them, and re-layouts: none -> 0.6 us  [local(): jnp.where(first, jnp.ones((8, 128), jnp.float32), jnp.zeros((8, 128), jnp...]
where the time goes in v11:
time: 48.8 us; the launch traced here: 48.5 us
  Pallas kernels  17.9 us (37%)
  blocking collectives  17.2 us (35%)
  starting transfers between devices  5.41 us (11%)
  waiting for transfers between devices  3.68 us (8%)
  local copies, waits for them, and re-layouts  2.35 us (5%)
  other arithmetic  1.24 us (3%)
  between operations  0.72 us (1%)
    all_gather x1, blocking collectives, local(): received = lax.all_gather(chip_part, 'ctx', axis=0, tiled=False)  17.2 us
    pallas_call x1, Pallas kernels, mix(): pl.pallas_call(_mix_kernel, grid=(chan_count // block,), in_specs=[x_spec...  11 us
    pallas_call x1, Pallas kernels, contributions(): pl.pallas_call(_contrib_kernel, grid=(chan_count // CHAN_BLOCK,), in_spec...  6.84 us
    ppermute x2, starting transfers between devices, swap_cores(): return lax.ppermute(value, 'dec', [(0, 1), (1, 0)])  3.05 us
    ppermute x2, waiting for transfers between devices, swap_cores(): return lax.ppermute(value, 'dec', [(0, 1), (1, 0)])  2.82 us
    ppermute x1, starting transfers between devices, from_behind(): lax.ppermute(value, axis, [(source, source + steps) for source in range(i...  2.36 us
    select_n x1, other arithmetic, local(): jnp.where(first, lo(shard_decay) * lo(contribution) + lo(other), hi(shard...  1.1 us
    slice x1, local copies, waits for them, and re-layouts, local(): edge_rows = projected[:, row_count - (tap_count - 1):, :]  1.02 us
  transfers between devices with their start and end apart: 3, of which 3 were waited for; matrix products, arithmetic and copies ran while one was open for 0% of the time, Pallas kernels for 0%

profile of v11, /device:TPU:0, one launch (start us, length us, event | category | flops | bytes accessed | tf_op | source)
XLA Modules:
  0.0 48.5 jit_solution(9217750618368003663)
XLA Ops:
  0.6 0.0 copy-start.1
  0.6 1.0 %slice.35 = bf16[3,2,4096]{2,1,0:T(2,128)(2,1)S(1)} slice(bf16[3,128,4096]{2,1,0:T(8,128)(2,1)} %x_ref.3), slice={[0:3], [126:128], [0:4096]} | slice | bytes 98304 | tf_op jit(solution)/shard_map/slice | solution.py:161
  1.7 2.4 %collective-permute-start = (bf16[3,2,4096]{2,1,0:T(2,128)(2,1)S(1)}, bf16[3,2,4096]{2,1,0:T(2,128)(2,1)S(1)}, u32[]{:S(2)}, u32[]{:S(2)}) collective-permute-start(bf16[3,2,4096]{2,1,0:T(2,128)(2,1)S(1)} %slice.35), channel_id=1, source_target_pairs={{0,1},{1,4},{4,5},{5,8},{8,9},{9,12},{12,13},{2,3},{3,6},{6,7},{7,... | collective-permute-start | bytes 147464 | tf_op jit(solution)/shard_map/ppermute | solution.py:18
  4.0 0.9 %collective-permute-done.halo_ref = bf16[3,2,4096]{2,1,0:T(2,128)(2,1)S(1)} collective-permute-done((bf16[3,2,4096]{2,1,0:T(2,128)(2,1)S(1)}, bf16[3,2,4096]{2,1,0:T(2,128)(2,1)S(1)}, u32[]{:S(2)}, u32[]{:S(2)}) %collective-permute-start) | collective-permute-done | bytes 49184 | tf_op jit(solution)/shard_map/ppermute | solution.py:18
  4.9 0.0 copy-start.5
  4.9 0.6 %copy-done.5 = bf16[3,2,4096]{2,1,0:T(2,128)(2,1)} copy-done((bf16[3,2,4096]{2,1,0:T(2,128)(2,1)}, bf16[3,2,4096]{2,1,0:T(2,128)(2,1)S(1)}, u32[]{:S(2)}) %copy-start.5) | copy-done | bytes 49176
  5.5 6.8 %shard_map.68 = (f32[16,4096]{1,0:T(8,128)}, f32[128,4096]{1,0:T(8,128)}) custom-call(bf16[3,128,4096]{2,1,0:T(8,128)(2,1)} %x_ref.3, bf16[3,2,4096]{2,1,0:T(2,128)(2,1)} %copy-done.5, f32[3,3,4096]{2,1,0:T(4,128)} %filt_ref.3, f32[16,4096]{1,0:T(8,128)} %rate_ref.3), custom_call_target="tpu_custom_call" | custom-call | tf_op jit(solution)/shard_map/pallas_call | solution.py:114
  12.4 3.0 %collective-permute-start.1 = (f32[16,4096]{1,0:T(8,128)}, f32[16,4096]{1,0:T(8,128)S(1)}, u32[]{:S(2)}, u32[]{:S(2)}) collective-permute-start(f32[16,4096]{1,0:T(8,128)} %get-tuple-element.4), channel_id=1, source_target_pairs={{0,1},{1,0},{2,3},{3,2},{4,5},{5,4},{6,7},{7,6},{8,9},{9,8},{10,11... | collective-permute-start | bytes 786440 | tf_op jit(solution)/shard_map/ppermute | solution.py:153
  15.3 0.0 copy-done.1
  15.4 0.0 copy-start
  15.4 1.3 %collective-permute-done.1.other_ref = f32[16,4096]{1,0:T(8,128)S(1)} collective-permute-done((f32[16,4096]{1,0:T(8,128)}, f32[16,4096]{1,0:T(8,128)S(1)}, u32[]{:S(2)}, u32[]{:S(2)}) %collective-permute-start.1) | collective-permute-done | bytes 262176 | tf_op jit(solution)/shard_map/ppermute | solution.py:153
  16.7 0.0 copy-start.2
  16.7 1.1 %fusion.1 = f32[16,2048]{1,0:T(8,128)S(1)} fusion(f32[16,4096]{1,0:T(8,128)S(1)} %collective-permute-done.1.other_ref, f32[16,4096]{1,0:T(8,128)} %get-tuple-element.4, f32[16,4096]{1,0:T(8,128)S(1)} %multiply_exponential_fusion.decay_ref, pred[]{:T(512)S(6)} %eq.14), kind=kLoop, calls=%fused_computation.8 | loop fusion | flops 163840 | bytes 917505 | tf_op jit(solution)/shard_map/jit(_where)/select_n | solution.py:171
  17.8 17.2 %all-gather = f32[64,2048]{1,0:T(8,128)S(1)} all-gather(f32[16,2048]{1,0:T(8,128)S(1)} %fusion.1), channel_id=2, replica_groups=mesh['grp'=2,'ctx'=4,'chan'=2,'dec'=2] {'ctx'}, dimensions={0}, use_global_device_ids=true | all-gather | bytes 655360 | tf_op jit(solution)/shard_map/all_gather | solution.py:177
  35.0 0.1 select_select_fusion
  35.1 0.0 copy-start.3
  35.1 0.1 collective-permute-start.2
  35.2 1.5 %collective-permute-done.2.partner_ref = f32[32,2048]{1,0:T(8,128)S(1)} collective-permute-done((f32[32,2048]{1,0:T(8,128)S(1)}, f32[32,2048]{1,0:T(8,128)S(1)}, u32[]{:S(2)}, u32[]{:S(2)}) %collective-permute-start.2) | collective-permute-done | bytes 262176 | tf_op jit(solution)/shard_map/ppermute | solution.py:153
  36.7 0.0 copy-start.4
  36.7 0.6 %select_n.51.flag_ref = f32[8,128]{1,0:T(8,128)} broadcast(f32[]{:T(128)S(6)} %select_n.50), dimensions={} | broadcast | bytes 4100 | tf_op jit(solution)/shard_map/jit(_where)/select_n | solution.py:187
  37.3 0.0 copy-done
  37.3 0.0 copy-done.2
  37.3 0.0 copy-done.3
  37.3 0.1 copy-done.4
  37.4 11.0 %shard_map.69 = (bf16[128,4096]{1,0:T(8,128)(2,1)}, f32[16,4096]{1,0:T(8,128)}) custom-call(bf16[3,128,4096]{2,1,0:T(8,128)(2,1)} %x_ref.3, bf16[3,2,4096]{2,1,0:T(2,128)(2,1)} %copy-done.5, f32[3,3,4096]{2,1,0:T(4,128)} %filt_ref.3, f32[16,4096]{1,0:T(8,128)} %rate_ref.3, f32[16,4096]{1,0:T(8,128)} %res_ref.1, f32[1,4096]{1,0:T(1,128)} %bitcast.1, ...), custom_call_target="tpu_custom_call" | custom-call | tf_op jit(solution)/shard_map/pallas_call | solution.py:137
  (2 shorter events, 0.1 us)
Async XLA Ops:
  0.6 14.7 %copy-start.1 = (f32[16,4096]{1,0:T(8,128)S(1)}, f32[16,4096]{1,0:T(8,128)}, u32[]{:S(2)}) copy-start(f32[16,4096]{1,0:T(8,128)} %rate_ref.3) | copy-start | bytes 786436
  1.7 3.2 %collective-permute-start = (bf16[3,2,4096]{2,1,0:T(2,128)(2,1)S(1)}, bf16[3,2,4096]{2,1,0:T(2,128)(2,1)S(1)}, u32[]{:S(2)}, u32[]{:S(2)}) collective-permute-start(bf16[3,2,4096]{2,1,0:T(2,128)(2,1)S(1)} %slice.35), channel_id=1, source_target_pairs={{0,1},{1,4},{4,5},{5,8},{8,9},{9,12},{12,13},{2,3},{3,6},{6,7},{7,... | collective-permute-start | bytes 147464 | tf_op jit(solution)/shard_map/ppermute | solution.py:18
  4.9 0.6 %copy-start.5 = (bf16[3,2,4096]{2,1,0:T(2,128)(2,1)}, bf16[3,2,4096]{2,1,0:T(2,128)(2,1)S(1)}, u32[]{:S(2)}) copy-start(bf16[3,2,4096]{2,1,0:T(2,128)(2,1)S(1)} %collective-permute-done.halo_ref) | copy-start | bytes 147460
  12.4 4.4 %collective-permute-start.1 = (f32[16,4096]{1,0:T(8,128)}, f32[16,4096]{1,0:T(8,128)S(1)}, u32[]{:S(2)}, u32[]{:S(2)}) collective-permute-start(f32[16,4096]{1,0:T(8,128)} %get-tuple-element.4), channel_id=1, source_target_pairs={{0,1},{1,0},{2,3},{3,2},{4,5},{5,4},{6,7},{7,6},{8,9},{9,8},{10,11... | collective-permute-start | bytes 786440 | tf_op jit(solution)/shard_map/ppermute | solution.py:153
  15.4 21.9 %copy-start = (f32[16,4096]{1,0:T(8,128)}, f32[16,4096]{1,0:T(8,128)S(1)}, u32[]{:S(2)}) copy-start(f32[16,4096]{1,0:T(8,128)S(1)} %multiply_exponential_fusion.decay_ref) | copy-start | bytes 786436
  16.7 20.6 %copy-start.2 = (f32[16,4096]{1,0:T(8,128)}, f32[16,4096]{1,0:T(8,128)S(1)}, u32[]{:S(2)}) copy-start(f32[16,4096]{1,0:T(8,128)S(1)} %collective-permute-done.1.other_ref) | copy-start | bytes 786436
  35.1 2.2 %copy-start.3 = (f32[32,2048]{1,0:T(8,128)}, f32[32,2048]{1,0:T(8,128)S(1)}, u32[]{:S(2)}) copy-start(f32[32,2048]{1,0:T(8,128)S(1)} %pad_maximum_fusion.own_ref) | copy-start | bytes 786436
  35.1 1.6 %collective-permute-start.2 = (f32[32,2048]{1,0:T(8,128)S(1)}, f32[32,2048]{1,0:T(8,128)S(1)}, u32[]{:S(2)}, u32[]{:S(2)}) collective-permute-start(f32[32,2048]{1,0:T(8,128)S(1)} %pad_maximum_fusion.own_ref), channel_id=1, source_target_pairs={{0,1},{1,0},{2,3},{3,2},{4,5},{5,4},{6,7},{7,6},{8,9},{9,8},{10,11... | collective-permute-start | bytes 786440 | tf_op jit(solution)/shard_map/ppermute | solution.py:153
  36.7 0.7 %copy-start.4 = (f32[32,2048]{1,0:T(8,128)}, f32[32,2048]{1,0:T(8,128)S(1)}, u32[]{:S(2)}) copy-start(f32[32,2048]{1,0:T(8,128)S(1)} %collective-permute-done.2.partner_ref) | copy-start | bytes 786436

commit v12 on v11

--- a/solution.py
+++ b/solution.py
@@ -82,9 +82,9 @@
 
 
 def _mix_kernel(x_ref, halo_ref, filt_ref, rate_ref, res_ref, skip_ref, own_ref, partner_ref, other_ref,
-                decay_ref, flag_ref, drive_ref, out_ref, fin_ref, conv_scr):
+                decay_ref, drive_ref, out_ref, fin_ref, conv_scr):
     modes = rate_ref.shape[0]
-    first = flag_ref[0:1, 0:1] > 0.5
+    first = lax.axis_index("dec") == 0
     in_low = pl.program_id(0) < pl.num_programs(0) // 2
     from_own = jnp.logical_not(jnp.logical_xor(first, in_low))
     halves = jnp.where(from_own, own_ref[...], partner_ref[...])
@@ -124,7 +124,7 @@
 
 
 def mix(projected, halo, short_filters, decay_rate, residue, skip, own, partner, other, shard_decay,
-        flag, drive):
+        drive):
     _, row_count, chan_count = projected.shape
     modes = decay_rate.shape[0]
     taps = short_filters.shape[1]
@@ -133,12 +133,11 @@
     tile_spec = pl.BlockSpec((row_count, block), lambda j: (0, j))
     per_half = chan_count // 2 // block
     half_spec = pl.BlockSpec((2 * modes, block), lambda j: (0, j % per_half))
-    flag_spec = pl.BlockSpec(flag.shape, lambda j: (0, 0))
     return pl.pallas_call(
         _mix_kernel,
         grid=(chan_count // block,),
         in_specs=[x_spec, halo_spec, filt_spec, mode_spec, mode_spec, row_spec, half_spec, half_spec,
-                  mode_spec, mode_spec, flag_spec, tile_spec],
+                  mode_spec, mode_spec, tile_spec],
         out_specs=[tile_spec, mode_spec],
         out_shape=[
             jax.ShapeDtypeStruct((row_count, chan_count), jnp.bfloat16),
@@ -146,7 +145,7 @@
         ],
         scratch_shapes=[pltpu.VMEM((row_count, block), jnp.float32)],
     )(projected, halo, short_filters, decay_rate, residue, skip[None, :], own, partner, other,
-      shard_decay, flag, drive)
+      shard_decay, drive)
 
 
 def swap_cores(value):
@@ -184,9 +183,8 @@
         running = chip_decay * running + received[chip]
     both = jnp.concatenate([entering, running], axis=0)
     other_both = swap_cores(both)
-    flag = jnp.where(first, jnp.ones((8, 128), jnp.float32), jnp.zeros((8, 128), jnp.float32))
     mixed, final_state = mix(projected, halo, short_filters, decay_rate, residue, skip, both,
-                             other_both, other, shard_decay, flag, drive)
+                             other_both, other, shard_decay, drive)
     return (mixed, final_state)
 
 

time: 48.8 us -> 48.5 us (level)
    select_n x1 -> x0, local copies, waits for them, and re-layouts: 0.6 us -> none  [local(): jnp.where(first, jnp.ones((8, 128), jnp.float32), jnp.zeros((8, 128), jnp...]
    unnamed x12, local copies, waits for them, and re-layouts: 0.73 us -> 1.33 us
where the time goes in v12:
time: 48.5 us; the launch traced here: 48.2 us
  Pallas kernels  17.6 us (36%)
  blocking collectives  17.2 us (35%)
  starting transfers between devices  5.41 us (11%)
  waiting for transfers between devices  3.68 us (8%)
  local copies, waits for them, and re-layouts  2.35 us (5%)
  other arithmetic  1.24 us (3%)
  between operations  0.71 us (1%)
    all_gather x1, blocking collectives, local(): received = lax.all_gather(chip_part, 'ctx', axis=0, tiled=False)  17.2 us
    pallas_call x1, Pallas kernels, mix(): pl.pallas_call(_mix_kernel, grid=(chan_count // block,), in_specs=[x_spec...  10.8 us
    pallas_call x1, Pallas kernels, contributions(): pl.pallas_call(_contrib_kernel, grid=(chan_count // CHAN_BLOCK,), in_spec...  6.84 us
    ppermute x2, starting transfers between devices, swap_cores(): return lax.ppermute(value, 'dec', [(0, 1), (1, 0)])  3.05 us
    ppermute x2, waiting for transfers between devices, swap_cores(): return lax.ppermute(value, 'dec', [(0, 1), (1, 0)])  2.82 us
    ppermute x1, starting transfers between devices, from_behind(): lax.ppermute(value, axis, [(source, source + steps) for source in range(i...  2.36 us
    unnamed x12, local copies, waits for them, and re-layouts  1.33 us
    select_n x1, other arithmetic, local(): jnp.where(first, lo(shard_decay) * lo(contribution) + lo(other), hi(shard...  1.1 us
  transfers between devices with their start and end apart: 3, of which 3 were waited for; matrix products, arithmetic and copies ran while one was open for 0% of the time, Pallas kernels for 0%

profile of v12, /device:TPU:0, one launch (start us, length us, event | category | flops | bytes accessed | tf_op | source)
XLA Modules:
  0.0 48.2 jit_solution(13059939210313459070)
XLA Ops:
  0.6 0.0 copy-start.1
  0.6 1.0 %slice.35 = bf16[3,2,4096]{2,1,0:T(2,128)(2,1)S(1)} slice(bf16[3,128,4096]{2,1,0:T(8,128)(2,1)} %x_ref.3), slice={[0:3], [126:128], [0:4096]} | slice | bytes 98304 | tf_op jit(solution)/shard_map/slice | solution.py:160
  1.7 2.4 %collective-permute-start = (bf16[3,2,4096]{2,1,0:T(2,128)(2,1)S(1)}, bf16[3,2,4096]{2,1,0:T(2,128)(2,1)S(1)}, u32[]{:S(2)}, u32[]{:S(2)}) collective-permute-start(bf16[3,2,4096]{2,1,0:T(2,128)(2,1)S(1)} %slice.35), channel_id=1, source_target_pairs={{0,1},{1,4},{4,5},{5,8},{8,9},{9,12},{12,13},{2,3},{3,6},{6,7},{7,... | collective-permute-start | bytes 147464 | tf_op jit(solution)/shard_map/ppermute | solution.py:18
  4.0 0.9 %collective-permute-done.halo_ref = bf16[3,2,4096]{2,1,0:T(2,128)(2,1)S(1)} collective-permute-done((bf16[3,2,4096]{2,1,0:T(2,128)(2,1)S(1)}, bf16[3,2,4096]{2,1,0:T(2,128)(2,1)S(1)}, u32[]{:S(2)}, u32[]{:S(2)}) %collective-permute-start) | collective-permute-done | bytes 49184 | tf_op jit(solution)/shard_map/ppermute | solution.py:18
  4.9 0.0 copy-start.5
  4.9 0.6 %copy-done.5 = bf16[3,2,4096]{2,1,0:T(2,128)(2,1)} copy-done((bf16[3,2,4096]{2,1,0:T(2,128)(2,1)}, bf16[3,2,4096]{2,1,0:T(2,128)(2,1)S(1)}, u32[]{:S(2)}) %copy-start.5) | copy-done | bytes 49176
  5.5 6.8 %shard_map.68 = (f32[16,4096]{1,0:T(8,128)}, f32[128,4096]{1,0:T(8,128)}) custom-call(bf16[3,128,4096]{2,1,0:T(8,128)(2,1)} %x_ref.3, bf16[3,2,4096]{2,1,0:T(2,128)(2,1)} %copy-done.5, f32[3,3,4096]{2,1,0:T(4,128)} %filt_ref.3, f32[16,4096]{1,0:T(8,128)} %rate_ref.3), custom_call_target="tpu_custom_call" | custom-call | tf_op jit(solution)/shard_map/pallas_call | solution.py:114
  12.4 3.0 %collective-permute-start.1 = (f32[16,4096]{1,0:T(8,128)}, f32[16,4096]{1,0:T(8,128)S(1)}, u32[]{:S(2)}, u32[]{:S(2)}) collective-permute-start(f32[16,4096]{1,0:T(8,128)} %get-tuple-element.4), channel_id=1, source_target_pairs={{0,1},{1,0},{2,3},{3,2},{4,5},{5,4},{6,7},{7,6},{8,9},{9,8},{10,11... | collective-permute-start | bytes 786440 | tf_op jit(solution)/shard_map/ppermute | solution.py:152
  15.3 0.0 copy-done.1
  15.4 0.0 copy-start
  15.4 1.3 %collective-permute-done.1.other_ref = f32[16,4096]{1,0:T(8,128)S(1)} collective-permute-done((f32[16,4096]{1,0:T(8,128)}, f32[16,4096]{1,0:T(8,128)S(1)}, u32[]{:S(2)}, u32[]{:S(2)}) %collective-permute-start.1) | collective-permute-done | bytes 262176 | tf_op jit(solution)/shard_map/ppermute | solution.py:152
  16.7 0.0 copy-start.2
  16.7 1.1 %fusion.1 = f32[16,2048]{1,0:T(8,128)S(1)} fusion(f32[16,4096]{1,0:T(8,128)S(1)} %collective-permute-done.1.other_ref, f32[16,4096]{1,0:T(8,128)} %get-tuple-element.4, f32[16,4096]{1,0:T(8,128)S(1)} %multiply_exponential_fusion.decay_ref, pred[]{:T(512)S(6)} %eq.14), kind=kLoop, calls=%fused_computation.8 | loop fusion | flops 163840 | bytes 917505 | tf_op jit(solution)/shard_map/jit(_where)/select_n | solution.py:170
  17.8 17.2 %all-gather = f32[64,2048]{1,0:T(8,128)S(1)} all-gather(f32[16,2048]{1,0:T(8,128)S(1)} %fusion.1), channel_id=2, replica_groups=mesh['grp'=2,'ctx'=4,'chan'=2,'dec'=2] {'ctx'}, dimensions={0}, use_global_device_ids=true | all-gather | bytes 655360 | tf_op jit(solution)/shard_map/all_gather | solution.py:176
  35.0 0.1 select_select_fusion
  35.1 0.0 copy-start.3
  35.1 0.1 collective-permute-start.2
  35.2 1.5 %collective-permute-done.2.partner_ref = f32[32,2048]{1,0:T(8,128)S(1)} collective-permute-done((f32[32,2048]{1,0:T(8,128)S(1)}, f32[32,2048]{1,0:T(8,128)S(1)}, u32[]{:S(2)}, u32[]{:S(2)}) %collective-permute-start.2) | collective-permute-done | bytes 262176 | tf_op jit(solution)/shard_map/ppermute | solution.py:152
  36.7 0.0 copy-start.4
  36.7 0.0 copy-done
  36.7 0.0 copy-done.2
  36.7 0.0 copy-done.3
  36.7 0.7 %copy-done.4 = f32[32,2048]{1,0:T(8,128)} copy-done((f32[32,2048]{1,0:T(8,128)}, f32[32,2048]{1,0:T(8,128)S(1)}, u32[]{:S(2)}) %copy-start.4) | copy-done | bytes 262168
  37.4 10.8 %shard_map.69 = (bf16[128,4096]{1,0:T(8,128)(2,1)}, f32[16,4096]{1,0:T(8,128)}) custom-call(bf16[3,128,4096]{2,1,0:T(8,128)(2,1)} %x_ref.3, bf16[3,2,4096]{2,1,0:T(2,128)(2,1)} %copy-done.5, f32[3,3,4096]{2,1,0:T(4,128)} %filt_ref.3, f32[16,4096]{1,0:T(8,128)} %rate_ref.3, f32[16,4096]{1,0:T(8,128)} %res_ref.1, f32[1,4096]{1,0:T(1,128)} %bitcast.1, ...), custom_call_target="tpu_custom_call" | custom-call | tf_op jit(solution)/shard_map/pallas_call | solution.py:136
  (2 shorter events, 0.1 us)
Async XLA Ops:
  0.6 14.7 %copy-start.1 = (f32[16,4096]{1,0:T(8,128)S(1)}, f32[16,4096]{1,0:T(8,128)}, u32[]{:S(2)}) copy-start(f32[16,4096]{1,0:T(8,128)} %rate_ref.3) | copy-start | bytes 786436
  1.7 3.2 %collective-permute-start = (bf16[3,2,4096]{2,1,0:T(2,128)(2,1)S(1)}, bf16[3,2,4096]{2,1,0:T(2,128)(2,1)S(1)}, u32[]{:S(2)}, u32[]{:S(2)}) collective-permute-start(bf16[3,2,4096]{2,1,0:T(2,128)(2,1)S(1)} %slice.35), channel_id=1, source_target_pairs={{0,1},{1,4},{4,5},{5,8},{8,9},{9,12},{12,13},{2,3},{3,6},{6,7},{7,... | collective-permute-start | bytes 147464 | tf_op jit(solution)/shard_map/ppermute | solution.py:18
  4.9 0.6 %copy-start.5 = (bf16[3,2,4096]{2,1,0:T(2,128)(2,1)}, bf16[3,2,4096]{2,1,0:T(2,128)(2,1)S(1)}, u32[]{:S(2)}) copy-start(bf16[3,2,4096]{2,1,0:T(2,128)(2,1)S(1)} %collective-permute-done.halo_ref) | copy-start | bytes 147460
  12.4 4.4 %collective-permute-start.1 = (f32[16,4096]{1,0:T(8,128)}, f32[16,4096]{1,0:T(8,128)S(1)}, u32[]{:S(2)}, u32[]{:S(2)}) collective-permute-start(f32[16,4096]{1,0:T(8,128)} %get-tuple-element.4), channel_id=1, source_target_pairs={{0,1},{1,0},{2,3},{3,2},{4,5},{5,4},{6,7},{7,6},{8,9},{9,8},{10,11... | collective-permute-start | bytes 786440 | tf_op jit(solution)/shard_map/ppermute | solution.py:152
  15.4 21.3 %copy-start = (f32[16,4096]{1,0:T(8,128)}, f32[16,4096]{1,0:T(8,128)S(1)}, u32[]{:S(2)}) copy-start(f32[16,4096]{1,0:T(8,128)S(1)} %multiply_exponential_fusion.decay_ref) | copy-start | bytes 786436
  16.7 20.0 %copy-start.2 = (f32[16,4096]{1,0:T(8,128)}, f32[16,4096]{1,0:T(8,128)S(1)}, u32[]{:S(2)}) copy-start(f32[16,4096]{1,0:T(8,128)S(1)} %collective-permute-done.1.other_ref) | copy-start | bytes 786436
  35.1 1.6 %copy-start.3 = (f32[32,2048]{1,0:T(8,128)}, f32[32,2048]{1,0:T(8,128)S(1)}, u32[]{:S(2)}) copy-start(f32[32,2048]{1,0:T(8,128)S(1)} %pad_maximum_fusion.own_ref) | copy-start | bytes 786436
  35.1 1.6 %collective-permute-start.2 = (f32[32,2048]{1,0:T(8,128)S(1)}, f32[32,2048]{1,0:T(8,128)S(1)}, u32[]{:S(2)}, u32[]{:S(2)}) collective-permute-start(f32[32,2048]{1,0:T(8,128)S(1)} %pad_maximum_fusion.own_ref), channel_id=1, source_target_pairs={{0,1},{1,0},{2,3},{3,2},{4,5},{5,4},{6,7},{7,6},{8,9},{9,8},{10,11... | collective-permute-start | bytes 786440 | tf_op jit(solution)/shard_map/ppermute | solution.py:152
  36.7 0.7 %copy-start.4 = (f32[32,2048]{1,0:T(8,128)}, f32[32,2048]{1,0:T(8,128)S(1)}, u32[]{:S(2)}) copy-start(f32[32,2048]{1,0:T(8,128)S(1)} %collective-permute-done.2.partner_ref) | copy-start | bytes 786436

commit v13 on v10

--- a/solution.py
+++ b/solution.py
@@ -136,6 +136,23 @@
         ],
         scratch_shapes=[pltpu.VMEM((row_count, CHAN_BLOCK), jnp.float32)],
     )(projected, halo, short_filters, decay_rate, residue, skip[None, :], prefix, final_state, drive)
+
+
+def gather_chips(part, chip_here):
+    chips = lax.axis_size("ctx")
+    held = part[None]
+    span = 1
+    while span < chips:
+        pairs = [(i, i ^ span) for i in range(chips)]
+        arrived = lax.ppermute(held, "ctx", pairs)
+        upper = (chip_here // span) % 2 == 1
+        held = jnp.where(
+            upper,
+            jnp.concatenate([arrived, held], axis=0),
+            jnp.concatenate([held, arrived], axis=0),
+        )
+        span *= 2
+    return held
 
 
 def swap_cores(value):
@@ -163,8 +180,8 @@
         hi(shard_decay) * hi(other) + hi(contribution),
     )
     half_decay = jnp.where(first, lo(shard_decay), hi(shard_decay))
-    received = lax.all_gather(chip_part, "ctx", axis=0, tiled=False)
     chip_here = lax.axis_index("ctx")
+    received = gather_chips(chip_part, chip_here)
     chip_decay = half_decay * half_decay
     running = jnp.zeros_like(chip_part)
     entering = jnp.zeros_like(chip_part)

time: 48.5 us -> 52.2 us (1.076)
  blocking collectives: 17.2 us -> 0 us
  waiting for transfers between devices: 3.69 us -> 19.1 us
  starting transfers between devices: 5.41 us -> 10.9 us
    all_gather x1 -> x0, blocking collectives: 17.2 us -> none  [local(): received = lax.all_gather(chip_part, 'ctx', axis=0, tiled=False)]
    ppermute x0 -> x2, waiting for transfers between devices: none -> 15.4 us  [gather_chips(): arrived = lax.ppermute(held, 'ctx', pairs)]
    ppermute x0 -> x2, starting transfers between devices: none -> 5.48 us  [gather_chips(): arrived = lax.ppermute(held, 'ctx', pairs)]
    broadcast_in_dim x0 -> x1, other arithmetic: none -> 1.01 us  [gather_chips(): held = part[None]]
    select_n x1 -> x2, other arithmetic: 1.01 us -> 0.06 us  [gather_chips(): jnp.where(upper, jnp.concatenate([arrived, held], axis=0), jnp.concatenat...]
  transfers between devices with their start and end apart: 3 -> 5, of which waited for: 3 -> 5; matrix products, arithmetic and copies ran while one was open for 0% -> 0% of each run, Pallas kernels for 0% -> 0%
where the time goes in v13:
time: 52.2 us; the launch traced here: 52 us
  waiting for transfers between devices  19.1 us (37%)
  Pallas kernels  17.5 us (34%)
  starting transfers between devices  10.9 us (21%)
  other arithmetic  2.09 us (4%)
  local copies, waits for them, and re-layouts  1.65 us (3%)
  between operations  0.7 us (1%)
    ppermute x2, waiting for transfers between devices, gather_chips(): arrived = lax.ppermute(held, 'ctx', pairs)  15.4 us
    pallas_call x1, Pallas kernels, mix(): pl.pallas_call(_mix_kernel, grid=(chan_count // CHAN_BLOCK,), in_specs=[x...  10.7 us
    pallas_call x1, Pallas kernels, contributions(): pl.pallas_call(_contrib_kernel, grid=(chan_count // CHAN_BLOCK,), in_spec...  6.84 us
    ppermute x2, starting transfers between devices, gather_chips(): arrived = lax.ppermute(held, 'ctx', pairs)  5.48 us
    ppermute x2, starting transfers between devices, swap_cores(): return lax.ppermute(value, 'dec', [(0, 1), (1, 0)])  3.05 us
    ppermute x2, waiting for transfers between devices, swap_cores(): return lax.ppermute(value, 'dec', [(0, 1), (1, 0)])  2.84 us
    ppermute x1, starting transfers between devices, from_behind(): lax.ppermute(value, axis, [(source, source + steps) for source in range(i...  2.36 us
  transfers between devices with their start and end apart: 5, of which 5 were waited for; matrix products, arithmetic and copies ran while one was open for 0% of the time, Pallas kernels for 0%

profile of v13, /device:TPU:0, one launch (start us, length us, event | category | flops | bytes accessed | tf_op | source)
XLA Modules:
  0.0 52.0 jit_solution(8816047684059408129)
XLA Ops:
  0.6 0.0 copy-start
  0.6 1.0 %slice.41 = bf16[3,2,4096]{2,1,0:T(2,128)(2,1)S(1)} slice(bf16[3,128,4096]{2,1,0:T(8,128)(2,1)} %x_ref.3), slice={[0:3], [126:128], [0:4096]} | slice | bytes 98304 | tf_op jit(solution)/shard_map/slice | solution.py:167
  1.7 2.4 %collective-permute-start = (bf16[3,2,4096]{2,1,0:T(2,128)(2,1)S(1)}, bf16[3,2,4096]{2,1,0:T(2,128)(2,1)S(1)}, u32[]{:S(2)}, u32[]{:S(2)}) collective-permute-start(bf16[3,2,4096]{2,1,0:T(2,128)(2,1)S(1)} %slice.41), channel_id=1, source_target_pairs={{0,1},{1,4},{4,5},{5,8},{8,9},{9,12},{12,13},{2,3},{3,6},{6,7},{7,... | collective-permute-start | bytes 147464 | tf_op jit(solution)/shard_map/ppermute | solution.py:18
  4.0 0.9 %collective-permute-done.halo_ref = bf16[3,2,4096]{2,1,0:T(2,128)(2,1)S(1)} collective-permute-done((bf16[3,2,4096]{2,1,0:T(2,128)(2,1)S(1)}, bf16[3,2,4096]{2,1,0:T(2,128)(2,1)S(1)}, u32[]{:S(2)}, u32[]{:S(2)}) %collective-permute-start) | collective-permute-done | bytes 49184 | tf_op jit(solution)/shard_map/ppermute | solution.py:18
  4.9 0.0 copy-start.1
  4.9 0.6 %copy-done.1 = bf16[3,2,4096]{2,1,0:T(2,128)(2,1)} copy-done((bf16[3,2,4096]{2,1,0:T(2,128)(2,1)}, bf16[3,2,4096]{2,1,0:T(2,128)(2,1)S(1)}, u32[]{:S(2)}) %copy-start.1) | copy-done | bytes 49176
  5.5 6.8 %shard_map.68 = (f32[16,4096]{1,0:T(8,128)}, f32[128,4096]{1,0:T(8,128)}) custom-call(bf16[3,128,4096]{2,1,0:T(8,128)(2,1)} %x_ref.3, bf16[3,2,4096]{2,1,0:T(2,128)(2,1)} %copy-done.1, f32[3,3,4096]{2,1,0:T(4,128)} %filt_ref.3, f32[16,4096]{1,0:T(8,128)} %rate_ref.3), custom_call_target="tpu_custom_call" | custom-call | tf_op jit(solution)/shard_map/pallas_call | solution.py:109
  12.4 3.0 %collective-permute-start.1 = (f32[16,4096]{1,0:T(8,128)}, f32[16,4096]{1,0:T(8,128)S(1)}, u32[]{:S(2)}, u32[]{:S(2)}) collective-permute-start(f32[16,4096]{1,0:T(8,128)} %get-tuple-element.4), channel_id=1, source_target_pairs={{0,1},{1,0},{2,3},{3,2},{4,5},{5,4},{6,7},{7,6},{8,9},{9,8},{10,11... | collective-permute-start | bytes 786440 | tf_op jit(solution)/shard_map/ppermute | solution.py:159
  15.3 0.0 copy-done
  15.4 1.3 %collective-permute-done.1 = f32[16,4096]{1,0:T(8,128)S(1)} collective-permute-done((f32[16,4096]{1,0:T(8,128)}, f32[16,4096]{1,0:T(8,128)S(1)}, u32[]{:S(2)}, u32[]{:S(2)}) %collective-permute-start.1) | collective-permute-done | bytes 262176 | tf_op jit(solution)/shard_map/ppermute | solution.py:159
  16.7 1.0 %fusion.7 = f32[1,16,2048]{2,1,0:T(8,128)S(1)} fusion(f32[16,4096]{1,0:T(8,128)S(1)} %collective-permute-done.1, f32[16,4096]{1,0:T(8,128)} %get-tuple-element.4, f32[16,4096]{1,0:T(8,128)S(1)} %multiply_exponential_fusion, pred[]{:T(512)S(6)} %eq.22), kind=kLoop, calls=%fused_computation.20 | loop fusion | flops 163840 | bytes 917505 | tf_op jit(solution)/shard_map/broadcast_in_dim | solution.py:143
  17.7 2.7 %collective-permute-start.2 = (f32[1,16,2048]{2,1,0:T(8,128)S(1)}, f32[1,16,2048]{2,1,0:T(8,128)S(1)}, u32[]{:S(2)}, u32[]{:S(2)}) collective-permute-start(f32[1,16,2048]{2,1,0:T(8,128)S(1)} %fusion.7), channel_id=1, source_target_pairs={{0,4},{4,0},{8,12},{12,8},{1,5},{5,1},{9,13},{13,9},{2,6},{6,2},{1... | collective-permute-start | bytes 393224 | tf_op jit(solution)/shard_map/ppermute | solution.py:147
  20.4 3.8 %collective-permute-done.2 = f32[1,16,2048]{2,1,0:T(8,128)S(1)} collective-permute-done((f32[1,16,2048]{2,1,0:T(8,128)S(1)}, f32[1,16,2048]{2,1,0:T(8,128)S(1)}, u32[]{:S(2)}, u32[]{:S(2)}) %collective-permute-start.2) | collective-permute-done | bytes 131104 | tf_op jit(solution)/shard_map/ppermute | solution.py:147
  24.2 2.8 %collective-permute-start.3 = (f32[2,16,2048]{2,1,0:T(8,128)S(1)}, f32[2,16,2048]{2,1,0:T(8,128)S(1)}, u32[]{:S(2)}, u32[]{:S(2)}) collective-permute-start(f32[2,16,2048]{2,1,0:T(8,128)S(1)} %maximum_select_fusion.1), channel_id=1, source_target_pairs={{0,8},{4,12},{8,0},{12,4},{1,9},{5,13},{9,1},{13,5},{2,10},{6,14},... | collective-permute-start | bytes 786440 | tf_op jit(solution)/shard_map/ppermute | solution.py:147
  27.0 11.6 %collective-permute-done.3 = f32[2,16,2048]{2,1,0:T(8,128)S(1)} collective-permute-done((f32[2,16,2048]{2,1,0:T(8,128)S(1)}, f32[2,16,2048]{2,1,0:T(8,128)S(1)}, u32[]{:S(2)}, u32[]{:S(2)}) %collective-permute-start.3) | collective-permute-done | bytes 262176 | tf_op jit(solution)/shard_map/ppermute | solution.py:147
  38.7 0.1 select_select_fusion
  38.8 0.1 collective-permute-start.4
  38.9 1.5 %collective-permute-done.4 = f32[32,2048]{1,0:T(8,128)S(1)} collective-permute-done((f32[32,2048]{1,0:T(8,128)S(1)}, f32[32,2048]{1,0:T(8,128)S(1)}, u32[]{:S(2)}, u32[]{:S(2)}) %collective-permute-start.4) | collective-permute-done | bytes 262176 | tf_op jit(solution)/shard_map/ppermute | solution.py:159
  40.4 0.9 %pad_maximum_fusion = (f32[16,4096]{1,0:T(8,128)}, f32[16,4096]{1,0:T(8,128)}) fusion(f32[32,2048]{1,0:T(8,128)S(1)} %get-tuple-element.11, f32[32,2048]{1,0:T(8,128)S(1)} %get-tuple-element.10, f32[16,4096]{1,0:T(8,128)S(1)} %collective-permute-done.1, f32[16,4096]{1,0:T(8,128)S(1)} %copy-done, pred[]{:T(512)S(6)} %eq.22), kind=kLoop, calls=%fused_computation.4 | loop fusion | flops 458752 | bytes 1572865 | tf_op jit(solution)/shard_map/concatenate | solution.py:195
  41.3 10.7 %shard_map.69 = (bf16[128,4096]{1,0:T(8,128)(2,1)}, f32[16,4096]{1,0:T(8,128)}) custom-call(bf16[3,128,4096]{2,1,0:T(8,128)(2,1)} %x_ref.3, bf16[3,2,4096]{2,1,0:T(2,128)(2,1)} %copy-done.1, f32[3,3,4096]{2,1,0:T(4,128)} %filt_ref.3, f32[16,4096]{1,0:T(8,128)} %rate_ref.3, f32[16,4096]{1,0:T(8,128)} %res_ref.1, f32[1,4096]{1,0:T(1,128)} %bitcast.35, ...), custom_call_target="tpu_custom_call" | custom-call | tf_op jit(solution)/shard_map/pallas_call | solution.py:128
  (5 shorter events, 0.2 us)
Async XLA Ops:
  0.6 14.7 %copy-start = (f32[16,4096]{1,0:T(8,128)S(1)}, f32[16,4096]{1,0:T(8,128)}, u32[]{:S(2)}) copy-start(f32[16,4096]{1,0:T(8,128)} %rate_ref.3) | copy-start | bytes 786436
  1.7 3.2 %collective-permute-start = (bf16[3,2,4096]{2,1,0:T(2,128)(2,1)S(1)}, bf16[3,2,4096]{2,1,0:T(2,128)(2,1)S(1)}, u32[]{:S(2)}, u32[]{:S(2)}) collective-permute-start(bf16[3,2,4096]{2,1,0:T(2,128)(2,1)S(1)} %slice.41), channel_id=1, source_target_pairs={{0,1},{1,4},{4,5},{5,8},{8,9},{9,12},{12,13},{2,3},{3,6},{6,7},{7,... | collective-permute-start | bytes 147464 | tf_op jit(solution)/shard_map/ppermute | solution.py:18
  4.9 0.6 %copy-start.1 = (bf16[3,2,4096]{2,1,0:T(2,128)(2,1)}, bf16[3,2,4096]{2,1,0:T(2,128)(2,1)S(1)}, u32[]{:S(2)}) copy-start(bf16[3,2,4096]{2,1,0:T(2,128)(2,1)S(1)} %collective-permute-done.halo_ref) | copy-start | bytes 147460
  12.4 4.4 %collective-permute-start.1 = (f32[16,4096]{1,0:T(8,128)}, f32[16,4096]{1,0:T(8,128)S(1)}, u32[]{:S(2)}, u32[]{:S(2)}) collective-permute-start(f32[16,4096]{1,0:T(8,128)} %get-tuple-element.4), channel_id=1, source_target_pairs={{0,1},{1,0},{2,3},{3,2},{4,5},{5,4},{6,7},{7,6},{8,9},{9,8},{10,11... | collective-permute-start | bytes 786440 | tf_op jit(solution)/shard_map/ppermute | solution.py:159
  17.7 6.5 %collective-permute-start.2 = (f32[1,16,2048]{2,1,0:T(8,128)S(1)}, f32[1,16,2048]{2,1,0:T(8,128)S(1)}, u32[]{:S(2)}, u32[]{:S(2)}) collective-permute-start(f32[1,16,2048]{2,1,0:T(8,128)S(1)} %fusion.7), channel_id=1, source_target_pairs={{0,4},{4,0},{8,12},{12,8},{1,5},{5,1},{9,13},{13,9},{2,6},{6,2},{1... | collective-permute-start | bytes 393224 | tf_op jit(solution)/shard_map/ppermute | solution.py:147
  24.2 14.4 %collective-permute-start.3 = (f32[2,16,2048]{2,1,0:T(8,128)S(1)}, f32[2,16,2048]{2,1,0:T(8,128)S(1)}, u32[]{:S(2)}, u32[]{:S(2)}) collective-permute-start(f32[2,16,2048]{2,1,0:T(8,128)S(1)} %maximum_select_fusion.1), channel_id=1, source_target_pairs={{0,8},{4,12},{8,0},{12,4},{1,9},{5,13},{9,1},{13,5},{2,10},{6,14},... | collective-permute-start | bytes 786440 | tf_op jit(solution)/shard_map/ppermute | solution.py:147
  38.8 1.6 %collective-permute-start.4 = (f32[32,2048]{1,0:T(8,128)S(1)}, f32[32,2048]{1,0:T(8,128)S(1)}, u32[]{:S(2)}, u32[]{:S(2)}) collective-permute-start(f32[32,2048]{1,0:T(8,128)S(1)} %pad_maximum_fusion.1), channel_id=1, source_target_pairs={{0,1},{1,0},{2,3},{3,2},{4,5},{5,4},{6,7},{7,6},{8,9},{9,8},{10,11... | collective-permute-start | bytes 786440 | tf_op jit(solution)/shard_map/ppermute | solution.py:159

commit v14 on v10

--- a/solution.py
+++ b/solution.py
@@ -94,7 +94,7 @@
 
 def _specs(row_count, modes, taps, features=3):
     x_spec = pl.BlockSpec((features, row_count, CHAN_BLOCK), lambda j: (0, 0, j))
-    halo_spec = pl.BlockSpec((features, taps - 1, CHAN_BLOCK), lambda j: (0, 0, j))
+    halo_spec = pl.BlockSpec((features, 2 * ROW_GROUP, CHAN_BLOCK), lambda j: (0, 0, j))
     filt_spec = pl.BlockSpec((features, taps, CHAN_BLOCK), lambda j: (0, 0, j))
     mode_spec = pl.BlockSpec((modes, CHAN_BLOCK), lambda j: (0, j))
     row_spec = pl.BlockSpec((1, CHAN_BLOCK), lambda j: (0, j))
@@ -147,7 +147,8 @@
     row_count = projected.shape[1]
     chan_count = projected.shape[2]
     modes = decay_rate.shape[0]
-    edge_rows = projected[:, row_count - (tap_count - 1) :, :]
+    edge_count = min(2 * ROW_GROUP, row_count)
+    edge_rows = projected[:, row_count - edge_count :, :]
     halo = from_behind(edge_rows, ("ctx", "dec"), 1)
     contribution, drive = contributions(projected, halo, short_filters, decay_rate)
     core = lax.axis_index("dec")

time: 48.5 us -> 52.4 us (1.080)
  starting transfers between devices: 5.41 us -> 8.51 us
    ppermute x2, starting transfers between devices: 3.05 us -> 6.13 us  [swap_cores(): return lax.ppermute(value, 'dec', [(0, 1), (1, 0)])]
where the time goes in v14:
time: 52.4 us; the launch traced here: 52.1 us
  Pallas kernels  17.6 us (34%)
  blocking collectives  17.3 us (33%)
  starting transfers between devices  8.51 us (16%)
  waiting for transfers between devices  4.14 us (8%)
  other arithmetic  2.04 us (4%)
  local copies, waits for them, and re-layouts  1.83 us (3%)
  between operations  0.69 us (1%)
    all_gather x1, blocking collectives, local(): received = lax.all_gather(chip_part, 'ctx', axis=0, tiled=False)  17.3 us
    pallas_call x1, Pallas kernels, mix(): pl.pallas_call(_mix_kernel, grid=(chan_count // CHAN_BLOCK,), in_specs=[x...  10.7 us
    pallas_call x1, Pallas kernels, contributions(): pl.pallas_call(_contrib_kernel, grid=(chan_count // CHAN_BLOCK,), in_spec...  6.9 us
    ppermute x2, starting transfers between devices, swap_cores(): return lax.ppermute(value, 'dec', [(0, 1), (1, 0)])  6.13 us
    ppermute x2, waiting for transfers between devices, swap_cores(): return lax.ppermute(value, 'dec', [(0, 1), (1, 0)])  2.83 us
    ppermute x1, starting transfers between devices, from_behind(): lax.ppermute(value, axis, [(source, source + steps) for source in range(i...  2.38 us
    ppermute x1, waiting for transfers between devices, from_behind(): lax.ppermute(value, axis, [(source, source + steps) for source in range(i...  1.31 us
    slice x1, local copies, waits for them, and re-layouts, local(): edge_rows = projected[:, row_count - edge_count:, :]  1.07 us
  transfers between devices with their start and end apart: 3, of which 3 were waited for; matrix products, arithmetic and copies ran while one was open for 0% of the time, Pallas kernels for 0%

profile of v14, /device:TPU:0, one launch (start us, length us, event | category | flops | bytes accessed | tf_op | source)
XLA Modules:
  0.0 52.1 jit_solution(7126636744684509723)
XLA Ops:
  0.6 0.0 copy-start
  0.6 1.1 %slice.41 = bf16[3,16,4096]{2,1,0:T(8,128)(2,1)S(1)} slice(bf16[3,128,4096]{2,1,0:T(8,128)(2,1)} %x_ref.3), slice={[0:3], [112:128], [0:4096]} | slice | bytes 786432 | tf_op jit(solution)/shard_map/slice | solution.py:151
  1.7 2.4 %collective-permute-start = (bf16[3,16,4096]{2,1,0:T(8,128)(2,1)S(1)}, bf16[3,16,4096]{2,1,0:T(8,128)(2,1)S(1)}, u32[]{:S(2)}, u32[]{:S(2)}) collective-permute-start(bf16[3,16,4096]{2,1,0:T(8,128)(2,1)S(1)} %slice.41), channel_id=1, source_target_pairs={{0,1},{1,4},{4,5},{5,8},{8,9},{9,12},{12,13},{2,3},{3,6},{6,7},{7,... | collective-permute-start | bytes 1179656 | tf_op jit(solution)/shard_map/ppermute | solution.py:18
  4.1 1.3 %collective-permute-done.halo_ref = bf16[3,16,4096]{2,1,0:T(8,128)(2,1)S(1)} collective-permute-done((bf16[3,16,4096]{2,1,0:T(8,128)(2,1)S(1)}, bf16[3,16,4096]{2,1,0:T(8,128)(2,1)S(1)}, u32[]{:S(2)}, u32[]{:S(2)}) %collective-permute-start) | collective-permute-done | bytes 393248 | tf_op jit(solution)/shard_map/ppermute | solution.py:18
  5.4 0.0 copy-start.1
  5.4 0.8 %copy-done.1 = bf16[3,16,4096]{2,1,0:T(8,128)(2,1)} copy-done((bf16[3,16,4096]{2,1,0:T(8,128)(2,1)}, bf16[3,16,4096]{2,1,0:T(8,128)(2,1)S(1)}, u32[]{:S(2)}) %copy-start.1) | copy-done | bytes 393240
  6.2 6.9 %shard_map.68 = (f32[16,4096]{1,0:T(8,128)}, f32[128,4096]{1,0:T(8,128)}) custom-call(bf16[3,128,4096]{2,1,0:T(8,128)(2,1)} %x_ref.3, bf16[3,16,4096]{2,1,0:T(8,128)(2,1)} %copy-done.1, f32[3,3,4096]{2,1,0:T(4,128)} %filt_ref.3, f32[16,4096]{1,0:T(8,128)} %rate_ref.3), custom_call_target="tpu_custom_call" | custom-call | tf_op jit(solution)/shard_map/pallas_call | solution.py:109
  13.1 6.1 %collective-permute-start.1 = (f32[16,4096]{1,0:T(8,128)}, f32[16,4096]{1,0:T(8,128)S(1)}, u32[]{:S(2)}, u32[]{:S(2)}) collective-permute-start(f32[16,4096]{1,0:T(8,128)} %get-tuple-element.4), channel_id=1, source_target_pairs={{0,1},{1,0},{2,3},{3,2},{4,5},{5,4},{6,7},{7,6},{8,9},{9,8},{10,11... | collective-permute-start | bytes 786440 | tf_op jit(solution)/shard_map/ppermute | solution.py:142
  19.1 0.0 copy-done
  19.2 1.3 %collective-permute-done.1 = f32[16,4096]{1,0:T(8,128)S(1)} collective-permute-done((f32[16,4096]{1,0:T(8,128)}, f32[16,4096]{1,0:T(8,128)S(1)}, u32[]{:S(2)}, u32[]{:S(2)}) %collective-permute-start.1) | collective-permute-done | bytes 262176 | tf_op jit(solution)/shard_map/ppermute | solution.py:142
  20.5 1.0 %fusion.2 = f32[16,2048]{1,0:T(8,128)S(1)} fusion(f32[16,4096]{1,0:T(8,128)S(1)} %collective-permute-done.1, f32[16,4096]{1,0:T(8,128)} %get-tuple-element.4, f32[16,4096]{1,0:T(8,128)S(1)} %multiply_exponential_fusion, pred[]{:T(512)S(6)} %eq.13), kind=kLoop, calls=%fused_computation.13 | loop fusion | flops 163840 | bytes 917505 | tf_op jit(solution)/shard_map/jit(_where)/select_n | solution.py:161
  21.5 17.3 %all-gather = f32[64,2048]{1,0:T(8,128)S(1)} all-gather(f32[16,2048]{1,0:T(8,128)S(1)} %fusion.2), channel_id=2, replica_groups=mesh['grp'=2,'ctx'=4,'chan'=2,'dec'=2] {'ctx'}, dimensions={0}, use_global_device_ids=true | all-gather | bytes 655360 | tf_op jit(solution)/shard_map/all_gather | solution.py:167
  38.8 0.1 select_select_fusion
  38.9 0.1 collective-permute-start.2
  39.0 1.5 %collective-permute-done.2 = f32[32,2048]{1,0:T(8,128)S(1)} collective-permute-done((f32[32,2048]{1,0:T(8,128)S(1)}, f32[32,2048]{1,0:T(8,128)S(1)}, u32[]{:S(2)}, u32[]{:S(2)}) %collective-permute-start.2) | collective-permute-done | bytes 262176 | tf_op jit(solution)/shard_map/ppermute | solution.py:142
  40.6 0.9 %pad_maximum_fusion = (f32[16,4096]{1,0:T(8,128)}, f32[16,4096]{1,0:T(8,128)}) fusion(f32[32,2048]{1,0:T(8,128)S(1)} %get-tuple-element.11, f32[32,2048]{1,0:T(8,128)S(1)} %get-tuple-element.10, f32[16,4096]{1,0:T(8,128)S(1)} %collective-permute-done.1, f32[16,4096]{1,0:T(8,128)S(1)} %copy-done, pred[]{:T(512)S(6)} %eq.13), kind=kLoop, calls=%fused_computation.3 | loop fusion | flops 458752 | bytes 1572865 | tf_op jit(solution)/shard_map/concatenate | solution.py:179
  41.4 10.7 %shard_map.69 = (bf16[128,4096]{1,0:T(8,128)(2,1)}, f32[16,4096]{1,0:T(8,128)}) custom-call(bf16[3,128,4096]{2,1,0:T(8,128)(2,1)} %x_ref.3, bf16[3,16,4096]{2,1,0:T(8,128)(2,1)} %copy-done.1, f32[3,3,4096]{2,1,0:T(4,128)} %filt_ref.3, f32[16,4096]{1,0:T(8,128)} %rate_ref.3, f32[16,4096]{1,0:T(8,128)} %res_ref.1, f32[1,4096]{1,0:T(1,128)} %bitcast.1, ...), custom_call_target="tpu_custom_call" | custom-call | tf_op jit(solution)/shard_map/pallas_call | solution.py:128
  (3 shorter events, 0.1 us)
Async XLA Ops:
  0.6 18.5 %copy-start = (f32[16,4096]{1,0:T(8,128)S(1)}, f32[16,4096]{1,0:T(8,128)}, u32[]{:S(2)}) copy-start(f32[16,4096]{1,0:T(8,128)} %rate_ref.3) | copy-start | bytes 786436
  1.7 3.7 %collective-permute-start = (bf16[3,16,4096]{2,1,0:T(8,128)(2,1)S(1)}, bf16[3,16,4096]{2,1,0:T(8,128)(2,1)S(1)}, u32[]{:S(2)}, u32[]{:S(2)}) collective-permute-start(bf16[3,16,4096]{2,1,0:T(8,128)(2,1)S(1)} %slice.41), channel_id=1, source_target_pairs={{0,1},{1,4},{4,5},{5,8},{8,9},{9,12},{12,13},{2,3},{3,6},{6,7},{7,... | collective-permute-start | bytes 1179656 | tf_op jit(solution)/shard_map/ppermute | solution.py:18
  5.4 0.8 %copy-start.1 = (bf16[3,16,4096]{2,1,0:T(8,128)(2,1)}, bf16[3,16,4096]{2,1,0:T(8,128)(2,1)S(1)}, u32[]{:S(2)}) copy-start(bf16[3,16,4096]{2,1,0:T(8,128)(2,1)S(1)} %collective-permute-done.halo_ref) | copy-start | bytes 1179652
  13.1 7.4 %collective-permute-start.1 = (f32[16,4096]{1,0:T(8,128)}, f32[16,4096]{1,0:T(8,128)S(1)}, u32[]{:S(2)}, u32[]{:S(2)}) collective-permute-start(f32[16,4096]{1,0:T(8,128)} %get-tuple-element.4), channel_id=1, source_target_pairs={{0,1},{1,0},{2,3},{3,2},{4,5},{5,4},{6,7},{7,6},{8,9},{9,8},{10,11... | collective-permute-start | bytes 786440 | tf_op jit(solution)/shard_map/ppermute | solution.py:142
  38.9 1.6 %collective-permute-start.2 = (f32[32,2048]{1,0:T(8,128)S(1)}, f32[32,2048]{1,0:T(8,128)S(1)}, u32[]{:S(2)}, u32[]{:S(2)}) collective-permute-start(f32[32,2048]{1,0:T(8,128)S(1)} %pad_maximum_fusion.1), channel_id=1, source_target_pairs={{0,1},{1,0},{2,3},{3,2},{4,5},{5,4},{6,7},{7,6},{8,9},{9,8},{10,11... | collective-permute-start | bytes 786440 | tf_op jit(solution)/shard_map/ppermute | solution.py:142

commit v15 on v10

--- a/solution.py
+++ b/solution.py
@@ -24,7 +24,15 @@
     taps = filt_ref[index]
     last = halo[halo.shape[0] - 1 : halo.shape[0]]
     second = halo[halo.shape[0] - 2 : halo.shape[0] - 1]
-    body = taps[0:1] * x + taps[1:2] * pltpu.roll(x, 1, 0) + taps[2:3] * pltpu.roll(x, 2, 0)
+    raw = x_ref[index]
+    row_count = raw.shape[0]
+    to_row = lax.broadcasted_iota(jnp.int32, (row_count, row_count), 0)
+    from_row = lax.broadcasted_iota(jnp.int32, (row_count, row_count), 1)
+    shift1 = jnp.where(from_row == to_row - 1, 1.0, 0.0).astype(raw.dtype)
+    shift2 = jnp.where(from_row == to_row - 2, 1.0, 0.0).astype(raw.dtype)
+    moved1 = jnp.dot(shift1, raw, preferred_element_type=jnp.float32)
+    moved2 = jnp.dot(shift2, raw, preferred_element_type=jnp.float32)
+    body = taps[0:1] * x + taps[1:2] * moved1 + taps[2:3] * moved2
     head_x = x[:ROW_GROUP]
     rows = lax.broadcasted_iota(jnp.int32, head_x.shape, 0)
     back1 = jnp.where(rows == 0, last, pltpu.roll(head_x, 1, 0))

time: 48.5 us -> 48.7 us (level)
  no operation moved by 1% of the time
where the time goes in v15:
time: 48.7 us; the launch traced here: 48.4 us
  Pallas kernels  17.8 us (37%)
  blocking collectives  17.2 us (35%)
  starting transfers between devices  5.41 us (11%)
  waiting for transfers between devices  3.69 us (8%)
  other arithmetic  2.05 us (4%)
  local copies, waits for them, and re-layouts  1.64 us (3%)
  between operations  0.69 us (1%)
    all_gather x1, blocking collectives, local(): received = lax.all_gather(chip_part, 'ctx', axis=0, tiled=False)  17.2 us
    pallas_call x1, Pallas kernels, mix(): pl.pallas_call(_mix_kernel, grid=(chan_count // CHAN_BLOCK,), in_specs=[x...  10.9 us
    pallas_call x1, Pallas kernels, contributions(): pl.pallas_call(_contrib_kernel, grid=(chan_count // CHAN_BLOCK,), in_spec...  6.88 us
    ppermute x2, starting transfers between devices, swap_cores(): return lax.ppermute(value, 'dec', [(0, 1), (1, 0)])  3.05 us
    ppermute x2, waiting for transfers between devices, swap_cores(): return lax.ppermute(value, 'dec', [(0, 1), (1, 0)])  2.83 us
    ppermute x1, starting transfers between devices, from_behind(): lax.ppermute(value, axis, [(source, source + steps) for source in range(i...  2.36 us
    slice x1, local copies, waits for them, and re-layouts, local(): edge_rows = projected[:, row_count - (tap_count - 1):, :]  1.02 us
    select_n x1, other arithmetic, local(): jnp.where(first, lo(shard_decay) * lo(contribution) + lo(other), hi(shard...  1.01 us
  transfers between devices with their start and end apart: 3, of which 3 were waited for; matrix products, arithmetic and copies ran while one was open for 0% of the time, Pallas kernels for 0%

profile of v15, /device:TPU:0, one launch (start us, length us, event | category | flops | bytes accessed | tf_op | source)
XLA Modules:
  0.0 48.4 jit_solution(16823216088393359511)
XLA Ops:
  0.6 0.0 copy-start
  0.6 1.0 %slice.41 = bf16[3,2,4096]{2,1,0:T(2,128)(2,1)S(1)} slice(bf16[3,128,4096]{2,1,0:T(8,128)(2,1)} %x_ref.3), slice={[0:3], [126:128], [0:4096]} | slice | bytes 98304 | tf_op jit(solution)/shard_map/slice | solution.py:158
  1.7 2.4 %collective-permute-start = (bf16[3,2,4096]{2,1,0:T(2,128)(2,1)S(1)}, bf16[3,2,4096]{2,1,0:T(2,128)(2,1)S(1)}, u32[]{:S(2)}, u32[]{:S(2)}) collective-permute-start(bf16[3,2,4096]{2,1,0:T(2,128)(2,1)S(1)} %slice.41), channel_id=1, source_target_pairs={{0,1},{1,4},{4,5},{5,8},{8,9},{9,12},{12,13},{2,3},{3,6},{6,7},{7,... | collective-permute-start | bytes 147464 | tf_op jit(solution)/shard_map/ppermute | solution.py:18
  4.0 0.9 %collective-permute-done.halo_ref = bf16[3,2,4096]{2,1,0:T(2,128)(2,1)S(1)} collective-permute-done((bf16[3,2,4096]{2,1,0:T(2,128)(2,1)S(1)}, bf16[3,2,4096]{2,1,0:T(2,128)(2,1)S(1)}, u32[]{:S(2)}, u32[]{:S(2)}) %collective-permute-start) | collective-permute-done | bytes 49184 | tf_op jit(solution)/shard_map/ppermute | solution.py:18
  4.9 0.0 copy-start.1
  4.9 0.6 %copy-done.1 = bf16[3,2,4096]{2,1,0:T(2,128)(2,1)} copy-done((bf16[3,2,4096]{2,1,0:T(2,128)(2,1)}, bf16[3,2,4096]{2,1,0:T(2,128)(2,1)S(1)}, u32[]{:S(2)}) %copy-start.1) | copy-done | bytes 49176
  5.5 6.9 %shard_map.68 = (f32[16,4096]{1,0:T(8,128)}, f32[128,4096]{1,0:T(8,128)}) custom-call(bf16[3,128,4096]{2,1,0:T(8,128)(2,1)} %x_ref.3, bf16[3,2,4096]{2,1,0:T(2,128)(2,1)} %copy-done.1, f32[3,3,4096]{2,1,0:T(4,128)} %filt_ref.3, f32[16,4096]{1,0:T(8,128)} %rate_ref.3), custom_call_target="tpu_custom_call" | custom-call | tf_op jit(solution)/shard_map/pallas_call | solution.py:117
  12.4 3.0 %collective-permute-start.1 = (f32[16,4096]{1,0:T(8,128)}, f32[16,4096]{1,0:T(8,128)S(1)}, u32[]{:S(2)}, u32[]{:S(2)}) collective-permute-start(f32[16,4096]{1,0:T(8,128)} %get-tuple-element.4), channel_id=1, source_target_pairs={{0,1},{1,0},{2,3},{3,2},{4,5},{5,4},{6,7},{7,6},{8,9},{9,8},{10,11... | collective-permute-start | bytes 786440 | tf_op jit(solution)/shard_map/ppermute | solution.py:150
  15.4 0.0 copy-done
  15.4 1.3 %collective-permute-done.1 = f32[16,4096]{1,0:T(8,128)S(1)} collective-permute-done((f32[16,4096]{1,0:T(8,128)}, f32[16,4096]{1,0:T(8,128)S(1)}, u32[]{:S(2)}, u32[]{:S(2)}) %collective-permute-start.1) | collective-permute-done | bytes 262176 | tf_op jit(solution)/shard_map/ppermute | solution.py:150
  16.7 1.0 %fusion.2 = f32[16,2048]{1,0:T(8,128)S(1)} fusion(f32[16,4096]{1,0:T(8,128)S(1)} %collective-permute-done.1, f32[16,4096]{1,0:T(8,128)} %get-tuple-element.4, f32[16,4096]{1,0:T(8,128)S(1)} %multiply_exponential_fusion, pred[]{:T(512)S(6)} %eq.13), kind=kLoop, calls=%fused_computation.13 | loop fusion | flops 163840 | bytes 917505 | tf_op jit(solution)/shard_map/jit(_where)/select_n | solution.py:168
  17.8 17.2 %all-gather = f32[64,2048]{1,0:T(8,128)S(1)} all-gather(f32[16,2048]{1,0:T(8,128)S(1)} %fusion.2), channel_id=2, replica_groups=mesh['grp'=2,'ctx'=4,'chan'=2,'dec'=2] {'ctx'}, dimensions={0}, use_global_device_ids=true | all-gather | bytes 655360 | tf_op jit(solution)/shard_map/all_gather | solution.py:174
  34.9 0.1 select_select_fusion
  35.0 0.1 collective-permute-start.2
  35.1 1.5 %collective-permute-done.2 = f32[32,2048]{1,0:T(8,128)S(1)} collective-permute-done((f32[32,2048]{1,0:T(8,128)S(1)}, f32[32,2048]{1,0:T(8,128)S(1)}, u32[]{:S(2)}, u32[]{:S(2)}) %collective-permute-start.2) | collective-permute-done | bytes 262176 | tf_op jit(solution)/shard_map/ppermute | solution.py:150
  36.7 0.9 %pad_maximum_fusion = (f32[16,4096]{1,0:T(8,128)}, f32[16,4096]{1,0:T(8,128)}) fusion(f32[32,2048]{1,0:T(8,128)S(1)} %get-tuple-element.11, f32[32,2048]{1,0:T(8,128)S(1)} %get-tuple-element.10, f32[16,4096]{1,0:T(8,128)S(1)} %collective-permute-done.1, f32[16,4096]{1,0:T(8,128)S(1)} %copy-done, pred[]{:T(512)S(6)} %eq.13), kind=kLoop, calls=%fused_computation.3 | loop fusion | flops 458752 | bytes 1572865 | tf_op jit(solution)/shard_map/concatenate | solution.py:186
  37.5 10.9 %shard_map.69 = (bf16[128,4096]{1,0:T(8,128)(2,1)}, f32[16,4096]{1,0:T(8,128)}) custom-call(bf16[3,128,4096]{2,1,0:T(8,128)(2,1)} %x_ref.3, bf16[3,2,4096]{2,1,0:T(2,128)(2,1)} %copy-done.1, f32[3,3,4096]{2,1,0:T(4,128)} %filt_ref.3, f32[16,4096]{1,0:T(8,128)} %rate_ref.3, f32[16,4096]{1,0:T(8,128)} %res_ref.1, f32[1,4096]{1,0:T(1,128)} %bitcast.1, ...), custom_call_target="tpu_custom_call" | custom-call | tf_op jit(solution)/shard_map/pallas_call | solution.py:136
  (3 shorter events, 0.1 us)
Async XLA Ops:
  0.6 14.7 %copy-start = (f32[16,4096]{1,0:T(8,128)S(1)}, f32[16,4096]{1,0:T(8,128)}, u32[]{:S(2)}) copy-start(f32[16,4096]{1,0:T(8,128)} %rate_ref.3) | copy-start | bytes 786436
  1.7 3.2 %collective-permute-start = (bf16[3,2,4096]{2,1,0:T(2,128)(2,1)S(1)}, bf16[3,2,4096]{2,1,0:T(2,128)(2,1)S(1)}, u32[]{:S(2)}, u32[]{:S(2)}) collective-permute-start(bf16[3,2,4096]{2,1,0:T(2,128)(2,1)S(1)} %slice.41), channel_id=1, source_target_pairs={{0,1},{1,4},{4,5},{5,8},{8,9},{9,12},{12,13},{2,3},{3,6},{6,7},{7,... | collective-permute-start | bytes 147464 | tf_op jit(solution)/shard_map/ppermute | solution.py:18
  4.9 0.6 %copy-start.1 = (bf16[3,2,4096]{2,1,0:T(2,128)(2,1)}, bf16[3,2,4096]{2,1,0:T(2,128)(2,1)S(1)}, u32[]{:S(2)}) copy-start(bf16[3,2,4096]{2,1,0:T(2,128)(2,1)S(1)} %collective-permute-done.halo_ref) | copy-start | bytes 147460
  12.4 4.4 %collective-permute-start.1 = (f32[16,4096]{1,0:T(8,128)}, f32[16,4096]{1,0:T(8,128)S(1)}, u32[]{:S(2)}, u32[]{:S(2)}) collective-permute-start(f32[16,4096]{1,0:T(8,128)} %get-tuple-element.4), channel_id=1, source_target_pairs={{0,1},{1,0},{2,3},{3,2},{4,5},{5,4},{6,7},{7,6},{8,9},{9,8},{10,11... | collective-permute-start | bytes 786440 | tf_op jit(solution)/shard_map/ppermute | solution.py:150
  35.0 1.6 %collective-permute-start.2 = (f32[32,2048]{1,0:T(8,128)S(1)}, f32[32,2048]{1,0:T(8,128)S(1)}, u32[]{:S(2)}, u32[]{:S(2)}) collective-permute-start(f32[32,2048]{1,0:T(8,128)S(1)} %pad_maximum_fusion.1), channel_id=1, source_target_pairs={{0,1},{1,0},{2,3},{3,2},{4,5},{5,4},{6,7},{7,6},{8,9},{9,8},{10,11... | collective-permute-start | bytes 786440 | tf_op jit(solution)/shard_map/ppermute | solution.py:150

commit v16 on v10

--- a/solution.py
+++ b/solution.py
@@ -66,7 +66,7 @@
                 conv_ref[pl.ds(start, ROW_GROUP), lanes] = _reduce_rows(ys)
             return state
 
-        finals.append(lax.fori_loop(0, row_count // ROW_GROUP, body, state[:, lanes]))
+        finals.append(lax.fori_loop(0, row_count // ROW_GROUP, body, state[:, lanes], unroll=4))
     return jnp.concatenate(finals, axis=1)
 
 

time: 48.5 us -> 47.4 us (0.977)
  Pallas kernels: 17.5 us -> 16.4 us
    pallas_call x1, Pallas kernels: 10.7 us -> 9.84 us  [mix(): pl.pallas_call(_mix_kernel, grid=(chan_count // CHAN_BLOCK,), in_specs=[x...]
where the time goes in v16:
time: 47.4 us; the launch traced here: 47.1 us
  blocking collectives  17.2 us (36%)
  Pallas kernels  16.4 us (35%)
  starting transfers between devices  5.41 us (11%)
  waiting for transfers between devices  3.69 us (8%)
  other arithmetic  2.05 us (4%)
  local copies, waits for them, and re-layouts  1.64 us (3%)
  between operations  0.69 us (1%)
    all_gather x1, blocking collectives, local(): received = lax.all_gather(chip_part, 'ctx', axis=0, tiled=False)  17.2 us
    pallas_call x1, Pallas kernels, mix(): pl.pallas_call(_mix_kernel, grid=(chan_count // CHAN_BLOCK,), in_specs=[x...  9.84 us
    pallas_call x1, Pallas kernels, contributions(): pl.pallas_call(_contrib_kernel, grid=(chan_count // CHAN_BLOCK,), in_spec...  6.6 us
    ppermute x2, starting transfers between devices, swap_cores(): return lax.ppermute(value, 'dec', [(0, 1), (1, 0)])  3.05 us
    ppermute x2, waiting for transfers between devices, swap_cores(): return lax.ppermute(value, 'dec', [(0, 1), (1, 0)])  2.83 us
    ppermute x1, starting transfers between devices, from_behind(): lax.ppermute(value, axis, [(source, source + steps) for source in range(i...  2.36 us
    slice x1, local copies, waits for them, and re-layouts, local(): edge_rows = projected[:, row_count - (tap_count - 1):, :]  1.02 us
    select_n x1, other arithmetic, local(): jnp.where(first, lo(shard_decay) * lo(contribution) + lo(other), hi(shard...  1.01 us
  transfers between devices with their start and end apart: 3, of which 3 were waited for; matrix products, arithmetic and copies ran while one was open for 0% of the time, Pallas kernels for 0%

profile of v16, /device:TPU:0, one launch (start us, length us, event | category | flops | bytes accessed | tf_op | source)
XLA Modules:
  0.0 47.1 jit_solution(13068492546134389258)
XLA Ops:
  0.6 0.0 copy-start
  0.6 1.0 %slice.41 = bf16[3,2,4096]{2,1,0:T(2,128)(2,1)S(1)} slice(bf16[3,128,4096]{2,1,0:T(8,128)(2,1)} %x_ref.3), slice={[0:3], [126:128], [0:4096]} | slice | bytes 98304 | tf_op jit(solution)/shard_map/slice | solution.py:150
  1.7 2.4 %collective-permute-start = (bf16[3,2,4096]{2,1,0:T(2,128)(2,1)S(1)}, bf16[3,2,4096]{2,1,0:T(2,128)(2,1)S(1)}, u32[]{:S(2)}, u32[]{:S(2)}) collective-permute-start(bf16[3,2,4096]{2,1,0:T(2,128)(2,1)S(1)} %slice.41), channel_id=1, source_target_pairs={{0,1},{1,4},{4,5},{5,8},{8,9},{9,12},{12,13},{2,3},{3,6},{6,7},{7,... | collective-permute-start | bytes 147464 | tf_op jit(solution)/shard_map/ppermute | solution.py:18
  4.0 0.9 %collective-permute-done.halo_ref = bf16[3,2,4096]{2,1,0:T(2,128)(2,1)S(1)} collective-permute-done((bf16[3,2,4096]{2,1,0:T(2,128)(2,1)S(1)}, bf16[3,2,4096]{2,1,0:T(2,128)(2,1)S(1)}, u32[]{:S(2)}, u32[]{:S(2)}) %collective-permute-start) | collective-permute-done | bytes 49184 | tf_op jit(solution)/shard_map/ppermute | solution.py:18
  4.9 0.0 copy-start.1
  4.9 0.6 %copy-done.1 = bf16[3,2,4096]{2,1,0:T(2,128)(2,1)} copy-done((bf16[3,2,4096]{2,1,0:T(2,128)(2,1)}, bf16[3,2,4096]{2,1,0:T(2,128)(2,1)S(1)}, u32[]{:S(2)}) %copy-start.1) | copy-done | bytes 49176
  5.5 6.6 %shard_map.68 = (f32[16,4096]{1,0:T(8,128)}, f32[128,4096]{1,0:T(8,128)}) custom-call(bf16[3,128,4096]{2,1,0:T(8,128)(2,1)} %x_ref.3, bf16[3,2,4096]{2,1,0:T(2,128)(2,1)} %copy-done.1, f32[3,3,4096]{2,1,0:T(4,128)} %filt_ref.3, f32[16,4096]{1,0:T(8,128)} %rate_ref.3), custom_call_target="tpu_custom_call" | custom-call | tf_op jit(solution)/shard_map/pallas_call | solution.py:109
  12.1 3.0 %collective-permute-start.1 = (f32[16,4096]{1,0:T(8,128)}, f32[16,4096]{1,0:T(8,128)S(1)}, u32[]{:S(2)}, u32[]{:S(2)}) collective-permute-start(f32[16,4096]{1,0:T(8,128)} %get-tuple-element.4), channel_id=1, source_target_pairs={{0,1},{1,0},{2,3},{3,2},{4,5},{5,4},{6,7},{7,6},{8,9},{9,8},{10,11... | collective-permute-start | bytes 786440 | tf_op jit(solution)/shard_map/ppermute | solution.py:142
  15.1 0.0 copy-done
  15.2 1.3 %collective-permute-done.1 = f32[16,4096]{1,0:T(8,128)S(1)} collective-permute-done((f32[16,4096]{1,0:T(8,128)}, f32[16,4096]{1,0:T(8,128)S(1)}, u32[]{:S(2)}, u32[]{:S(2)}) %collective-permute-start.1) | collective-permute-done | bytes 262176 | tf_op jit(solution)/shard_map/ppermute | solution.py:142
  16.5 1.0 %fusion.2 = f32[16,2048]{1,0:T(8,128)S(1)} fusion(f32[16,4096]{1,0:T(8,128)S(1)} %collective-permute-done.1, f32[16,4096]{1,0:T(8,128)} %get-tuple-element.4, f32[16,4096]{1,0:T(8,128)S(1)} %multiply_exponential_fusion, pred[]{:T(512)S(6)} %eq.13), kind=kLoop, calls=%fused_computation.13 | loop fusion | flops 163840 | bytes 917505 | tf_op jit(solution)/shard_map/jit(_where)/select_n | solution.py:160
  17.5 17.2 %all-gather = f32[64,2048]{1,0:T(8,128)S(1)} all-gather(f32[16,2048]{1,0:T(8,128)S(1)} %fusion.2), channel_id=2, replica_groups=mesh['grp'=2,'ctx'=4,'chan'=2,'dec'=2] {'ctx'}, dimensions={0}, use_global_device_ids=true | all-gather | bytes 655360 | tf_op jit(solution)/shard_map/all_gather | solution.py:166
  34.6 0.1 select_select_fusion
  34.8 0.1 collective-permute-start.2
  34.8 1.5 %collective-permute-done.2 = f32[32,2048]{1,0:T(8,128)S(1)} collective-permute-done((f32[32,2048]{1,0:T(8,128)S(1)}, f32[32,2048]{1,0:T(8,128)S(1)}, u32[]{:S(2)}, u32[]{:S(2)}) %collective-permute-start.2) | collective-permute-done | bytes 262176 | tf_op jit(solution)/shard_map/ppermute | solution.py:142
  36.4 0.9 %pad_maximum_fusion = (f32[16,4096]{1,0:T(8,128)}, f32[16,4096]{1,0:T(8,128)}) fusion(f32[32,2048]{1,0:T(8,128)S(1)} %get-tuple-element.11, f32[32,2048]{1,0:T(8,128)S(1)} %get-tuple-element.10, f32[16,4096]{1,0:T(8,128)S(1)} %collective-permute-done.1, f32[16,4096]{1,0:T(8,128)S(1)} %copy-done, pred[]{:T(512)S(6)} %eq.13), kind=kLoop, calls=%fused_computation.3 | loop fusion | flops 458752 | bytes 1572865 | tf_op jit(solution)/shard_map/concatenate | solution.py:178
  37.3 9.8 %shard_map.69 = (bf16[128,4096]{1,0:T(8,128)(2,1)}, f32[16,4096]{1,0:T(8,128)}) custom-call(bf16[3,128,4096]{2,1,0:T(8,128)(2,1)} %x_ref.3, bf16[3,2,4096]{2,1,0:T(2,128)(2,1)} %copy-done.1, f32[3,3,4096]{2,1,0:T(4,128)} %filt_ref.3, f32[16,4096]{1,0:T(8,128)} %rate_ref.3, f32[16,4096]{1,0:T(8,128)} %res_ref.1, f32[1,4096]{1,0:T(1,128)} %bitcast.1, ...), custom_call_target="tpu_custom_call" | custom-call | tf_op jit(solution)/shard_map/pallas_call | solution.py:128
  (3 shorter events, 0.1 us)
Async XLA Ops:
  0.6 14.5 %copy-start = (f32[16,4096]{1,0:T(8,128)S(1)}, f32[16,4096]{1,0:T(8,128)}, u32[]{:S(2)}) copy-start(f32[16,4096]{1,0:T(8,128)} %rate_ref.3) | copy-start | bytes 786436
  1.7 3.2 %collective-permute-start = (bf16[3,2,4096]{2,1,0:T(2,128)(2,1)S(1)}, bf16[3,2,4096]{2,1,0:T(2,128)(2,1)S(1)}, u32[]{:S(2)}, u32[]{:S(2)}) collective-permute-start(bf16[3,2,4096]{2,1,0:T(2,128)(2,1)S(1)} %slice.41), channel_id=1, source_target_pairs={{0,1},{1,4},{4,5},{5,8},{8,9},{9,12},{12,13},{2,3},{3,6},{6,7},{7,... | collective-permute-start | bytes 147464 | tf_op jit(solution)/shard_map/ppermute | solution.py:18
  4.9 0.6 %copy-start.1 = (bf16[3,2,4096]{2,1,0:T(2,128)(2,1)}, bf16[3,2,4096]{2,1,0:T(2,128)(2,1)S(1)}, u32[]{:S(2)}) copy-start(bf16[3,2,4096]{2,1,0:T(2,128)(2,1)S(1)} %collective-permute-done.halo_ref) | copy-start | bytes 147460
  12.1 4.4 %collective-permute-start.1 = (f32[16,4096]{1,0:T(8,128)}, f32[16,4096]{1,0:T(8,128)S(1)}, u32[]{:S(2)}, u32[]{:S(2)}) collective-permute-start(f32[16,4096]{1,0:T(8,128)} %get-tuple-element.4), channel_id=1, source_target_pairs={{0,1},{1,0},{2,3},{3,2},{4,5},{5,4},{6,7},{7,6},{8,9},{9,8},{10,11... | collective-permute-start | bytes 786440 | tf_op jit(solution)/shard_map/ppermute | solution.py:142
  34.8 1.6 %collective-permute-start.2 = (f32[32,2048]{1,0:T(8,128)S(1)}, f32[32,2048]{1,0:T(8,128)S(1)}, u32[]{:S(2)}, u32[]{:S(2)}) collective-permute-start(f32[32,2048]{1,0:T(8,128)S(1)} %pad_maximum_fusion.1), channel_id=1, source_target_pairs={{0,1},{1,0},{2,3},{3,2},{4,5},{5,4},{6,7},{7,6},{8,9},{9,8},{10,11... | collective-permute-start | bytes 786440 | tf_op jit(solution)/shard_map/ppermute | solution.py:142

commit v17 on v16

--- a/solution.py
+++ b/solution.py
@@ -43,7 +43,7 @@
     return jnp.where(m1, b[0] + pltpu.roll(b[0], 7, 0), b[1] + pltpu.roll(b[1], 1, 0))
 
 
-def _scan_rows(drive_ref, decay, residue, state, conv_ref):
+def _scan_rows(drive_ref, decay, residue, state, conv_ref, unroll=4):
     row_count = drive_ref.shape[0]
     low = slice(0, ROW_GROUP)
     high = slice(ROW_GROUP, 2 * ROW_GROUP)
@@ -66,7 +66,7 @@
                 conv_ref[pl.ds(start, ROW_GROUP), lanes] = _reduce_rows(ys)
             return state
 
-        finals.append(lax.fori_loop(0, row_count // ROW_GROUP, body, state[:, lanes], unroll=4))
+        finals.append(lax.fori_loop(0, row_count // ROW_GROUP, body, state[:, lanes], unroll=unroll))
     return jnp.concatenate(finals, axis=1)
 
 
@@ -78,7 +78,7 @@
     block = rate_ref.shape[1]
     start = pl.multiple_of(pl.program_id(0) * block, block)
     state = jnp.zeros(rate_ref.shape, jnp.float32)
-    out_ref[:, pl.ds(start, block)] = _scan_rows(drive_ref, decay, None, state, None)
+    out_ref[:, pl.ds(start, block)] = _scan_rows(drive_ref, decay, None, state, None, 8)
 
 
 def _mix_kernel(x_ref, halo_ref, filt_ref, rate_ref, res_ref, skip_ref, init_ref, fin_in_ref, drive_ref,

time: 47.4 us -> 47.4 us (level)
  no operation moved by 1% of the time
where the time goes in v17:
time: 47.4 us; the launch traced here: 47.1 us
  blocking collectives  17.2 us (36%)
  Pallas kernels  16.4 us (35%)
  starting transfers between devices  5.41 us (11%)
  waiting for transfers between devices  3.69 us (8%)
  other arithmetic  2.05 us (4%)
  local copies, waits for them, and re-layouts  1.64 us (3%)
  between operations  0.69 us (1%)
    all_gather x1, blocking collectives, local(): received = lax.all_gather(chip_part, 'ctx', axis=0, tiled=False)  17.2 us
    pallas_call x1, Pallas kernels, mix(): pl.pallas_call(_mix_kernel, grid=(chan_count // CHAN_BLOCK,), in_specs=[x...  9.84 us
    pallas_call x1, Pallas kernels, contributions(): pl.pallas_call(_contrib_kernel, grid=(chan_count // CHAN_BLOCK,), in_spec...  6.56 us
    ppermute x2, starting transfers between devices, swap_cores(): return lax.ppermute(value, 'dec', [(0, 1), (1, 0)])  3.05 us
    ppermute x2, waiting for transfers between devices, swap_cores(): return lax.ppermute(value, 'dec', [(0, 1), (1, 0)])  2.83 us
    ppermute x1, starting transfers between devices, from_behind(): lax.ppermute(value, axis, [(source, source + steps) for source in range(i...  2.36 us
    slice x1, local copies, waits for them, and re-layouts, local(): edge_rows = projected[:, row_count - (tap_count - 1):, :]  1.02 us
    select_n x1, other arithmetic, local(): jnp.where(first, lo(shard_decay) * lo(contribution) + lo(other), hi(shard...  1.01 us
  transfers between devices with their start and end apart: 3, of which 3 were waited for; matrix products, arithmetic and copies ran while one was open for 0% of the time, Pallas kernels for 0%

profile of v17, /device:TPU:0, one launch (start us, length us, event | category | flops | bytes accessed | tf_op | source)
XLA Modules:
  0.0 47.1 jit_solution(10936394483804894639)
XLA Ops:
  0.6 0.0 copy-start
  0.6 1.0 %slice.41 = bf16[3,2,4096]{2,1,0:T(2,128)(2,1)S(1)} slice(bf16[3,128,4096]{2,1,0:T(8,128)(2,1)} %x_ref.3), slice={[0:3], [126:128], [0:4096]} | slice | bytes 98304 | tf_op jit(solution)/shard_map/slice | solution.py:150
  1.7 2.4 %collective-permute-start = (bf16[3,2,4096]{2,1,0:T(2,128)(2,1)S(1)}, bf16[3,2,4096]{2,1,0:T(2,128)(2,1)S(1)}, u32[]{:S(2)}, u32[]{:S(2)}) collective-permute-start(bf16[3,2,4096]{2,1,0:T(2,128)(2,1)S(1)} %slice.41), channel_id=1, source_target_pairs={{0,1},{1,4},{4,5},{5,8},{8,9},{9,12},{12,13},{2,3},{3,6},{6,7},{7,... | collective-permute-start | bytes 147464 | tf_op jit(solution)/shard_map/ppermute | solution.py:18
  4.0 0.9 %collective-permute-done.halo_ref = bf16[3,2,4096]{2,1,0:T(2,128)(2,1)S(1)} collective-permute-done((bf16[3,2,4096]{2,1,0:T(2,128)(2,1)S(1)}, bf16[3,2,4096]{2,1,0:T(2,128)(2,1)S(1)}, u32[]{:S(2)}, u32[]{:S(2)}) %collective-permute-start) | collective-permute-done | bytes 49184 | tf_op jit(solution)/shard_map/ppermute | solution.py:18
  4.9 0.0 copy-start.1
  4.9 0.6 %copy-done.1 = bf16[3,2,4096]{2,1,0:T(2,128)(2,1)} copy-done((bf16[3,2,4096]{2,1,0:T(2,128)(2,1)}, bf16[3,2,4096]{2,1,0:T(2,128)(2,1)S(1)}, u32[]{:S(2)}) %copy-start.1) | copy-done | bytes 49176
  5.5 6.6 %shard_map.68 = (f32[16,4096]{1,0:T(8,128)}, f32[128,4096]{1,0:T(8,128)}) custom-call(bf16[3,128,4096]{2,1,0:T(8,128)(2,1)} %x_ref.3, bf16[3,2,4096]{2,1,0:T(2,128)(2,1)} %copy-done.1, f32[3,3,4096]{2,1,0:T(4,128)} %filt_ref.3, f32[16,4096]{1,0:T(8,128)} %rate_ref.3), custom_call_target="tpu_custom_call" | custom-call | tf_op jit(solution)/shard_map/pallas_call | solution.py:109
  12.1 3.0 %collective-permute-start.1 = (f32[16,4096]{1,0:T(8,128)}, f32[16,4096]{1,0:T(8,128)S(1)}, u32[]{:S(2)}, u32[]{:S(2)}) collective-permute-start(f32[16,4096]{1,0:T(8,128)} %get-tuple-element.4), channel_id=1, source_target_pairs={{0,1},{1,0},{2,3},{3,2},{4,5},{5,4},{6,7},{7,6},{8,9},{9,8},{10,11... | collective-permute-start | bytes 786440 | tf_op jit(solution)/shard_map/ppermute | solution.py:142
  15.1 0.0 copy-done
  15.1 1.3 %collective-permute-done.1 = f32[16,4096]{1,0:T(8,128)S(1)} collective-permute-done((f32[16,4096]{1,0:T(8,128)}, f32[16,4096]{1,0:T(8,128)S(1)}, u32[]{:S(2)}, u32[]{:S(2)}) %collective-permute-start.1) | collective-permute-done | bytes 262176 | tf_op jit(solution)/shard_map/ppermute | solution.py:142
  16.4 1.0 %fusion.2 = f32[16,2048]{1,0:T(8,128)S(1)} fusion(f32[16,4096]{1,0:T(8,128)S(1)} %collective-permute-done.1, f32[16,4096]{1,0:T(8,128)} %get-tuple-element.4, f32[16,4096]{1,0:T(8,128)S(1)} %multiply_exponential_fusion, pred[]{:T(512)S(6)} %eq.13), kind=kLoop, calls=%fused_computation.13 | loop fusion | flops 163840 | bytes 917505 | tf_op jit(solution)/shard_map/jit(_where)/select_n | solution.py:160
  17.4 17.2 %all-gather = f32[64,2048]{1,0:T(8,128)S(1)} all-gather(f32[16,2048]{1,0:T(8,128)S(1)} %fusion.2), channel_id=2, replica_groups=mesh['grp'=2,'ctx'=4,'chan'=2,'dec'=2] {'ctx'}, dimensions={0}, use_global_device_ids=true | all-gather | bytes 655360 | tf_op jit(solution)/shard_map/all_gather | solution.py:166
  34.6 0.1 select_select_fusion
  34.7 0.1 collective-permute-start.2
  34.8 1.5 %collective-permute-done.2 = f32[32,2048]{1,0:T(8,128)S(1)} collective-permute-done((f32[32,2048]{1,0:T(8,128)S(1)}, f32[32,2048]{1,0:T(8,128)S(1)}, u32[]{:S(2)}, u32[]{:S(2)}) %collective-permute-start.2) | collective-permute-done | bytes 262176 | tf_op jit(solution)/shard_map/ppermute | solution.py:142
  36.4 0.9 %pad_maximum_fusion = (f32[16,4096]{1,0:T(8,128)}, f32[16,4096]{1,0:T(8,128)}) fusion(f32[32,2048]{1,0:T(8,128)S(1)} %get-tuple-element.11, f32[32,2048]{1,0:T(8,128)S(1)} %get-tuple-element.10, f32[16,4096]{1,0:T(8,128)S(1)} %collective-permute-done.1, f32[16,4096]{1,0:T(8,128)S(1)} %copy-done, pred[]{:T(512)S(6)} %eq.13), kind=kLoop, calls=%fused_computation.3 | loop fusion | flops 458752 | bytes 1572865 | tf_op jit(solution)/shard_map/concatenate | solution.py:178
  37.2 9.8 %shard_map.69 = (bf16[128,4096]{1,0:T(8,128)(2,1)}, f32[16,4096]{1,0:T(8,128)}) custom-call(bf16[3,128,4096]{2,1,0:T(8,128)(2,1)} %x_ref.3, bf16[3,2,4096]{2,1,0:T(2,128)(2,1)} %copy-done.1, f32[3,3,4096]{2,1,0:T(4,128)} %filt_ref.3, f32[16,4096]{1,0:T(8,128)} %rate_ref.3, f32[16,4096]{1,0:T(8,128)} %res_ref.1, f32[1,4096]{1,0:T(1,128)} %bitcast.1, ...), custom_call_target="tpu_custom_call" | custom-call | tf_op jit(solution)/shard_map/pallas_call | solution.py:128
  (3 shorter events, 0.1 us)
Async XLA Ops:
  0.6 14.4 %copy-start = (f32[16,4096]{1,0:T(8,128)S(1)}, f32[16,4096]{1,0:T(8,128)}, u32[]{:S(2)}) copy-start(f32[16,4096]{1,0:T(8,128)} %rate_ref.3) | copy-start | bytes 786436
  1.7 3.2 %collective-permute-start = (bf16[3,2,4096]{2,1,0:T(2,128)(2,1)S(1)}, bf16[3,2,4096]{2,1,0:T(2,128)(2,1)S(1)}, u32[]{:S(2)}, u32[]{:S(2)}) collective-permute-start(bf16[3,2,4096]{2,1,0:T(2,128)(2,1)S(1)} %slice.41), channel_id=1, source_target_pairs={{0,1},{1,4},{4,5},{5,8},{8,9},{9,12},{12,13},{2,3},{3,6},{6,7},{7,... | collective-permute-start | bytes 147464 | tf_op jit(solution)/shard_map/ppermute | solution.py:18
  4.9 0.6 %copy-start.1 = (bf16[3,2,4096]{2,1,0:T(2,128)(2,1)}, bf16[3,2,4096]{2,1,0:T(2,128)(2,1)S(1)}, u32[]{:S(2)}) copy-start(bf16[3,2,4096]{2,1,0:T(2,128)(2,1)S(1)} %collective-permute-done.halo_ref) | copy-start | bytes 147460
  12.1 4.4 %collective-permute-start.1 = (f32[16,4096]{1,0:T(8,128)}, f32[16,4096]{1,0:T(8,128)S(1)}, u32[]{:S(2)}, u32[]{:S(2)}) collective-permute-start(f32[16,4096]{1,0:T(8,128)} %get-tuple-element.4), channel_id=1, source_target_pairs={{0,1},{1,0},{2,3},{3,2},{4,5},{5,4},{6,7},{7,6},{8,9},{9,8},{10,11... | collective-permute-start | bytes 786440 | tf_op jit(solution)/shard_map/ppermute | solution.py:142
  34.7 1.6 %collective-permute-start.2 = (f32[32,2048]{1,0:T(8,128)S(1)}, f32[32,2048]{1,0:T(8,128)S(1)}, u32[]{:S(2)}, u32[]{:S(2)}) collective-permute-start(f32[32,2048]{1,0:T(8,128)S(1)} %pad_maximum_fusion.1), channel_id=1, source_target_pairs={{0,1},{1,0},{2,3},{3,2},{4,5},{5,4},{6,7},{7,6},{8,9},{9,8},{10,11... | collective-permute-start | bytes 786440 | tf_op jit(solution)/shard_map/ppermute | solution.py:142

commit v18 on v15

--- a/solution.py
+++ b/solution.py
@@ -74,7 +74,7 @@
                 conv_ref[pl.ds(start, ROW_GROUP), lanes] = _reduce_rows(ys)
             return state
 
-        finals.append(lax.fori_loop(0, row_count // ROW_GROUP, body, state[:, lanes]))
+        finals.append(lax.fori_loop(0, row_count // ROW_GROUP, body, state[:, lanes], unroll=4))
     return jnp.concatenate(finals, axis=1)
 
 

time: 48.7 us -> 47.6 us (0.977)
  Pallas kernels: 17.8 us -> 16.7 us
    pallas_call x1, Pallas kernels: 10.9 us -> 10 us  [mix(): pl.pallas_call(_mix_kernel, grid=(chan_count // CHAN_BLOCK,), in_specs=[x...]
where the time goes in v18:
time: 47.6 us; the launch traced here: 47.3 us
  blocking collectives  17.2 us (36%)
  Pallas kernels  16.7 us (35%)
  starting transfers between devices  5.41 us (11%)
  waiting for transfers between devices  3.69 us (8%)
  other arithmetic  2.05 us (4%)
  local copies, waits for them, and re-layouts  1.64 us (3%)
  between operations  0.69 us (1%)
    all_gather x1, blocking collectives, local(): received = lax.all_gather(chip_part, 'ctx', axis=0, tiled=False)  17.2 us
    pallas_call x1, Pallas kernels, mix(): pl.pallas_call(_mix_kernel, grid=(chan_count // CHAN_BLOCK,), in_specs=[x...  10 us
    pallas_call x1, Pallas kernels, contributions(): pl.pallas_call(_contrib_kernel, grid=(chan_count // CHAN_BLOCK,), in_spec...  6.63 us
    ppermute x2, starting transfers between devices, swap_cores(): return lax.ppermute(value, 'dec', [(0, 1), (1, 0)])  3.05 us
    ppermute x2, waiting for transfers between devices, swap_cores(): return lax.ppermute(value, 'dec', [(0, 1), (1, 0)])  2.83 us
    ppermute x1, starting transfers between devices, from_behind(): lax.ppermute(value, axis, [(source, source + steps) for source in range(i...  2.36 us
    slice x1, local copies, waits for them, and re-layouts, local(): edge_rows = projected[:, row_count - (tap_count - 1):, :]  1.02 us
    select_n x1, other arithmetic, local(): jnp.where(first, lo(shard_decay) * lo(contribution) + lo(other), hi(shard...  1.01 us
  transfers between devices with their start and end apart: 3, of which 3 were waited for; matrix products, arithmetic and copies ran while one was open for 0% of the time, Pallas kernels for 0%

profile of v18, /device:TPU:0, one launch (start us, length us, event | category | flops | bytes accessed | tf_op | source)
XLA Modules:
  0.0 47.3 jit_solution(14377781539605989024)
XLA Ops:
  0.6 0.0 copy-start
  0.6 1.0 %slice.41 = bf16[3,2,4096]{2,1,0:T(2,128)(2,1)S(1)} slice(bf16[3,128,4096]{2,1,0:T(8,128)(2,1)} %x_ref.3), slice={[0:3], [126:128], [0:4096]} | slice | bytes 98304 | tf_op jit(solution)/shard_map/slice | solution.py:158
  1.7 2.4 %collective-permute-start = (bf16[3,2,4096]{2,1,0:T(2,128)(2,1)S(1)}, bf16[3,2,4096]{2,1,0:T(2,128)(2,1)S(1)}, u32[]{:S(2)}, u32[]{:S(2)}) collective-permute-start(bf16[3,2,4096]{2,1,0:T(2,128)(2,1)S(1)} %slice.41), channel_id=1, source_target_pairs={{0,1},{1,4},{4,5},{5,8},{8,9},{9,12},{12,13},{2,3},{3,6},{6,7},{7,... | collective-permute-start | bytes 147464 | tf_op jit(solution)/shard_map/ppermute | solution.py:18
  4.0 0.9 %collective-permute-done.halo_ref = bf16[3,2,4096]{2,1,0:T(2,128)(2,1)S(1)} collective-permute-done((bf16[3,2,4096]{2,1,0:T(2,128)(2,1)S(1)}, bf16[3,2,4096]{2,1,0:T(2,128)(2,1)S(1)}, u32[]{:S(2)}, u32[]{:S(2)}) %collective-permute-start) | collective-permute-done | bytes 49184 | tf_op jit(solution)/shard_map/ppermute | solution.py:18
  4.9 0.0 copy-start.1
  4.9 0.6 %copy-done.1 = bf16[3,2,4096]{2,1,0:T(2,128)(2,1)} copy-done((bf16[3,2,4096]{2,1,0:T(2,128)(2,1)}, bf16[3,2,4096]{2,1,0:T(2,128)(2,1)S(1)}, u32[]{:S(2)}) %copy-start.1) | copy-done | bytes 49176
  5.5 6.6 %shard_map.68 = (f32[16,4096]{1,0:T(8,128)}, f32[128,4096]{1,0:T(8,128)}) custom-call(bf16[3,128,4096]{2,1,0:T(8,128)(2,1)} %x_ref.3, bf16[3,2,4096]{2,1,0:T(2,128)(2,1)} %copy-done.1, f32[3,3,4096]{2,1,0:T(4,128)} %filt_ref.3, f32[16,4096]{1,0:T(8,128)} %rate_ref.3), custom_call_target="tpu_custom_call" | custom-call | tf_op jit(solution)/shard_map/pallas_call | solution.py:117
  12.1 3.0 %collective-permute-start.1 = (f32[16,4096]{1,0:T(8,128)}, f32[16,4096]{1,0:T(8,128)S(1)}, u32[]{:S(2)}, u32[]{:S(2)}) collective-permute-start(f32[16,4096]{1,0:T(8,128)} %get-tuple-element.4), channel_id=1, source_target_pairs={{0,1},{1,0},{2,3},{3,2},{4,5},{5,4},{6,7},{7,6},{8,9},{9,8},{10,11... | collective-permute-start | bytes 786440 | tf_op jit(solution)/shard_map/ppermute | solution.py:150
  15.1 0.0 copy-done
  15.2 1.3 %collective-permute-done.1 = f32[16,4096]{1,0:T(8,128)S(1)} collective-permute-done((f32[16,4096]{1,0:T(8,128)}, f32[16,4096]{1,0:T(8,128)S(1)}, u32[]{:S(2)}, u32[]{:S(2)}) %collective-permute-start.1) | collective-permute-done | bytes 262176 | tf_op jit(solution)/shard_map/ppermute | solution.py:150
  16.5 1.0 %fusion.2 = f32[16,2048]{1,0:T(8,128)S(1)} fusion(f32[16,4096]{1,0:T(8,128)S(1)} %collective-permute-done.1, f32[16,4096]{1,0:T(8,128)} %get-tuple-element.4, f32[16,4096]{1,0:T(8,128)S(1)} %multiply_exponential_fusion, pred[]{:T(512)S(6)} %eq.13), kind=kLoop, calls=%fused_computation.13 | loop fusion | flops 163840 | bytes 917505 | tf_op jit(solution)/shard_map/jit(_where)/select_n | solution.py:168
  17.5 17.2 %all-gather = f32[64,2048]{1,0:T(8,128)S(1)} all-gather(f32[16,2048]{1,0:T(8,128)S(1)} %fusion.2), channel_id=2, replica_groups=mesh['grp'=2,'ctx'=4,'chan'=2,'dec'=2] {'ctx'}, dimensions={0}, use_global_device_ids=true | all-gather | bytes 655360 | tf_op jit(solution)/shard_map/all_gather | solution.py:174
  34.7 0.1 select_select_fusion
  34.8 0.1 collective-permute-start.2
  34.9 1.5 %collective-permute-done.2 = f32[32,2048]{1,0:T(8,128)S(1)} collective-permute-done((f32[32,2048]{1,0:T(8,128)S(1)}, f32[32,2048]{1,0:T(8,128)S(1)}, u32[]{:S(2)}, u32[]{:S(2)}) %collective-permute-start.2) | collective-permute-done | bytes 262176 | tf_op jit(solution)/shard_map/ppermute | solution.py:150
  36.4 0.9 %pad_maximum_fusion = (f32[16,4096]{1,0:T(8,128)}, f32[16,4096]{1,0:T(8,128)}) fusion(f32[32,2048]{1,0:T(8,128)S(1)} %get-tuple-element.11, f32[32,2048]{1,0:T(8,128)S(1)} %get-tuple-element.10, f32[16,4096]{1,0:T(8,128)S(1)} %collective-permute-done.1, f32[16,4096]{1,0:T(8,128)S(1)} %copy-done, pred[]{:T(512)S(6)} %eq.13), kind=kLoop, calls=%fused_computation.3 | loop fusion | flops 458752 | bytes 1572865 | tf_op jit(solution)/shard_map/concatenate | solution.py:186
  37.3 10.0 %shard_map.69 = (bf16[128,4096]{1,0:T(8,128)(2,1)}, f32[16,4096]{1,0:T(8,128)}) custom-call(bf16[3,128,4096]{2,1,0:T(8,128)(2,1)} %x_ref.3, bf16[3,2,4096]{2,1,0:T(2,128)(2,1)} %copy-done.1, f32[3,3,4096]{2,1,0:T(4,128)} %filt_ref.3, f32[16,4096]{1,0:T(8,128)} %rate_ref.3, f32[16,4096]{1,0:T(8,128)} %res_ref.1, f32[1,4096]{1,0:T(1,128)} %bitcast.1, ...), custom_call_target="tpu_custom_call" | custom-call | tf_op jit(solution)/shard_map/pallas_call | solution.py:136
  (3 shorter events, 0.1 us)
Async XLA Ops:
  0.6 14.5 %copy-start = (f32[16,4096]{1,0:T(8,128)S(1)}, f32[16,4096]{1,0:T(8,128)}, u32[]{:S(2)}) copy-start(f32[16,4096]{1,0:T(8,128)} %rate_ref.3) | copy-start | bytes 786436
  1.7 3.2 %collective-permute-start = (bf16[3,2,4096]{2,1,0:T(2,128)(2,1)S(1)}, bf16[3,2,4096]{2,1,0:T(2,128)(2,1)S(1)}, u32[]{:S(2)}, u32[]{:S(2)}) collective-permute-start(bf16[3,2,4096]{2,1,0:T(2,128)(2,1)S(1)} %slice.41), channel_id=1, source_target_pairs={{0,1},{1,4},{4,5},{5,8},{8,9},{9,12},{12,13},{2,3},{3,6},{6,7},{7,... | collective-permute-start | bytes 147464 | tf_op jit(solution)/shard_map/ppermute | solution.py:18
  4.9 0.6 %copy-start.1 = (bf16[3,2,4096]{2,1,0:T(2,128)(2,1)}, bf16[3,2,4096]{2,1,0:T(2,128)(2,1)S(1)}, u32[]{:S(2)}) copy-start(bf16[3,2,4096]{2,1,0:T(2,128)(2,1)S(1)} %collective-permute-done.halo_ref) | copy-start | bytes 147460
  12.1 4.4 %collective-permute-start.1 = (f32[16,4096]{1,0:T(8,128)}, f32[16,4096]{1,0:T(8,128)S(1)}, u32[]{:S(2)}, u32[]{:S(2)}) collective-permute-start(f32[16,4096]{1,0:T(8,128)} %get-tuple-element.4), channel_id=1, source_target_pairs={{0,1},{1,0},{2,3},{3,2},{4,5},{5,4},{6,7},{7,6},{8,9},{9,8},{10,11... | collective-permute-start | bytes 786440 | tf_op jit(solution)/shard_map/ppermute | solution.py:150
  34.8 1.6 %collective-permute-start.2 = (f32[32,2048]{1,0:T(8,128)S(1)}, f32[32,2048]{1,0:T(8,128)S(1)}, u32[]{:S(2)}, u32[]{:S(2)}) collective-permute-start(f32[32,2048]{1,0:T(8,128)S(1)} %pad_maximum_fusion.1), channel_id=1, source_target_pairs={{0,1},{1,0},{2,3},{3,2},{4,5},{5,4},{6,7},{7,6},{8,9},{9,8},{10,11... | collective-permute-start | bytes 786440 | tf_op jit(solution)/shard_map/ppermute | solution.py:150
